TPU v7x, 128 devices: a whole 4x4x4 slice. The times are simulated.
128 devices in a mesh: lon: 8 (over z_lo, x), lat: 16 (over y, z_hi, core).
Axes of the slice: x: 4, y: 4, z: 4 (z_hi: 2, z_lo: 2; z = z_hi * 2 + z_lo), core: 2. Of those that a mesh axis runs over, the one named last changes fastest.
Arguments:
- adjoint: float32 [4, 10, 1024, 4096], P(None, None, 'lat', 'lon'), may hold values from -6 to 6
- trajectory: float32 [4, 10, 1024, 4096], P(None, None, 'lat', 'lon'), may hold values from -6 to 6
- diffusivity: float32 [10, 1024, 4096], P(None, 'lat', 'lon'), may hold values from 0.06 to 0.24
- land_mask: int32 [10, 1024, 4096], P(None, 'lat', 'lon'), may hold values 0 or 1
- coriolis: float32 [1024], P('lat'), may hold values from -0.3 to 0.3
- obs_values: float32 [65536, 128], P(('lon', 'lat')), may hold values from -6 to 6
- obs_weight: float32 [65536], P(('lon', 'lat')), may hold values from 0.5 to 4
- obs_owner: int32 [65536, 1], P(('lon', 'lat')), may hold values from 0 to 127; in each aligned block of 512 rows (0 to 511, 512 to 1023, ...) at most 8 rows name the same one
- obs_offset: int32 [65536], P(('lon', 'lat')), may hold values from 0 to 10239
- fold_partner: int32 [4096], P('lon'), may hold values from 0 to 4095, as said below
Outputs:
- adjoint_out: float32 [4, 10, 1024, 4096], P(None, None, 'lat', 'lon')
Inputs may be any that keep to these rules, and one draw needn't show every extreme that they name: `obs_owner`: in the rows of one device no owner is named by more than 8 rows, a bound that some block reaches. fold_partner is the mirror of the tripolar fold: fold_partner[i] = (4095 - i + o) modulo 4096 for one even offset o.
All inputs are finite; a program needn't handle non-finite values. No bound on the sum of `land_mask` on one device may be relied on, other than what follows from the above.
Results may differ from a plain program's by a relative error of at most 0.000059.
Values sent between devices are 32-bit elements; how exact they have to be, the bound alone decides.
No kernel may reach another device: no remote copies, remote signals or barrier semaphores. Data moves between devices by JAX's collectives and lax.ppermute only.
A program may use at most 320 MiB of HBM per device.

v0:
```python
import functools

import jax
import jax.numpy as jnp
from jax import lax
from jax.experimental import pallas as pl
from jax.experimental.pallas import tpu as pltpu
from jax.sharding import PartitionSpec as P

NSUB = 3
CAP = 8
HALO = 3
PAD_ROWS = 8
PAD_LANES = 128


def exact_dot(left, right, left_dim):
    return lax.dot_general(
        left,
        right,
        (((left_dim,), (0,)), ((), ())),
        precision=lax.Precision.HIGHEST,
        preferred_element_type=jnp.float32,
    )


def mix_kernel(adj_ref, mask_ref, diff_ref, rows_ref, cols_ref, cor_ref, out_ref, xs, ds):
    fields = adj_ref.shape[0]
    h, w = adj_ref.shape[2], adj_ref.shape[3]
    hp, wp = xs.shape[1], xs.shape[2]
    wet = mask_ref[0].astype(jnp.float32)
    for f in range(fields):
        xs[f, 0:h, 0:w] = adj_ref[f, 0] * wet
        xs[f, h:hp, 0:w] = rows_ref[f, 0]
        xs[f, :, w:wp] = cols_ref[f, 0]
    ds[0:h, 0:w] = diff_ref[0]
    ds[h:hp, 0:w] = rows_ref[fields, 0]
    ds[:, w:wp] = cols_ref[fields, 0]
    d = ds[...]
    done = []
    for f in range(fields):
        x = xs[f]
        for _ in range(NSUB):
            east = pltpu.roll(x, wp - 1, 1)
            west = pltpu.roll(x, 1, 1)
            north = pltpu.roll(x, hp - 1, 0)
            south = pltpu.roll(x, 1, 0)
            x = x + d * (east + west + north + south - 4.0 * x)
        done.append(x[0:h, 0:w])
    rot = cor_ref[...]
    out_ref[0, 0] = wet * done[0]
    out_ref[1, 0] = wet * done[1]
    out_ref[2, 0] = wet * (done[2] - rot * done[3])
    out_ref[3, 0] = wet * (done[3] + rot * done[2])


def mix_call(adjoint, land_mask, diffusivity, rows5, cols5, coriolis):
    fields, levels, h, w = adjoint.shape
    hp, wp = h + PAD_ROWS, w + PAD_LANES
    return pl.pallas_call(
        mix_kernel,
        grid=(levels,),
        in_specs=[
            pl.BlockSpec((fields, 1, h, w), lambda k: (0, k, 0, 0)),
            pl.BlockSpec((1, h, w), lambda k: (k, 0, 0)),
            pl.BlockSpec((1, h, w), lambda k: (k, 0, 0)),
            pl.BlockSpec((fields + 1, 1, PAD_ROWS, w), lambda k: (0, k, 0, 0)),
            pl.BlockSpec((fields + 1, 1, hp, PAD_LANES), lambda k: (0, k, 0, 0)),
            pl.BlockSpec((h, 1), lambda k: (0, 0)),
        ],
        out_specs=pl.BlockSpec((fields, 1, h, w), lambda k: (0, k, 0, 0)),
        out_shape=jax.ShapeDtypeStruct(adjoint.shape, jnp.float32),
        scratch_shapes=[
            pltpu.VMEM((fields, hp, wp), jnp.float32),
            pltpu.VMEM((hp, wp), jnp.float32),
        ],
    )(adjoint, land_mask, diffusivity, rows5, cols5, coriolis.reshape(h, 1))


def fold_rows(top_msg, fold_partner, width):
    lon_count = lax.axis_size("lon")
    lat_count = lax.axis_size("lat")
    lon = lax.axis_index("lon")
    nx = lon_count * width
    first = lon * width
    offset = (fold_partner[0] + first - (nx - 1)) % nx
    shift_tiles = offset // width
    shift_in = offset % width
    top = lat_count - 1

    def branch(q):
        def run(msg):
            pairs_a, pairs_b = [], []
            for t in range(lon_count):
                src_a = (lon_count - 1 - t + q) % lon_count
                src_b = (src_a + 1) % lon_count
                pairs_a.append((src_a * lat_count + top, t * lat_count + top))
                pairs_b.append((src_b * lat_count + top, t * lat_count + top))
            got_a = lax.ppermute(msg, ("lon", "lat"), pairs_a)
            got_b = lax.ppermute(msg, ("lon", "lat"), pairs_b)
            return jnp.concatenate([got_a, got_b], axis=2)

        return run

    both = lax.switch(shift_tiles, [branch(q) for q in range(lon_count)], top_msg)
    window = lax.dynamic_slice_in_dim(both, shift_in, width, axis=2)
    return window[:, ::-1, ::-1]


def per_device(
    adjoint,
    trajectory,
    diffusivity,
    land_mask,
    coriolis,
    obs_values,
    obs_weight,
    obs_owner,
    obs_offset,
    fold_partner,
):
    fields, levels, h, w = adjoint.shape
    lat_count = lax.axis_size("lat")
    lon_count = lax.axis_size("lon")
    lat = lax.axis_index("lat")
    n_work = fields * levels
    sign = jnp.array([1.0, 1.0, -1.0, -1.0], jnp.float32).reshape(fields, 1, 1, 1)

    def edge(rows):
        wet_rows = land_mask[:, rows, :].astype(jnp.float32)
        work_rows = adjoint[:, :, rows, :] * wet_rows[None]
        return work_rows, diffusivity[:, rows, :]

    top_work, top_diff = edge(slice(h - HALO, h))
    bot_work, bot_diff = edge(slice(0, HALO))
    top_msg = jnp.concatenate([top_work.reshape(n_work, HALO, w), top_diff], axis=0)
    bot_msg = jnp.concatenate([bot_work.reshape(n_work, HALO, w), bot_diff], axis=0)
    up = [(i, i + 1) for i in range(lat_count - 1)]
    down = [(i + 1, i) for i in range(lat_count - 1)]
    from_below = lax.ppermute(top_msg, "lat", up)
    from_above = lax.ppermute(bot_msg, "lat", down)
    signed_top = jnp.concatenate(
        [(top_work * sign).reshape(n_work, HALO, w), top_diff], axis=0
    )
    folded = fold_rows(signed_top, fold_partner, w)
    north = jnp.where(lat == lat_count - 1, folded, from_above)
    gap = jnp.zeros((n_work + levels, PAD_ROWS - 2 * HALO, w), jnp.float32)
    rows_all = jnp.concatenate([north, gap, from_below], axis=1)
    rows5 = rows_all.reshape(fields + 1, levels, PAD_ROWS, w)

    work_first = adjoint[:, :, :, :HALO] * land_mask[None, :, :, :HALO].astype(jnp.float32)
    work_last = adjoint[:, :, :, w - HALO :] * land_mask[None, :, :, w - HALO :].astype(jnp.float32)
    first = jnp.concatenate(
        [
            jnp.concatenate([work_first.reshape(n_work, h, HALO), diffusivity[:, :, :HALO]], 0),
            rows_all[:, :, :HALO],
        ],
        axis=1,
    )
    last = jnp.concatenate(
        [
            jnp.concatenate([work_last.reshape(n_work, h, HALO), diffusivity[:, :, w - HALO :]], 0),
            rows_all[:, :, w - HALO :],
        ],
        axis=1,
    )
    ring_west = [(i, (i - 1) % lon_count) for i in range(lon_count)]
    ring_east = [(i, (i + 1) % lon_count) for i in range(lon_count)]
    first_t = jnp.swapaxes(first, 1, 2)
    last_t = jnp.swapaxes(last, 1, 2)
    east_halo = jnp.swapaxes(lax.ppermute(first_t, "lon", ring_west), 1, 2)
    west_halo = jnp.swapaxes(lax.ppermute(last_t, "lon", ring_east), 1, 2)
    hp = h + PAD_ROWS
    middle = jnp.zeros((n_work + levels, hp, PAD_LANES - 2 * HALO), jnp.float32)
    cols5 = jnp.concatenate([east_halo, middle, west_halo], axis=2).reshape(
        fields + 1, levels, hp, PAD_LANES
    )

    mixed_wet = mix_call(adjoint, land_mask, diffusivity, rows5, cols5, coriolis)

    devices = lon_count * lat_count
    seg_width = obs_values.shape[1]
    rows_sent = obs_values.shape[0]
    owner_index = obs_owner[:, 0]
    one_hot = (owner_index[:, None] == jnp.arange(devices, dtype=jnp.int32)[None, :]).astype(
        jnp.bfloat16
    )
    row_ids = jnp.arange(rows_sent, dtype=jnp.int32)
    before = (row_ids[None, :] < row_ids[:, None]).astype(jnp.bfloat16)
    earlier = lax.dot_general(
        before, one_hot, (((1,), (0,)), ((), ())), preferred_element_type=jnp.float32
    )
    slot_index = jnp.sum(earlier * one_hot.astype(jnp.float32), axis=1).astype(jnp.int32)
    dest_index = owner_index * CAP + slot_index
    slot_ids = jnp.arange(devices * CAP, dtype=jnp.int32)
    placement = (dest_index[:, None] == slot_ids[None, :]).astype(jnp.float32)
    send_values = exact_dot(placement, obs_values, 0).reshape(devices, CAP, seg_width)
    meta = jnp.stack([obs_weight, obs_offset.astype(jnp.float32)], axis=1)
    send_meta = exact_dot(placement, meta, 0).reshape(devices, CAP, 2)
    send_meta = jnp.swapaxes(send_meta, 1, 2).reshape(devices, 2 * CAP)
    send_meta = jnp.pad(send_meta, ((0, 0), (0, seg_width - 2 * CAP)))
    send = jnp.concatenate([send_values.reshape(devices, CAP * seg_width), send_meta], axis=1)
    got = lax.all_to_all(send, ("lon", "lat"), split_axis=0, concat_axis=0, tiled=True)
    got_values = got[:, : CAP * seg_width].reshape(devices * CAP, seg_width)
    got_meta = got[:, CAP * seg_width : CAP * seg_width + 2 * CAP].reshape(devices, 2, CAP)
    got_weight = got_meta[:, 0, :].reshape(devices * CAP)
    got_offset = got_meta[:, 1, :].reshape(devices * CAP).astype(jnp.int32)

    segments = w // seg_width
    seg_local = got_offset % segments
    rest = got_offset // segments
    row_local = rest % h
    layer = rest // h
    index = jnp.stack([layer, row_local, seg_local * seg_width], axis=1)
    traj3 = trajectory.reshape(n_work, h, w)
    gdn = lax.GatherDimensionNumbers(
        offset_dims=(1,), collapsed_slice_dims=(0, 1), start_index_map=(0, 1, 2)
    )
    sampled = lax.gather(
        traj3, index, gdn, (1, 1, seg_width), mode=lax.GatherScatterMode.PROMISE_IN_BOUNDS
    )
    level_index = jnp.stack([layer % levels, row_local, seg_local * seg_width], axis=1)
    wet_rows = lax.gather(
        land_mask, level_index, gdn, (1, 1, seg_width), mode=lax.GatherScatterMode.PROMISE_IN_BOUNDS
    ).astype(jnp.float32)
    misfit = got_weight[:, None] * (sampled - got_values)
    sdn = lax.ScatterDimensionNumbers(
        update_window_dims=(1,), inserted_window_dims=(0, 1), scatter_dims_to_operand_dims=(0, 1, 2)
    )
    out3 = lax.scatter_add(
        mixed_wet.reshape(n_work, h, w),
        index,
        wet_rows * misfit,
        sdn,
        mode=lax.GatherScatterMode.PROMISE_IN_BOUNDS,
    )
    return out3.reshape(adjoint.shape)


def solution(mesh):
    return jax.shard_map(
        per_device,
        mesh=mesh,
        in_specs=(
            P(None, None, "lat", "lon"),
            P(None, None, "lat", "lon"),
            P(None, "lat", "lon"),
            P(None, "lat", "lon"),
            P("lat"),
            P(("lon", "lat"), None),
            P(("lon", "lat")),
            P(("lon", "lat"), None),
            P(("lon", "lat")),
            P("lon"),
        ),
        out_specs=P(None, None, "lat", "lon"),
        check_vma=False,
    )
```

profile of v0, /device:TPU:95, one launch (start us, length us, event | category | flops | bytes accessed | tf_op | source)
XLA Modules:
  0.0 18707.2 jit_solution(11691468153724365942)
XLA Ops:
  7.6 10.6 all-to-all-start
  29.0 12.8 conditional.1
  32.8 8.3 collective-permute-done.15
  52.6 5.0 collective-permute-start.18
  63.0 3.4 pad_maximum_fusion.8
  66.4 20.8 shard_map.109
  89.6 4707.2 %while.4 = (s32[]{:T(128)}, f32[40,64,512]{2,1,0:T(8,128)}, s32[1024,3]{0,1:T(4,128)S(1)}, f32[1024,128]{1,0:T(8,128)}, s32[]{:T(128)}, /*index=5*/s32[]{:T(128)}) while((s32[]{:T(128)}, f32[40,64,512]{2,1,0:T(8,128)}, s32[1024,3]{0,1:T(4,128)S(1)}, f32[1024,128]{1,0:T(8,128)}, s32[]{:T(128)}, /*index=5*/s32[]{:T(128)}) %tuple.117), condition=%wide.while_cond.1, body=%wide.while_body.1.sunk | while | flops 2 | bytes 2193 | solution.py:219
  4796.8 3993.4 %while.3 = (s32[]{:T(128)}, s32[10,64,512]{2,1,0:T(8,128)S(1)}, s32[1024,3]{0,1:T(4,128)S(1)}, s32[1024,128]{1,0:T(8,128)}, s32[]{:T(128)}, /*index=5*/s32[]{:T(128)}) while((s32[]{:T(128)}, s32[10,64,512]{2,1,0:T(8,128)S(1)}, s32[1024,3]{0,1:T(4,128)S(1)}, s32[1024,128]{1,0:T(8,128)}, s32[]{:T(128)}, /*index=5*/s32[]{:T(128)}) %tuple.114), condition=%wide.while_cond, body=%wide.while_body.sunk | while | flops 2 | bytes 2193 | solution.py:223
  8791.6 9915.6 %while.5 = (s32[]{:T(128)}, f32[40,64,512]{2,1,0:T(8,128)}, s32[1024,3]{0,1:T(4,128)S(1)}, f32[1024,128]{1,0:T(8,128)S(1)}, s32[]{:T(128)}, /*index=5*/s32[3]{0:T(128)S(1)}) while((s32[]{:T(128)}, f32[40,64,512]{2,1,0:T(8,128)}, s32[1024,3]{0,1:T(4,128)S(1)}, f32[1024,128]{1,0:T(8,128)S(1)}, s32[]{:T(128)}, /*index=5*/s32[3]{0:T(128)S(1)}) %tuple.116), condition=%wide.while_cond.2, body=%wide.while_body.2.sunk | while | flops 275 | bytes 2735 | solution.py:230
  8862.7 3.2 broadcast_select_fusion.3
  8930.3 3.2 broadcast_select_fusion.3
  9036.8 3.2 broadcast_select_fusion.3
  9075.6 3.2 broadcast_select_fusion.3
  9114.3 3.2 broadcast_select_fusion.3
  9220.9 3.2 broadcast_select_fusion.3
  9327.4 3.2 broadcast_select_fusion.3
  9366.1 3.2 broadcast_select_fusion.3
  9404.9 3.2 broadcast_select_fusion.3
  9511.4 3.2 broadcast_select_fusion.3
  9550.2 3.2 broadcast_select_fusion.3
  9617.9 3.2 broadcast_select_fusion.3
  9656.6 3.2 broadcast_select_fusion.3
  9724.4 3.2 broadcast_select_fusion.3
  9763.1 3.2 broadcast_select_fusion.3
  9830.9 3.2 broadcast_select_fusion.3
  9869.6 3.2 broadcast_select_fusion.3
  10150.3 3.2 broadcast_select_fusion.3
  10189.0 3.2 broadcast_select_fusion.3
  10295.5 3.2 broadcast_select_fusion.3
  10334.3 3.2 broadcast_select_fusion.3
  10440.8 3.2 broadcast_select_fusion.3
  11670.9 3.3 broadcast_select_fusion.3
  (13386 shorter events, 18576.0 us)
Async XLA Ops:
  0.0 4.3 copy-start
  6.3 12.9 copy-start.1
  6.4 12.9 copy-start.9
  7.6 79.7 all-to-all-start
  21.7 28.6 collective-permute-start.16
  25.5 24.8 collective-permute-start.17
  29.1 12.0 collective-permute-start.15
  32.1 9.0 collective-permute-start.14
  41.9 0.8 copy-start.4
  42.7 2.4 copy-start.3
  42.7 2.5 copy-start.5
  50.3 2.2 copy-start.6
  50.4 7.5 copy-start.8
  52.6 7.4 collective-permute-start.18
  57.7 3.4 collective-permute-start.19
  63.0 3.4 copy-start.2
  89.0 8702.6 %copy-start.7 = (s32[3]{0:T(128)S(1)}, s32[3]{0:T(128)}, u32[]{:S(2)}) copy-start(s32[3]{0:T(128)} %constant.249) | copy-start | bytes 40
where the time goes:
time: 19100 us; the launch traced here: 18700 us
  local copies, waits for them, and re-layouts  12600 us (66%)
  other arithmetic  6000 us (31%)
    gather x8192, local copies, waits for them, and re-layouts  8700 us
    scatter-add x2048, other arithmetic  5990 us
    scatter-add x3072, local copies, waits for them, and re-layouts  3920 us

commit v1 on v0

--- a/solution.py
+++ b/solution.py
@@ -77,6 +77,54 @@
     )(adjoint, land_mask, diffusivity, rows5, cols5, coriolis.reshape(h, 1))
 
 
+def obs_kernel(where_ref, weight_ref, vals_ref, traj_ref, mask_ref, base_ref, out_ref):
+    out_ref[...] = base_ref[...]
+    seg_width = vals_ref.shape[1]
+    sub = lax.broadcasted_iota(jnp.int32, (8, seg_width), 0)
+
+    def body(o, carry):
+        first = pl.multiple_of(o * 8, 8)
+        vals8 = vals_ref[pl.ds(first, 8), :]
+        for j in range(8):
+            i = first + j
+            layer = where_ref[0, i]
+            row = where_ref[1, i]
+            col = pl.multiple_of(where_ref[2, i], seg_width)
+            level = where_ref[3, i]
+            tile = pl.multiple_of((row // 8) * 8, 8)
+            rows = pl.ds(tile, 8)
+            cols = pl.ds(col, seg_width)
+            sampled = traj_ref[layer, rows, cols]
+            misfit = weight_ref[i] * (sampled - vals8[j : j + 1, :])
+            wet = mask_ref[level, rows, cols].astype(jnp.float32)
+            hit = sub == row - tile
+            cur = out_ref[layer, rows, cols]
+            out_ref[layer, rows, cols] = cur + jnp.where(hit, wet * misfit, 0.0)
+        return carry
+
+    lax.fori_loop(0, vals_ref.shape[0] // 8, body, 0)
+
+
+def obs_call(where, weight, values, traj3, land_mask, base3):
+    whole = lambda shape: pl.BlockSpec(shape, lambda i, *_: (0,) * len(shape))
+    return pl.pallas_call(
+        obs_kernel,
+        grid_spec=pltpu.PrefetchScalarGridSpec(
+            num_scalar_prefetch=2,
+            grid=(1,),
+            in_specs=[
+                whole(values.shape),
+                whole(traj3.shape),
+                whole(land_mask.shape),
+                whole(base3.shape),
+            ],
+            out_specs=whole(base3.shape),
+        ),
+        out_shape=jax.ShapeDtypeStruct(base3.shape, jnp.float32),
+        compiler_params=pltpu.CompilerParams(vmem_limit_bytes=60 * 1024 * 1024),
+    )(where, weight, values, traj3, land_mask, base3)
+
+
 def fold_rows(top_msg, fold_partner, width):
     lon_count = lax.axis_size("lon")
     lat_count = lax.axis_size("lat")
@@ -211,28 +259,14 @@
     rest = got_offset // segments
     row_local = rest % h
     layer = rest // h
-    index = jnp.stack([layer, row_local, seg_local * seg_width], axis=1)
-    traj3 = trajectory.reshape(n_work, h, w)
-    gdn = lax.GatherDimensionNumbers(
-        offset_dims=(1,), collapsed_slice_dims=(0, 1), start_index_map=(0, 1, 2)
-    )
-    sampled = lax.gather(
-        traj3, index, gdn, (1, 1, seg_width), mode=lax.GatherScatterMode.PROMISE_IN_BOUNDS
-    )
-    level_index = jnp.stack([layer % levels, row_local, seg_local * seg_width], axis=1)
-    wet_rows = lax.gather(
-        land_mask, level_index, gdn, (1, 1, seg_width), mode=lax.GatherScatterMode.PROMISE_IN_BOUNDS
-    ).astype(jnp.float32)
-    misfit = got_weight[:, None] * (sampled - got_values)
-    sdn = lax.ScatterDimensionNumbers(
-        update_window_dims=(1,), inserted_window_dims=(0, 1), scatter_dims_to_operand_dims=(0, 1, 2)
-    )
-    out3 = lax.scatter_add(
+    where = jnp.stack([layer, row_local, seg_local * seg_width, layer % levels], axis=0)
+    out3 = obs_call(
+        where,
+        got_weight,
+        got_values,
+        trajectory.reshape(n_work, h, w),
+        land_mask,
         mixed_wet.reshape(n_work, h, w),
-        index,
-        wet_rows * misfit,
-        sdn,
-        mode=lax.GatherScatterMode.PROMISE_IN_BOUNDS,
     )
     return out3.reshape(adjoint.shape)
 

time: 19100 us -> 120 us (0.01); the launches traced: 18700 us -> 118 us
  local copies, waits for them, and re-layouts: 12600 us -> 23.4 us
  other arithmetic: 6000 us -> 14.7 us
    gather x8192 -> x0, local copies, waits for them, and re-layouts: 8700 us -> none
    scatter-add x2048 -> x0, other arithmetic: 5990 us -> none
    scatter-add x3072 -> x0, local copies, waits for them, and re-layouts: 3920 us -> none
where the time goes in v1:
time: 120 us; the launch traced here: 118 us
  Pallas kernels  42.9 us (36%)
  starting transfers between devices  23.6 us (20%)
  local copies, waits for them, and re-layouts  23.4 us (20%)
  other arithmetic  14.7 us (12%)
  waiting for transfers between devices  7.79 us (6%)
  matrix products  4.46 us (4%)
    pallas_call x1, Pallas kernels, obs_call(): pl.pallas_call(obs_kernel, grid_spec=pltpu.PrefetchScalarGridSpec(num_sca...  22 us
    pallas_call x1, Pallas kernels, mix_call(): pl.pallas_call(mix_kernel, grid=(levels,), in_specs=[pl.BlockSpec((fields...  20.9 us
    all_to_all x1, starting transfers between devices, per_device(): lax.all_to_all(send, ('lon', 'lat'), split_axis=0, concat_axis=0, tiled=T...  10.2 us
    ppermute x1, waiting for transfers between devices, run(): got_a = lax.ppermute(msg, ('lon', 'lat'), pairs_a)  7.78 us
    ppermute x1, starting transfers between devices, run(): got_a = lax.ppermute(msg, ('lon', 'lat'), pairs_a)  4.81 us
    unnamed x23, local copies, waits for them, and re-layouts  4.6 us
    ppermute x1, starting transfers between devices, per_device(): west_halo = jnp.swapaxes(lax.ppermute(last_t, 'lon', ring_east), 1, 2)  3.62 us
    dot_general x2, matrix products, exact_dot(): lax.dot_general(left, right, (((left_dim,), (0,)), ((), ())), precision=l...  3.4 us
  transfers between devices with their start and end apart: 7, of which 1 were waited for; matrix products, arithmetic and copies ran while one was open for 26% of the time, Pallas kernels for 18%

profile of v1, /device:TPU:95, one launch (start us, length us, event | category | flops | bytes accessed | tf_op | source)
XLA Modules:
  0.0 118.2 jit_solution(14824523330831950766)
XLA Ops:
  0.7 1.1 fusion.2
  2.5 1.5 %fusion = f32[1024,2]{0,1:T(2,128)S(1)} fusion(s32[512]{0:T(512)S(1)} %bitcast.52, f32[512,1]{0,1:T(1,128)S(1)} %bitcast.54, f32[512,1]{0,1:T(1,128)} %bitcast.56), kind=kOutput, calls=%fused_computation.9 | convolution fusion | flops 13108224 | bytes 14336 | tf_op jit(solution)/shard_map/dot_general | solution.py:18
  4.3 1.9 %fusion.1 = f32[1024,128]{1,0:T(8,128)S(1)} fusion(f32[512,128]{1,0:T(8,128)S(1)} %copy-done, s32[512]{0:T(512)S(1)} %bitcast.53), kind=kOutput, calls=%fused_computation.10 | convolution fusion | flops 805830656 | bytes 788480 | tf_op jit(solution)/shard_map/dot_general | solution.py:18
  6.4 1.3 %all_to_all.8 = f32[128,1,1152]{2,1,0:T(1,128)} reshape(f32[128,1152]{1,0:T(8,128)S(1)} %select_maximum_fusion) | data formatting | bytes 1179648 | tf_op jit(solution)/shard_map/all_to_all | solution.py:251
  7.6 10.2 %all-to-all-start = ((f32[128,1,1152]{2,1,0:T(1,128)}), f32[128,1,1152]{2,1,0:T(1,128)S(1)}, u32[]{:S(2)}, u32[]{:S(2)}) async-start(f32[128,1,1152]{2,1,0:T(1,128)} %all_to_all.8), calls=%async_computation | async-start | bytes 1179648 | tf_op jit(solution)/shard_map/all_to_all | solution.py:251
  17.8 1.0 fusion.13
  18.9 1.5 %broadcast_multiply_fusion = (f32[4,10,3,512]{3,2,1,0:T(4,128)S(1)}, f32[4,10,3,512]{3,2,1,0:T(4,128)S(1)}, f32[4,10,3,512]{3,2,1,0:T(4,128)S(1)}) fusion(f32[4]{0:T(128)S(1)} %copy-done.8, f32[10,3,512]{2,1,0:T(4,128)S(1)} %get-tuple-element.39, f32[4,10,64,512]{3,2,1,0:T(8,128)} %adj_ref.1, f32[10,3,512]{2,1,0:T(4,128)S(1)} %get-tuple-element.38), kind=kLoop, calls=%fused_computation.32 | loop fusion | flops 184320 | bytes 1351696 | tf_op jit(solution)/shard_map/mul | solution.py:191
  20.5 0.8 pad_maximum_fusion.11
  21.3 3.0 %collective-permute-start.16 = (f32[50,3,512]{2,0,1:T(8,128)}, f32[50,3,512]{2,0,1:T(8,128)}, u32[]{:S(2)}, u32[]{:S(2)}) collective-permute-start(f32[50,3,512]{2,0,1:T(8,128)} %pad_maximum_fusion.11), channel_id=1, source_target_pairs={{1,0},{2,1},{3,2},{4,3},{5,4},{6,5},{7,6},{8,7},{9,8},{10,9},{11,1... | collective-permute-start | bytes 921608 | tf_op jit(solution)/shard_map/ppermute | solution.py:189
  24.4 0.8 pad_maximum_fusion.12
  25.2 1.3 %collective-permute-start.17 = (f32[50,3,512]{2,0,1:T(8,128)}, f32[50,3,512]{2,0,1:T(8,128)}, u32[]{:S(2)}, u32[]{:S(2)}) collective-permute-start(f32[50,3,512]{2,0,1:T(8,128)} %pad_maximum_fusion.12), channel_id=1, source_target_pairs={{0,1},{1,2},{2,3},{3,4},{4,5},{5,6},{6,7},{7,8},{8,9},{9,10},{10,1... | collective-permute-start | bytes 921608 | tf_op jit(solution)/shard_map/ppermute | solution.py:188
  26.5 1.2 %slice.61 = s32[1]{0:T(128)} slice(s32[512]{0:T(512)} %param.28), slice={[0:1]} | slice | bytes 8 | tf_op jit(solution)/shard_map/slice | solution.py:134
  28.3 1.0 slice_convert_fusion.1
  29.4 14.1 %conditional.1 = (f32[50,3,1024]{2,0,1:T(8,128)S(1)}) conditional(s32[]{:T(128)} %clamp.3, f32[50,3,512]{2,1,0:T(4,128)S(1)} %pad_maximum_fusion.10, f32[50,3,512]{2,1,0:T(4,128)S(1)} %pad_maximum_fusion.10, f32[50,3,512]{2,1,0:T(4,128)S(1)} %pad_maximum_fusion.10, f32[50,3,512]{2,1,0:T(4,128)S(1)} %pad_maximum_fusion.10, ...), branch_computations={%region_1.2_spmd, %region_2.3_spmd, %region_3.4_spmd, %region_4.5_... | conditional | flops 153600 | bytes 4915288 | solution.py:153
  30.1 4.8 %collective-permute-start.12 = (f32[50,3,512]{2,1,0:T(4,128)S(1)}, f32[50,3,512]{2,1,0:T(4,128)S(1)}, u32[]{:S(2)}, u32[]{:S(2)}) collective-permute-start(f32[50,3,512]{2,1,0:T(4,128)S(1)} %param.6), channel_id=1, source_target_pairs={{95,15},{79,31},{63,47},{47,63},{31,79},{15,95},{127,111},{111,127}} | collective-permute-start | bytes 921608 | tf_op jit(solution)/shard_map/cond/branch_6_fun/ppermute | solution.py:147
  35.0 7.8 %collective-permute-done.12 = f32[50,3,512]{2,1,0:T(4,128)S(1)} collective-permute-done((f32[50,3,512]{2,1,0:T(4,128)S(1)}, f32[50,3,512]{2,1,0:T(4,128)S(1)}, u32[]{:S(2)}, u32[]{:S(2)}) %collective-permute-start.12) | collective-permute-done | bytes 307232 | tf_op jit(solution)/shard_map/cond/branch_6_fun/ppermute | solution.py:147
  43.6 0.8 copy-done.3
  44.4 2.5 %slice_multiply_fusion.1 = (f32[4,10,64,3]{3,2,1,0:T(8,128)S(1)}, f32[4,10,64,3]{3,2,1,0:T(8,128)S(1)}) fusion(f32[4,10,64,512]{3,2,1,0:T(8,128)} %adj_ref.1, f32[10,64,3]{2,1,0:T(8,128)} %get-tuple-element.34, f32[10,64,3]{2,1,0:T(8,128)} %get-tuple-element.35), kind=kLoop, calls=%fused_computation.13 | loop fusion | flops 15360 | bytes 138240 | tf_op jit(solution)/shard_map/mul | solution.py:199
  46.9 0.9 fusion.12
  47.9 0.9 constant_dynamic-slice_fusion
  48.8 1.8 %copy.77 = f32[10,64,3]{1,0,2:T(8,128)} copy(f32[10,64,3]{2,1,0:T(8,128)} %get-tuple-element.36) | data formatting | bytes 15360
  50.5 1.8 %copy.78 = f32[10,64,3]{1,0,2:T(8,128)} copy(f32[10,64,3]{2,1,0:T(8,128)} %get-tuple-element.37) | data formatting | bytes 15360
  52.3 3.3 %rev.3 = f32[50,3,512]{2,0,1:T(8,128)} reverse(f32[50,3,512]{2,0,1:T(8,128)} %constant_dynamic-slice_fusion), dimensions={1,2} | reverse | bytes 614400 | tf_op jit(solution)/shard_map/rev | solution.py:155
  56.6 1.0 broadcast_select_fusion
  57.7 1.1 pad_maximum_fusion.9
  60.1 3.6 %collective-permute-start.19 = (f32[50,3,72]{2,0,1:T(8,128)S(1)}, f32[50,3,72]{2,0,1:T(8,128)S(1)}, u32[]{:S(2)}, u32[]{:S(2)}) collective-permute-start(f32[50,3,72]{2,0,1:T(8,128)S(1)} %maximum_bitcast_fusion.1), channel_id=1, source_target_pairs={{0,16},{16,32},{32,48},{48,64},{64,80},{80,96},{96,112},{112,0},{1... | collective-permute-start | bytes 129608 | tf_op jit(solution)/shard_map/ppermute | solution.py:220
  64.6 1.4 %copy.53 = f32[50,8,512]{2,1,0:T(8,128)} copy(f32[50,8,512]{2,0,1:T(8,128)S(1)} %pad_maximum_fusion.9) | data formatting | bytes 1638400 | tf_op jit(solution)/shard_map/concatenate | solution.py:196
  66.6 1.9 %copy.61 = f32[50,72,3]{2,1,0:T(8,128)} copy(f32[50,72,3]{1,0,2:T(8,128)S(1)} %bitcast.48) | data formatting | bytes 86400 | tf_op jit(solution)/shard_map/transpose | solution.py:220
  68.5 3.3 %pad_maximum_fusion.8 = f32[50,72,128]{2,1,0:T(8,128)} fusion(f32[50,72,3]{2,1,0:T(8,128)} %copy.61, f32[50,72,3]{2,1,0:T(8,128)S(1)} %copy.60, f32[128]{0:T(128)S(1)} %pad.22.clone), kind=kLoop, calls=%fused_computation.11 | loop fusion | flops 921600 | bytes 1930112 | tf_op jit(solution)/shard_map/concatenate | solution.py:223
  71.8 20.9 %shard_map.109 = f32[4,10,64,512]{3,2,1,0:T(8,128)} custom-call(f32[4,10,64,512]{3,2,1,0:T(8,128)} %adj_ref.1, s32[10,64,512]{2,1,0:T(8,128)} %mask_ref.3, f32[10,64,512]{2,1,0:T(8,128)} %diff_ref.1, f32[5,10,8,512]{3,2,1,0:T(8,128)} %bitcast.40, f32[5,10,72,128]{3,2,1,0:T(8,128)} %bitcast.36, f32[64,1]{1,0:T(8,128)} %copy.62.cor_ref), custom_call_target="tpu_custom_call" | custom-call | tf_op jit(solution)/shard_map/pallas_call | solution.py:60
  93.6 0.9 reshape.238.vals_ref
  96.2 22.0 %shard_map.110 = f32[40,64,512]{2,1,0:T(8,128)} custom-call(s32[4,1024]{1,0:T(4,128)} %pad_add_fusion.where_ref, f32[1024]{0:T(1024)} %reshape_squeeze.4.weight_ref, f32[1024,128]{1,0:T(8,128)} %reshape.238.vals_ref, f32[40,64,512]{2,1,0:T(8,128)} %bitcast.37, s32[10,64,512]{2,1,0:T(8,128)} %mask_ref.3, f32[40,64,512]{2,1,0:T(8,128)} %bitcast.35), custom_call_target="tpu_custom_call" | custom-call | tf_op jit(solution)/shard_map/pallas_call | solution.py:110
  (66 shorter events, 9.7 us)
Async XLA Ops:
  0.0 4.3 %copy-start = (f32[512,128]{1,0:T(8,128)S(1)}, f32[512,128]{1,0:T(8,128)}, u32[]{:S(2)}) copy-start(f32[512,128]{1,0:T(8,128)} %param.24) | copy-start | bytes 786436
  6.3 12.6 %copy-start.1 = (s32[10,64,512]{2,1,0:T(8,128)S(1)}, s32[10,64,512]{2,1,0:T(8,128)}, u32[]{:S(2)}) copy-start(s32[10,64,512]{2,1,0:T(8,128)} %mask_ref.3) | copy-start | bytes 3932164
  6.4 12.6 %copy-start.8 = (f32[4]{0:T(128)S(1)}, f32[4]{0:T(128)}, u32[]{:S(2)}) copy-start(f32[4]{0:T(128)} %constant.119.clone) | copy-start | bytes 52
  7.6 85.1 %all-to-all-start = ((f32[128,1,1152]{2,1,0:T(1,128)}), f32[128,1,1152]{2,1,0:T(1,128)S(1)}, u32[]{:S(2)}, u32[]{:S(2)}) async-start(f32[128,1,1152]{2,1,0:T(1,128)} %all_to_all.8), calls=%async_computation | async-start | bytes 1179648 | tf_op jit(solution)/shard_map/all_to_all | solution.py:251
  21.3 35.3 %collective-permute-start.16 = (f32[50,3,512]{2,0,1:T(8,128)}, f32[50,3,512]{2,0,1:T(8,128)}, u32[]{:S(2)}, u32[]{:S(2)}) collective-permute-start(f32[50,3,512]{2,0,1:T(8,128)} %pad_maximum_fusion.11), channel_id=1, source_target_pairs={{1,0},{2,1},{3,2},{4,3},{5,4},{6,5},{7,6},{8,7},{9,8},{10,9},{11,1... | collective-permute-start | bytes 921608 | tf_op jit(solution)/shard_map/ppermute | solution.py:189
  25.2 32.5 %collective-permute-start.17 = (f32[50,3,512]{2,0,1:T(8,128)}, f32[50,3,512]{2,0,1:T(8,128)}, u32[]{:S(2)}, u32[]{:S(2)}) collective-permute-start(f32[50,3,512]{2,0,1:T(8,128)} %pad_maximum_fusion.12), channel_id=1, source_target_pairs={{0,1},{1,2},{2,3},{3,4},{4,5},{5,6},{6,7},{7,8},{8,9},{9,10},{10,1... | collective-permute-start | bytes 921608 | tf_op jit(solution)/shard_map/ppermute | solution.py:188
  29.4 5.5 %collective-permute-start.13 = (f32[50,3,512]{2,1,0:T(4,128)S(1)}, f32[50,3,512]{2,1,0:T(4,128)S(1)}, u32[]{:S(2)}, u32[]{:S(2)}) collective-permute-start(f32[50,3,512]{2,1,0:T(4,128)S(1)} %param.6), channel_id=1, source_target_pairs={{111,15},{95,31},{79,47},{63,63},{47,79},{31,95},{15,111},{127,127}} | collective-permute-start | bytes 921608 | tf_op jit(solution)/shard_map/cond/branch_6_fun/ppermute | solution.py:148
  30.1 12.6 %collective-permute-start.12 = (f32[50,3,512]{2,1,0:T(4,128)S(1)}, f32[50,3,512]{2,1,0:T(4,128)S(1)}, u32[]{:S(2)}, u32[]{:S(2)}) collective-permute-start(f32[50,3,512]{2,1,0:T(4,128)S(1)} %param.6), channel_id=1, source_target_pairs={{95,15},{79,31},{63,47},{47,63},{31,79},{15,95},{127,111},{111,127}} | collective-permute-start | bytes 921608 | tf_op jit(solution)/shard_map/cond/branch_6_fun/ppermute | solution.py:147
  43.5 0.8 copy-start.3
  44.4 2.5 %copy-start.2 = (f32[10,64,512]{2,1,0:T(8,128)S(1)}, f32[10,64,512]{2,1,0:T(8,128)}, u32[]{:S(2)}) copy-start(f32[10,64,512]{2,1,0:T(8,128)} %diff_ref.1) | copy-start | bytes 3932164
  44.4 3.5 %copy-start.4 = (f32[50,3,1024]{2,0,1:T(8,128)S(1)}, f32[50,3,1024]{2,0,1:T(8,128)}, u32[]{:S(2)}) copy-start(f32[50,3,1024]{2,0,1:T(8,128)} %copy-done.3) | copy-start | bytes 1843204
  56.6 3.2 %copy-start.6 = (f32[10,64,3]{1,0,2:T(8,128)S(1)}, f32[10,64,3]{1,0,2:T(8,128)}, u32[]{:S(2)}) copy-start(f32[10,64,3]{1,0,2:T(8,128)} %copy.77) | copy-start | bytes 23044
  57.7 2.3 %copy-start.5 = (f32[10,64,3]{1,0,2:T(8,128)S(1)}, f32[10,64,3]{1,0,2:T(8,128)}, u32[]{:S(2)}) copy-start(f32[10,64,3]{1,0,2:T(8,128)} %copy.78) | copy-start | bytes 23044
  57.7 6.1 %copy-start.7 = (f32[64]{0:T(128)S(1)}, f32[64]{0:T(128)}, u32[]{:S(2)}) copy-start(f32[64]{0:T(128)} %param.23) | copy-start | bytes 772
  59.9 6.0 %collective-permute-start.18 = (f32[50,3,72]{2,0,1:T(8,128)S(1)}, f32[50,3,72]{2,0,1:T(8,128)S(1)}, u32[]{:S(2)}, u32[]{:S(2)}) collective-permute-start(f32[50,3,72]{2,0,1:T(8,128)S(1)} %maximum_bitcast_fusion), channel_id=1, source_target_pairs={{0,112},{16,0},{32,16},{48,32},{64,48},{80,64},{96,80},{112,96},{1... | collective-permute-start | bytes 129608 | tf_op jit(solution)/shard_map/ppermute | solution.py:219
  60.1 6.5 %collective-permute-start.19 = (f32[50,3,72]{2,0,1:T(8,128)S(1)}, f32[50,3,72]{2,0,1:T(8,128)S(1)}, u32[]{:S(2)}, u32[]{:S(2)}) collective-permute-start(f32[50,3,72]{2,0,1:T(8,128)S(1)} %maximum_bitcast_fusion.1), channel_id=1, source_target_pairs={{0,16},{16,32},{32,48},{48,64},{64,80},{80,96},{96,112},{112,0},{1... | collective-permute-start | bytes 129608 | tf_op jit(solution)/shard_map/ppermute | solution.py:220

commit v2 on v1

--- a/solution.py
+++ b/solution.py
@@ -87,20 +87,27 @@
         vals8 = vals_ref[pl.ds(first, 8), :]
         for j in range(8):
             i = first + j
-            layer = where_ref[0, i]
-            row = where_ref[1, i]
-            col = pl.multiple_of(where_ref[2, i], seg_width)
-            level = where_ref[3, i]
-            tile = pl.multiple_of((row // 8) * 8, 8)
-            rows = pl.ds(tile, 8)
-            cols = pl.ds(col, seg_width)
-            sampled = traj_ref[layer, rows, cols]
-            misfit = weight_ref[i] * (sampled - vals8[j : j + 1, :])
-            wet = mask_ref[level, rows, cols].astype(jnp.float32)
-            hit = sub == row - tile
-            cur = out_ref[layer, rows, cols]
-            out_ref[layer, rows, cols] = cur + jnp.where(hit, wet * misfit, 0.0)
+
+            @pl.when(weight_ref[i] != 0.0)
+            def _():
+                add_row(i, vals8[j : j + 1, :])
+
         return carry
+
+    def add_row(i, value):
+        layer = where_ref[0, i]
+        row = where_ref[1, i]
+        col = pl.multiple_of(where_ref[2, i], seg_width)
+        level = where_ref[3, i]
+        tile = pl.multiple_of((row // 8) * 8, 8)
+        rows = pl.ds(tile, 8)
+        cols = pl.ds(col, seg_width)
+        sampled = traj_ref[layer, rows, cols]
+        misfit = weight_ref[i] * (sampled - value)
+        wet = mask_ref[level, rows, cols].astype(jnp.float32)
+        hit = sub == row - tile
+        cur = out_ref[layer, rows, cols]
+        out_ref[layer, rows, cols] = cur + jnp.where(hit, wet * misfit, 0.0)
 
     lax.fori_loop(0, vals_ref.shape[0] // 8, body, 0)
 
@@ -151,8 +158,10 @@
         return run
 
     both = lax.switch(shift_tiles, [branch(q) for q in range(lon_count)], top_msg)
-    window = lax.dynamic_slice_in_dim(both, shift_in, width, axis=2)
-    return window[:, ::-1, ::-1]
+    source = lax.broadcasted_iota(jnp.int32, (2 * width, width), 0)
+    target = lax.broadcasted_iota(jnp.int32, (2 * width, width), 1)
+    pick = (source == width - 1 - target + shift_in).astype(jnp.float32)
+    return exact_dot(both, pick, 2)
 
 
 def per_device(
@@ -190,6 +199,9 @@
     signed_top = jnp.concatenate(
         [(top_work * sign).reshape(n_work, HALO, w), top_diff], axis=0
     )
+    signed_top = jnp.concatenate(
+        [signed_top[:, HALO - 1 - m : HALO - m, :] for m in range(HALO)], axis=1
+    )
     folded = fold_rows(signed_top, fold_partner, w)
     north = jnp.where(lat == lat_count - 1, folded, from_above)
     gap = jnp.zeros((n_work + levels, PAD_ROWS - 2 * HALO, w), jnp.float32)

time: 120 us -> 126 us (1.050)
  the two profiles are of different devices: /device:TPU:95 before, /device:TPU:123 now
where the time goes in v2:
time: 126 us; the launch traced here: 125 us
  Pallas kernels  53.8 us (43%)
  starting transfers between devices  21.5 us (17%)
  local copies, waits for them, and re-layouts  18.3 us (15%)
  other arithmetic  14.6 us (12%)
  waiting for transfers between devices  10.4 us (8%)
  matrix products  5.41 us (4%)
    pallas_call x1, Pallas kernels, obs_call(): pl.pallas_call(obs_kernel, grid_spec=pltpu.PrefetchScalarGridSpec(num_sca...  32.9 us
    pallas_call x1, Pallas kernels, mix_call(): pl.pallas_call(mix_kernel, grid=(levels,), in_specs=[pl.BlockSpec((fields...  20.9 us
    all_to_all x1, starting transfers between devices, per_device(): lax.all_to_all(send, ('lon', 'lat'), split_axis=0, concat_axis=0, tiled=T...  10 us
    ppermute x1, waiting for transfers between devices, run(): got_a = lax.ppermute(msg, ('lon', 'lat'), pairs_a)  5.21 us
    ppermute x1, waiting for transfers between devices, run(): got_b = lax.ppermute(msg, ('lon', 'lat'), pairs_b)  4.85 us
    dot_general x3, matrix products, exact_dot(): lax.dot_general(left, right, (((left_dim,), (0,)), ((), ())), precision=l...  4.34 us
    unnamed x19, local copies, waits for them, and re-layouts  3.76 us
    ppermute x1, starting transfers between devices, run(): got_b = lax.ppermute(msg, ('lon', 'lat'), pairs_b)  3.73 us
  transfers between devices with their start and end apart: 7, of which 3 were waited for; matrix products, arithmetic and copies ran while one was open for 22% of the time, Pallas kernels for 17%

profile of v2, /device:TPU:123, one launch (start us, length us, event | category | flops | bytes accessed | tf_op | source)
XLA Modules:
  0.0 125.2 jit_solution(2342946425135968979)
XLA Ops:
  0.7 1.1 fusion.8
  2.5 1.5 %fusion = f32[1024,2]{0,1:T(2,128)S(1)} fusion(s32[512]{0:T(512)S(1)} %bitcast.58, f32[512,1]{0,1:T(1,128)S(1)} %bitcast.60, f32[512,1]{0,1:T(1,128)} %bitcast.62), kind=kOutput, calls=%fused_computation.10 | convolution fusion | flops 13108224 | bytes 14336 | tf_op jit(solution)/shard_map/dot_general | solution.py:18
  4.3 1.9 %fusion.1 = f32[1024,128]{1,0:T(8,128)S(1)} fusion(f32[512,128]{1,0:T(8,128)S(1)} %copy-done, s32[512]{0:T(512)S(1)} %bitcast.59), kind=kOutput, calls=%fused_computation.11 | convolution fusion | flops 805830656 | bytes 788480 | tf_op jit(solution)/shard_map/dot_general | solution.py:18
  6.4 1.3 %all_to_all.8 = f32[128,1,1152]{2,1,0:T(1,128)} reshape(f32[128,1152]{1,0:T(8,128)S(1)} %select_maximum_fusion) | data formatting | bytes 1179648 | tf_op jit(solution)/shard_map/all_to_all | solution.py:263
  7.6 10.0 %all-to-all-start = ((f32[128,1,1152]{2,1,0:T(1,128)}), f32[128,1,1152]{2,1,0:T(1,128)S(1)}, u32[]{:S(2)}, u32[]{:S(2)}) async-start(f32[128,1,1152]{2,1,0:T(1,128)} %all_to_all.8), calls=%async_computation | async-start | bytes 1179648 | tf_op jit(solution)/shard_map/all_to_all | solution.py:263
  17.6 1.0 fusion.23
  18.8 1.5 %broadcast_multiply_fusion = (f32[4,10,3,512]{3,2,1,0:T(4,128)S(1)}, f32[4,10,3,512]{3,2,1,0:T(4,128)S(1)}, f32[4,10,3,512]{3,2,1,0:T(4,128)S(1)}) fusion(f32[4]{0:T(128)S(1)} %copy-done.6, f32[10,3,512]{2,1,0:T(4,128)S(1)} %get-tuple-element.39, f32[4,10,64,512]{3,2,1,0:T(8,128)} %adj_ref.1, f32[10,3,512]{2,1,0:T(4,128)S(1)} %get-tuple-element.38), kind=kLoop, calls=%fused_computation.43 | loop fusion | flops 184320 | bytes 1351696 | tf_op jit(solution)/shard_map/mul | solution.py:200
  20.4 0.8 pad_maximum_fusion.12
  21.2 3.0 %collective-permute-start.16 = (f32[50,3,512]{2,0,1:T(8,128)}, f32[50,3,512]{2,0,1:T(8,128)}, u32[]{:S(2)}, u32[]{:S(2)}) collective-permute-start(f32[50,3,512]{2,0,1:T(8,128)} %pad_maximum_fusion.12), channel_id=1, source_target_pairs={{1,0},{2,1},{3,2},{4,3},{5,4},{6,5},{7,6},{8,7},{9,8},{10,9},{11,1... | collective-permute-start | bytes 921608 | tf_op jit(solution)/shard_map/ppermute | solution.py:198
  24.2 0.7 pad_maximum_fusion.13
  25.0 1.3 %collective-permute-start.17 = (f32[50,3,512]{2,0,1:T(8,128)}, f32[50,3,512]{2,0,1:T(8,128)}, u32[]{:S(2)}, u32[]{:S(2)}) collective-permute-start(f32[50,3,512]{2,0,1:T(8,128)} %pad_maximum_fusion.13), channel_id=1, source_target_pairs={{0,1},{1,2},{2,3},{3,4},{4,5},{5,6},{6,7},{7,8},{8,9},{9,10},{10,1... | collective-permute-start | bytes 921608 | tf_op jit(solution)/shard_map/ppermute | solution.py:197
  26.3 1.2 slice.70
  28.2 1.0 slice_convert_fusion.1
  29.1 1.0 fusion.12
  30.1 2.5 %slice_multiply_fusion.1 = (f32[4,10,64,3]{3,2,1,0:T(8,128)S(1)}, f32[4,10,64,3]{3,2,1,0:T(8,128)S(1)}) fusion(f32[4,10,64,512]{3,2,1,0:T(8,128)} %adj_ref.1, f32[10,64,3]{2,1,0:T(8,128)} %get-tuple-element.34, f32[10,64,3]{2,1,0:T(8,128)} %get-tuple-element.35), kind=kLoop, calls=%fused_computation.16 | loop fusion | flops 15360 | bytes 138240 | tf_op jit(solution)/shard_map/mul | solution.py:211
  32.6 0.9 fusion.22
  33.6 1.8 %copy.97 = f32[10,64,3]{1,0,2:T(8,128)} copy(f32[10,64,3]{2,1,0:T(8,128)} %get-tuple-element.36) | data formatting | bytes 15360
  35.4 1.8 %copy.98 = f32[10,64,3]{1,0,2:T(8,128)} copy(f32[10,64,3]{2,1,0:T(8,128)} %get-tuple-element.37) | data formatting | bytes 15360
  38.2 16.5 %conditional.1 = (f32[50,3,1024]{2,0,1:T(8,128)S(1)}) conditional(s32[]{:T(128)} %clamp.3, f32[50,3,512]{2,1,0:T(4,128)} %fusion.12, f32[50,3,512]{2,1,0:T(4,128)} %fusion.12, f32[50,3,512]{2,1,0:T(4,128)} %fusion.12, f32[50,3,512]{2,1,0:T(4,128)} %fusion.12, f32[50,3,512]{2,1,0:T(4,128)} %fusion.12, ...), branch_computations={%region_1.2_spmd, %region_2.3_spmd, %region_3.4_spmd, %region_4.5_... | conditional | flops 153600 | bytes 4915288 | solution.py:160
  38.2 3.7 %collective-permute-start.9 = (f32[50,3,512]{2,1,0:T(4,128)}, f32[50,3,512]{2,1,0:T(4,128)S(1)}, u32[]{:S(2)}, u32[]{:S(2)}) collective-permute-start(f32[50,3,512]{2,1,0:T(4,128)} %param.4), channel_id=1, source_target_pairs={{79,15},{63,31},{47,47},{31,63},{15,79},{127,95},{111,111},{95,127}} | collective-permute-start | bytes 921608 | tf_op jit(solution)/shard_map/cond/branch_4_fun/ppermute | solution.py:155
  41.9 1.9 %collective-permute-start.8 = (f32[50,3,512]{2,1,0:T(4,128)}, f32[50,3,512]{2,1,0:T(4,128)S(1)}, u32[]{:S(2)}, u32[]{:S(2)}) collective-permute-start(f32[50,3,512]{2,1,0:T(4,128)} %param.4), channel_id=1, source_target_pairs={{63,15},{47,31},{31,47},{15,63},{127,79},{111,95},{95,111},{79,127}} | collective-permute-start | bytes 921608 | tf_op jit(solution)/shard_map/cond/branch_4_fun/ppermute | solution.py:154
  43.8 4.8 %collective-permute-done.9 = f32[50,3,512]{2,1,0:T(4,128)S(1)} collective-permute-done((f32[50,3,512]{2,1,0:T(4,128)}, f32[50,3,512]{2,1,0:T(4,128)S(1)}, u32[]{:S(2)}, u32[]{:S(2)}) %collective-permute-start.9) | collective-permute-done | bytes 307232 | tf_op jit(solution)/shard_map/cond/branch_4_fun/ppermute | solution.py:155
  48.7 5.2 %collective-permute-done.8 = f32[50,3,512]{2,1,0:T(4,128)S(1)} collective-permute-done((f32[50,3,512]{2,1,0:T(4,128)}, f32[50,3,512]{2,1,0:T(4,128)S(1)}, u32[]{:S(2)}, u32[]{:S(2)}) %collective-permute-start.8) | collective-permute-done | bytes 307232 | tf_op jit(solution)/shard_map/cond/branch_4_fun/ppermute | solution.py:154
  54.7 0.9 fusion.5
  55.7 1.1 pad_maximum_fusion.9
  58.1 1.5 %collective-permute-start.19 = (f32[50,3,72]{2,0,1:T(8,128)S(1)}, f32[50,3,72]{2,0,1:T(8,128)S(1)}, u32[]{:S(2)}, u32[]{:S(2)}) collective-permute-start(f32[50,3,72]{2,0,1:T(8,128)S(1)} %maximum_bitcast_fusion.1), channel_id=1, source_target_pairs={{0,16},{16,32},{32,48},{48,64},{64,80},{80,96},{96,112},{112,0},{1... | collective-permute-start | bytes 129608 | tf_op jit(solution)/shard_map/ppermute | solution.py:232
  60.4 1.4 %copy.73 = f32[50,8,512]{2,1,0:T(8,128)} copy(f32[50,8,512]{2,0,1:T(8,128)S(1)} %pad_maximum_fusion.9) | data formatting | bytes 1638400 | tf_op jit(solution)/shard_map/concatenate | solution.py:208
  62.8 1.9 %copy.81 = f32[50,72,3]{2,1,0:T(8,128)} copy(f32[50,72,3]{1,0,2:T(8,128)S(1)} %bitcast.54) | data formatting | bytes 86400 | tf_op jit(solution)/shard_map/transpose | solution.py:232
  64.6 3.3 %pad_maximum_fusion.8 = f32[50,72,128]{2,1,0:T(8,128)} fusion(f32[50,72,3]{2,1,0:T(8,128)} %copy.81, f32[50,72,3]{2,1,0:T(8,128)S(1)} %copy.80, f32[128]{0:T(128)S(1)} %pad.22.clone), kind=kLoop, calls=%fused_computation.14 | loop fusion | flops 921600 | bytes 1930112 | tf_op jit(solution)/shard_map/concatenate | solution.py:235
  67.9 20.9 %shard_map.109 = f32[4,10,64,512]{3,2,1,0:T(8,128)} custom-call(f32[4,10,64,512]{3,2,1,0:T(8,128)} %adj_ref.1, s32[10,64,512]{2,1,0:T(8,128)} %mask_ref.3, f32[10,64,512]{2,1,0:T(8,128)} %diff_ref.1, f32[5,10,8,512]{3,2,1,0:T(8,128)} %bitcast.46, f32[5,10,72,128]{3,2,1,0:T(8,128)} %bitcast.42, f32[64,1]{1,0:T(8,128)} %copy.82.cor_ref), custom_call_target="tpu_custom_call" | custom-call | tf_op jit(solution)/shard_map/pallas_call | solution.py:60
  89.7 0.9 reshape.238.vals_ref
  92.3 32.9 %shard_map.110 = f32[40,64,512]{2,1,0:T(8,128)} custom-call(s32[4,1024]{1,0:T(4,128)} %pad_add_fusion.where_ref, f32[1024]{0:T(1024)} %reshape_squeeze.4.weight_ref, f32[1024,128]{1,0:T(8,128)} %reshape.238.vals_ref, f32[40,64,512]{2,1,0:T(8,128)} %bitcast.43, s32[10,64,512]{2,1,0:T(8,128)} %mask_ref.3, f32[40,64,512]{2,1,0:T(8,128)} %bitcast.41), custom_call_target="tpu_custom_call" | custom-call | tf_op jit(solution)/shard_map/pallas_call | solution.py:117
  (61 shorter events, 9.2 us)
Async XLA Ops:
  0.0 4.3 %copy-start = (f32[512,128]{1,0:T(8,128)S(1)}, f32[512,128]{1,0:T(8,128)}, u32[]{:S(2)}) copy-start(f32[512,128]{1,0:T(8,128)} %param.24) | copy-start | bytes 786436
  6.3 12.4 %copy-start.1 = (s32[10,64,512]{2,1,0:T(8,128)S(1)}, s32[10,64,512]{2,1,0:T(8,128)}, u32[]{:S(2)}) copy-start(s32[10,64,512]{2,1,0:T(8,128)} %mask_ref.3) | copy-start | bytes 3932164
  6.4 12.4 %copy-start.6 = (f32[4]{0:T(128)S(1)}, f32[4]{0:T(128)}, u32[]{:S(2)}) copy-start(f32[4]{0:T(128)} %constant.118.clone) | copy-start | bytes 52
  7.6 81.2 %all-to-all-start = ((f32[128,1,1152]{2,1,0:T(1,128)}), f32[128,1,1152]{2,1,0:T(1,128)S(1)}, u32[]{:S(2)}, u32[]{:S(2)}) async-start(f32[128,1,1152]{2,1,0:T(1,128)} %all_to_all.8), calls=%async_computation | async-start | bytes 1179648 | tf_op jit(solution)/shard_map/all_to_all | solution.py:263
  21.2 33.5 %collective-permute-start.16 = (f32[50,3,512]{2,0,1:T(8,128)}, f32[50,3,512]{2,0,1:T(8,128)}, u32[]{:S(2)}, u32[]{:S(2)}) collective-permute-start(f32[50,3,512]{2,0,1:T(8,128)} %pad_maximum_fusion.12), channel_id=1, source_target_pairs={{1,0},{2,1},{3,2},{4,3},{5,4},{6,5},{7,6},{8,7},{9,8},{10,9},{11,1... | collective-permute-start | bytes 921608 | tf_op jit(solution)/shard_map/ppermute | solution.py:198
  25.0 30.7 %collective-permute-start.17 = (f32[50,3,512]{2,0,1:T(8,128)}, f32[50,3,512]{2,0,1:T(8,128)}, u32[]{:S(2)}, u32[]{:S(2)}) collective-permute-start(f32[50,3,512]{2,0,1:T(8,128)} %pad_maximum_fusion.13), channel_id=1, source_target_pairs={{0,1},{1,2},{2,3},{3,4},{4,5},{5,6},{6,7},{7,8},{8,9},{9,10},{10,1... | collective-permute-start | bytes 921608 | tf_op jit(solution)/shard_map/ppermute | solution.py:197
  30.1 2.5 %copy-start.2 = (f32[10,64,512]{2,1,0:T(8,128)S(1)}, f32[10,64,512]{2,1,0:T(8,128)}, u32[]{:S(2)}) copy-start(f32[10,64,512]{2,1,0:T(8,128)} %diff_ref.1) | copy-start | bytes 3932164
  38.2 10.5 %collective-permute-start.9 = (f32[50,3,512]{2,1,0:T(4,128)}, f32[50,3,512]{2,1,0:T(4,128)S(1)}, u32[]{:S(2)}, u32[]{:S(2)}) collective-permute-start(f32[50,3,512]{2,1,0:T(4,128)} %param.4), channel_id=1, source_target_pairs={{79,15},{63,31},{47,47},{31,63},{15,79},{127,95},{111,111},{95,127}} | collective-permute-start | bytes 921608 | tf_op jit(solution)/shard_map/cond/branch_4_fun/ppermute | solution.py:155
  41.9 12.0 %collective-permute-start.8 = (f32[50,3,512]{2,1,0:T(4,128)}, f32[50,3,512]{2,1,0:T(4,128)S(1)}, u32[]{:S(2)}, u32[]{:S(2)}) collective-permute-start(f32[50,3,512]{2,1,0:T(4,128)} %param.4), channel_id=1, source_target_pairs={{63,15},{47,31},{31,47},{15,63},{127,79},{111,95},{95,111},{79,127}} | collective-permute-start | bytes 921608 | tf_op jit(solution)/shard_map/cond/branch_4_fun/ppermute | solution.py:154
  55.6 2.2 %copy-start.4 = (f32[10,64,3]{1,0,2:T(8,128)S(1)}, f32[10,64,3]{1,0,2:T(8,128)}, u32[]{:S(2)}) copy-start(f32[10,64,3]{1,0,2:T(8,128)} %copy.97) | copy-start | bytes 23044
  55.6 2.3 %copy-start.3 = (f32[10,64,3]{1,0,2:T(8,128)S(1)}, f32[10,64,3]{1,0,2:T(8,128)}, u32[]{:S(2)}) copy-start(f32[10,64,3]{1,0,2:T(8,128)} %copy.98) | copy-start | bytes 23044
  55.7 4.0 %copy-start.5 = (f32[64]{0:T(128)S(1)}, f32[64]{0:T(128)}, u32[]{:S(2)}) copy-start(f32[64]{0:T(128)} %param.23) | copy-start | bytes 772
  57.9 3.9 %collective-permute-start.18 = (f32[50,3,72]{2,0,1:T(8,128)S(1)}, f32[50,3,72]{2,0,1:T(8,128)S(1)}, u32[]{:S(2)}, u32[]{:S(2)}) collective-permute-start(f32[50,3,72]{2,0,1:T(8,128)S(1)} %maximum_bitcast_fusion), channel_id=1, source_target_pairs={{0,112},{16,0},{32,16},{48,32},{64,48},{80,64},{96,80},{112,96},{1... | collective-permute-start | bytes 129608 | tf_op jit(solution)/shard_map/ppermute | solution.py:231
  58.1 4.7 %collective-permute-start.19 = (f32[50,3,72]{2,0,1:T(8,128)S(1)}, f32[50,3,72]{2,0,1:T(8,128)S(1)}, u32[]{:S(2)}, u32[]{:S(2)}) collective-permute-start(f32[50,3,72]{2,0,1:T(8,128)S(1)} %maximum_bitcast_fusion.1), channel_id=1, source_target_pairs={{0,16},{16,32},{32,48},{48,64},{64,80},{80,96},{96,112},{112,0},{1... | collective-permute-start | bytes 129608 | tf_op jit(solution)/shard_map/ppermute | solution.py:232

commit v3 on v2

--- a/solution.py
+++ b/solution.py
@@ -86,26 +86,18 @@
         first = pl.multiple_of(o * 8, 8)
         vals8 = vals_ref[pl.ds(first, 8), :]
         for j in range(8):
-            i = first + j
-
-            @pl.when(weight_ref[i] != 0.0)
-            def _():
-                add_row(i, vals8[j : j + 1, :])
-
+            add_row(first + j, vals8[j : j + 1, :])
         return carry
 
     def add_row(i, value):
         layer = where_ref[0, i]
-        row = where_ref[1, i]
-        col = pl.multiple_of(where_ref[2, i], seg_width)
+        rows = pl.ds(pl.multiple_of(where_ref[1, i], 8), 8)
+        cols = pl.ds(pl.multiple_of(where_ref[2, i], seg_width), seg_width)
         level = where_ref[3, i]
-        tile = pl.multiple_of((row // 8) * 8, 8)
-        rows = pl.ds(tile, 8)
-        cols = pl.ds(col, seg_width)
         sampled = traj_ref[layer, rows, cols]
         misfit = weight_ref[i] * (sampled - value)
         wet = mask_ref[level, rows, cols].astype(jnp.float32)
-        hit = sub == row - tile
+        hit = sub == where_ref[4, i]
         cur = out_ref[layer, rows, cols]
         out_ref[layer, rows, cols] = cur + jnp.where(hit, wet * misfit, 0.0)
 
@@ -260,7 +252,10 @@
     send_meta = jnp.swapaxes(send_meta, 1, 2).reshape(devices, 2 * CAP)
     send_meta = jnp.pad(send_meta, ((0, 0), (0, seg_width - 2 * CAP)))
     send = jnp.concatenate([send_values.reshape(devices, CAP * seg_width), send_meta], axis=1)
-    got = lax.all_to_all(send, ("lon", "lat"), split_axis=0, concat_axis=0, tiled=True)
+    send = send.reshape(lon_count, lat_count, send.shape[1])
+    hop = lax.all_to_all(send, "lat", split_axis=1, concat_axis=1, tiled=True)
+    got = lax.all_to_all(hop, "lon", split_axis=0, concat_axis=0, tiled=True)
+    got = got.reshape(devices, got.shape[2])
     got_values = got[:, : CAP * seg_width].reshape(devices * CAP, seg_width)
     got_meta = got[:, CAP * seg_width : CAP * seg_width + 2 * CAP].reshape(devices, 2, CAP)
     got_weight = got_meta[:, 0, :].reshape(devices * CAP)
@@ -271,7 +266,9 @@
     rest = got_offset // segments
     row_local = rest % h
     layer = rest // h
-    where = jnp.stack([layer, row_local, seg_local * seg_width, layer % levels], axis=0)
+    where = jnp.stack(
+        [layer, row_local // 8 * 8, seg_local * seg_width, layer % levels, row_local % 8], axis=0
+    )
     out3 = obs_call(
         where,
         got_weight,

time: 126 us -> 117 us (0.929)
  the two profiles are of different devices: /device:TPU:123 before, /device:TPU:95 now
where the time goes in v3:
time: 117 us; the launch traced here: 115 us
  Pallas kernels  39 us (33%)
  starting transfers between devices  25.8 us (22%)
  local copies, waits for them, and re-layouts  18.3 us (16%)
  other arithmetic  14.8 us (13%)
  waiting for transfers between devices  10.5 us (9%)
  matrix products  5.41 us (5%)
    pallas_call x1, Pallas kernels, mix_call(): pl.pallas_call(mix_kernel, grid=(levels,), in_specs=[pl.BlockSpec((fields...  20.9 us
    pallas_call x1, Pallas kernels, obs_call(): pl.pallas_call(obs_kernel, grid_spec=pltpu.PrefetchScalarGridSpec(num_sca...  18.1 us
    all_to_all x1, starting transfers between devices, per_device(): hop = lax.all_to_all(send, 'lat', split_axis=1, concat_axis=1, tiled=True)  7.43 us
    ppermute x1, waiting for transfers between devices, run(): got_b = lax.ppermute(msg, ('lon', 'lat'), pairs_b)  5.14 us
    all_to_all x1, starting transfers between devices, per_device(): got = lax.all_to_all(hop, 'lon', split_axis=0, concat_axis=0, tiled=True)  5.01 us
    dot_general x3, matrix products, exact_dot(): lax.dot_general(left, right, (((left_dim,), (0,)), ((), ())), precision=l...  4.34 us
    ppermute x1, waiting for transfers between devices, run(): got_a = lax.ppermute(msg, ('lon', 'lat'), pairs_a)  4.28 us
    unnamed x19, local copies, waits for them, and re-layouts  3.76 us
  transfers between devices with their start and end apart: 8, of which 3 were waited for; matrix products, arithmetic and copies ran while one was open for 24% of the time, Pallas kernels for 18%

profile of v3, /device:TPU:95, one launch (start us, length us, event | category | flops | bytes accessed | tf_op | source)
XLA Modules:
  0.0 115.0 jit_solution(8932494830241942268)
XLA Ops:
  0.7 1.1 fusion.8
  2.5 1.5 %fusion = f32[1024,2]{0,1:T(2,128)S(1)} fusion(s32[512]{0:T(512)S(1)} %bitcast.60, f32[512,1]{0,1:T(1,128)S(1)} %bitcast.62, f32[512,1]{0,1:T(1,128)} %bitcast.64), kind=kOutput, calls=%fused_computation.10 | convolution fusion | flops 13108224 | bytes 14336 | tf_op jit(solution)/shard_map/dot_general | solution.py:18
  4.3 1.9 %fusion.1 = f32[1024,128]{1,0:T(8,128)S(1)} fusion(f32[512,128]{1,0:T(8,128)S(1)} %copy-done, s32[512]{0:T(512)S(1)} %bitcast.61), kind=kOutput, calls=%fused_computation.11 | convolution fusion | flops 805830656 | bytes 788480 | tf_op jit(solution)/shard_map/dot_general | solution.py:18
  7.5 7.4 %all-to-all-start = ((f32[8,16,1152]{2,0,1:T(8,128)}), f32[8,16,1152]{2,0,1:T(8,128)S(1)}, u32[]{:S(2)}, u32[]{:S(2)}) async-start(f32[8,16,1152]{2,0,1:T(8,128)} %pad_maximum_fusion.10), calls=%async_computation | async-start | bytes 1179648 | tf_op jit(solution)/shard_map/all_to_all | solution.py:256
  15.0 1.0 fusion.24
  16.1 1.5 %broadcast_multiply_fusion = (f32[4,10,3,512]{3,2,1,0:T(4,128)S(1)}, f32[4,10,3,512]{3,2,1,0:T(4,128)S(1)}, f32[4,10,3,512]{3,2,1,0:T(4,128)S(1)}) fusion(f32[4]{0:T(128)S(1)} %copy-done.6, f32[10,3,512]{2,1,0:T(4,128)S(1)} %get-tuple-element.40, f32[4,10,64,512]{3,2,1,0:T(8,128)} %adj_ref.1, f32[10,3,512]{2,1,0:T(4,128)S(1)} %get-tuple-element.39), kind=kLoop, calls=%fused_computation.42 | loop fusion | flops 184320 | bytes 1351696 | tf_op jit(solution)/shard_map/mul | solution.py:192
  18.5 3.0 %collective-permute-start.16 = (f32[50,3,512]{2,0,1:T(8,128)}, f32[50,3,512]{2,0,1:T(8,128)}, u32[]{:S(2)}, u32[]{:S(2)}) collective-permute-start(f32[50,3,512]{2,0,1:T(8,128)} %pad_maximum_fusion.13), channel_id=1, source_target_pairs={{1,0},{2,1},{3,2},{4,3},{5,4},{6,5},{7,6},{8,7},{9,8},{10,9},{11,1... | collective-permute-start | bytes 921608 | tf_op jit(solution)/shard_map/ppermute | solution.py:190
  22.4 1.3 %collective-permute-start.17 = (f32[50,3,512]{2,0,1:T(8,128)}, f32[50,3,512]{2,0,1:T(8,128)}, u32[]{:S(2)}, u32[]{:S(2)}) collective-permute-start(f32[50,3,512]{2,0,1:T(8,128)} %pad_maximum_fusion.14), channel_id=1, source_target_pairs={{0,1},{1,2},{2,3},{3,4},{4,5},{5,6},{6,7},{7,8},{8,9},{9,10},{10,1... | collective-permute-start | bytes 921608 | tf_op jit(solution)/shard_map/ppermute | solution.py:189
  23.7 1.2 %slice.70 = s32[1]{0:T(128)} slice(s32[512]{0:T(512)} %param.28), slice={[0:1]} | slice | bytes 8 | tf_op jit(solution)/shard_map/slice | solution.py:133
  25.5 1.0 slice_convert_fusion.1
  26.5 1.0 fusion.12
  27.5 2.5 %slice_multiply_fusion.1 = (f32[4,10,64,3]{3,2,1,0:T(8,128)S(1)}, f32[4,10,64,3]{3,2,1,0:T(8,128)S(1)}) fusion(f32[4,10,64,512]{3,2,1,0:T(8,128)} %adj_ref.1, f32[10,64,3]{2,1,0:T(8,128)} %get-tuple-element.35, f32[10,64,3]{2,1,0:T(8,128)} %get-tuple-element.36), kind=kLoop, calls=%fused_computation.16 | loop fusion | flops 15360 | bytes 138240 | tf_op jit(solution)/shard_map/mul | solution.py:203
  30.0 0.9 fusion.23
  30.9 1.8 %copy.116 = f32[10,64,3]{1,0,2:T(8,128)} copy(f32[10,64,3]{2,1,0:T(8,128)} %get-tuple-element.37) | data formatting | bytes 15360
  32.7 1.8 %copy.117 = f32[10,64,3]{1,0,2:T(8,128)} copy(f32[10,64,3]{2,1,0:T(8,128)} %get-tuple-element.38) | data formatting | bytes 15360
  35.5 15.6 %conditional.1 = (f32[50,3,1024]{2,0,1:T(8,128)S(1)}) conditional(s32[]{:T(128)} %clamp.3, f32[50,3,512]{2,1,0:T(4,128)} %fusion.12, f32[50,3,512]{2,1,0:T(4,128)} %fusion.12, f32[50,3,512]{2,1,0:T(4,128)} %fusion.12, f32[50,3,512]{2,1,0:T(4,128)} %fusion.12, f32[50,3,512]{2,1,0:T(4,128)} %fusion.12, ...), branch_computations={%region_1.2_spmd, %region_2.3_spmd, %region_3.4_spmd, %region_4.5_... | conditional | flops 153600 | bytes 4915288 | solution.py:152
  35.5 3.0 %collective-permute-start.9 = (f32[50,3,512]{2,1,0:T(4,128)}, f32[50,3,512]{2,1,0:T(4,128)S(1)}, u32[]{:S(2)}, u32[]{:S(2)}) collective-permute-start(f32[50,3,512]{2,1,0:T(4,128)} %param.4), channel_id=1, source_target_pairs={{79,15},{63,31},{47,47},{31,63},{15,79},{127,95},{111,111},{95,127}} | collective-permute-start | bytes 921608 | tf_op jit(solution)/shard_map/cond/branch_4_fun/ppermute | solution.py:147
  38.6 2.3 %collective-permute-start.8 = (f32[50,3,512]{2,1,0:T(4,128)}, f32[50,3,512]{2,1,0:T(4,128)S(1)}, u32[]{:S(2)}, u32[]{:S(2)}) collective-permute-start(f32[50,3,512]{2,1,0:T(4,128)} %param.4), channel_id=1, source_target_pairs={{63,15},{47,31},{31,47},{15,63},{127,79},{111,95},{95,111},{79,127}} | collective-permute-start | bytes 921608 | tf_op jit(solution)/shard_map/cond/branch_4_fun/ppermute | solution.py:146
  40.9 5.1 %collective-permute-done.9 = f32[50,3,512]{2,1,0:T(4,128)S(1)} collective-permute-done((f32[50,3,512]{2,1,0:T(4,128)}, f32[50,3,512]{2,1,0:T(4,128)S(1)}, u32[]{:S(2)}, u32[]{:S(2)}) %collective-permute-start.9) | collective-permute-done | bytes 307232 | tf_op jit(solution)/shard_map/cond/branch_4_fun/ppermute | solution.py:147
  46.0 4.3 %collective-permute-done.8 = f32[50,3,512]{2,1,0:T(4,128)S(1)} collective-permute-done((f32[50,3,512]{2,1,0:T(4,128)}, f32[50,3,512]{2,1,0:T(4,128)S(1)}, u32[]{:S(2)}, u32[]{:S(2)}) %collective-permute-start.8) | collective-permute-done | bytes 307232 | tf_op jit(solution)/shard_map/cond/branch_4_fun/ppermute | solution.py:146
  51.1 0.9 fusion.5
  52.1 1.1 pad_maximum_fusion.9
  54.2 1.0 copy.82
  55.2 5.0 %all-to-all-start.1 = ((f32[8,16,1152]{2,1,0:T(8,128)}), f32[8,16,1152]{2,1,0:T(8,128)S(1)}, u32[]{:S(2)}, u32[]{:S(2)}) async-start(f32[8,16,1152]{2,1,0:T(8,128)} %copy.82), calls=%async_computation.1 | async-start | bytes 1179648 | tf_op jit(solution)/shard_map/all_to_all | solution.py:257
  61.1 3.1 %collective-permute-start.19 = (f32[50,3,72]{2,0,1:T(8,128)S(1)}, f32[50,3,72]{2,0,1:T(8,128)S(1)}, u32[]{:S(2)}, u32[]{:S(2)}) collective-permute-start(f32[50,3,72]{2,0,1:T(8,128)S(1)} %maximum_bitcast_fusion.1), channel_id=1, source_target_pairs={{0,16},{16,32},{32,48},{48,64},{64,80},{80,96},{96,112},{112,0},{1... | collective-permute-start | bytes 129608 | tf_op jit(solution)/shard_map/ppermute | solution.py:224
  64.9 1.4 %copy.92 = f32[50,8,512]{2,1,0:T(8,128)} copy(f32[50,8,512]{2,0,1:T(8,128)S(1)} %pad_maximum_fusion.9) | data formatting | bytes 1638400 | tf_op jit(solution)/shard_map/concatenate | solution.py:200
  66.4 1.1 collective-permute-done.18
  68.0 1.9 %copy.100 = f32[50,72,3]{2,1,0:T(8,128)} copy(f32[50,72,3]{1,0,2:T(8,128)S(1)} %bitcast.55) | data formatting | bytes 86400 | tf_op jit(solution)/shard_map/transpose | solution.py:224
  69.9 3.3 %pad_maximum_fusion.8 = f32[50,72,128]{2,1,0:T(8,128)} fusion(f32[50,72,3]{2,1,0:T(8,128)} %copy.100, f32[50,72,3]{2,1,0:T(8,128)S(1)} %copy.99, f32[128]{0:T(128)S(1)} %pad.22.clone), kind=kLoop, calls=%fused_computation.14 | loop fusion | flops 921600 | bytes 1930112 | tf_op jit(solution)/shard_map/concatenate | solution.py:227
  73.2 20.9 %shard_map.109 = f32[4,10,64,512]{3,2,1,0:T(8,128)} custom-call(f32[4,10,64,512]{3,2,1,0:T(8,128)} %adj_ref.1, s32[10,64,512]{2,1,0:T(8,128)} %mask_ref.3, f32[10,64,512]{2,1,0:T(8,128)} %diff_ref.1, f32[5,10,8,512]{3,2,1,0:T(8,128)} %bitcast.46, f32[5,10,72,128]{3,2,1,0:T(8,128)} %bitcast.42, f32[64,1]{1,0:T(8,128)} %copy.101.cor_ref), custom_call_target="tpu_custom_call" | custom-call | tf_op jit(solution)/shard_map/pallas_call | solution.py:60
  94.2 0.9 reshape.315.vals_ref
  96.9 18.1 %shard_map.110 = f32[40,64,512]{2,1,0:T(8,128)} custom-call(s32[5,1024]{1,0:T(8,128)} %stack.20.where_ref, f32[1024]{0:T(1024)} %reshape_squeeze.4.weight_ref, f32[1024,128]{1,0:T(8,128)} %reshape.315.vals_ref, f32[40,64,512]{2,1,0:T(8,128)} %bitcast.43, s32[10,64,512]{2,1,0:T(8,128)} %mask_ref.3, f32[40,64,512]{2,1,0:T(8,128)} %bitcast.41), custom_call_target="tpu_custom_call" | custom-call | tf_op jit(solution)/shard_map/pallas_call | solution.py:109
  (65 shorter events, 11.4 us)
Async XLA Ops:
  0.0 4.3 %copy-start = (f32[512,128]{1,0:T(8,128)S(1)}, f32[512,128]{1,0:T(8,128)}, u32[]{:S(2)}) copy-start(f32[512,128]{1,0:T(8,128)} %param.24) | copy-start | bytes 786436
  6.3 9.7 %copy-start.1 = (s32[10,64,512]{2,1,0:T(8,128)S(1)}, s32[10,64,512]{2,1,0:T(8,128)}, u32[]{:S(2)}) copy-start(s32[10,64,512]{2,1,0:T(8,128)} %mask_ref.3) | copy-start | bytes 3932164
  6.7 9.4 %copy-start.6 = (f32[4]{0:T(128)S(1)}, f32[4]{0:T(128)}, u32[]{:S(2)}) copy-start(f32[4]{0:T(128)} %constant.136.clone) | copy-start | bytes 52
  7.5 46.7 %all-to-all-start = ((f32[8,16,1152]{2,0,1:T(8,128)}), f32[8,16,1152]{2,0,1:T(8,128)S(1)}, u32[]{:S(2)}, u32[]{:S(2)}) async-start(f32[8,16,1152]{2,0,1:T(8,128)} %pad_maximum_fusion.10), calls=%async_computation | async-start | bytes 1179648 | tf_op jit(solution)/shard_map/all_to_all | solution.py:256
  18.5 32.7 %collective-permute-start.16 = (f32[50,3,512]{2,0,1:T(8,128)}, f32[50,3,512]{2,0,1:T(8,128)}, u32[]{:S(2)}, u32[]{:S(2)}) collective-permute-start(f32[50,3,512]{2,0,1:T(8,128)} %pad_maximum_fusion.13), channel_id=1, source_target_pairs={{1,0},{2,1},{3,2},{4,3},{5,4},{6,5},{7,6},{8,7},{9,8},{10,9},{11,1... | collective-permute-start | bytes 921608 | tf_op jit(solution)/shard_map/ppermute | solution.py:190
  22.4 29.7 %collective-permute-start.17 = (f32[50,3,512]{2,0,1:T(8,128)}, f32[50,3,512]{2,0,1:T(8,128)}, u32[]{:S(2)}, u32[]{:S(2)}) collective-permute-start(f32[50,3,512]{2,0,1:T(8,128)} %pad_maximum_fusion.14), channel_id=1, source_target_pairs={{0,1},{1,2},{2,3},{3,4},{4,5},{5,6},{6,7},{7,8},{8,9},{9,10},{10,1... | collective-permute-start | bytes 921608 | tf_op jit(solution)/shard_map/ppermute | solution.py:189
  27.5 2.5 %copy-start.2 = (f32[10,64,512]{2,1,0:T(8,128)S(1)}, f32[10,64,512]{2,1,0:T(8,128)}, u32[]{:S(2)}) copy-start(f32[10,64,512]{2,1,0:T(8,128)} %diff_ref.1) | copy-start | bytes 3932164
  35.5 10.5 %collective-permute-start.9 = (f32[50,3,512]{2,1,0:T(4,128)}, f32[50,3,512]{2,1,0:T(4,128)S(1)}, u32[]{:S(2)}, u32[]{:S(2)}) collective-permute-start(f32[50,3,512]{2,1,0:T(4,128)} %param.4), channel_id=1, source_target_pairs={{79,15},{63,31},{47,47},{31,63},{15,79},{127,95},{111,111},{95,127}} | collective-permute-start | bytes 921608 | tf_op jit(solution)/shard_map/cond/branch_4_fun/ppermute | solution.py:147
  38.6 11.8 %collective-permute-start.8 = (f32[50,3,512]{2,1,0:T(4,128)}, f32[50,3,512]{2,1,0:T(4,128)S(1)}, u32[]{:S(2)}, u32[]{:S(2)}) collective-permute-start(f32[50,3,512]{2,1,0:T(4,128)} %param.4), channel_id=1, source_target_pairs={{63,15},{47,31},{31,47},{15,63},{127,79},{111,95},{95,111},{79,127}} | collective-permute-start | bytes 921608 | tf_op jit(solution)/shard_map/cond/branch_4_fun/ppermute | solution.py:146
  53.2 7.0 %copy-start.4 = (f32[10,64,3]{1,0,2:T(8,128)S(1)}, f32[10,64,3]{1,0,2:T(8,128)}, u32[]{:S(2)}) copy-start(f32[10,64,3]{1,0,2:T(8,128)} %copy.116) | copy-start | bytes 23044
  53.4 7.6 %copy-start.3 = (f32[10,64,3]{1,0,2:T(8,128)S(1)}, f32[10,64,3]{1,0,2:T(8,128)}, u32[]{:S(2)}) copy-start(f32[10,64,3]{1,0,2:T(8,128)} %copy.117) | copy-start | bytes 23044
  53.4 10.8 %copy-start.5 = (f32[64]{0:T(128)S(1)}, f32[64]{0:T(128)}, u32[]{:S(2)}) copy-start(f32[64]{0:T(128)} %param.23) | copy-start | bytes 772
  55.2 38.9 %all-to-all-start.1 = ((f32[8,16,1152]{2,1,0:T(8,128)}), f32[8,16,1152]{2,1,0:T(8,128)S(1)}, u32[]{:S(2)}, u32[]{:S(2)}) async-start(f32[8,16,1152]{2,1,0:T(8,128)} %copy.82), calls=%async_computation.1 | async-start | bytes 1179648 | tf_op jit(solution)/shard_map/all_to_all | solution.py:257
  60.3 7.1 %collective-permute-start.18 = (f32[50,3,72]{2,0,1:T(8,128)S(1)}, f32[50,3,72]{2,0,1:T(8,128)S(1)}, u32[]{:S(2)}, u32[]{:S(2)}) collective-permute-start(f32[50,3,72]{2,0,1:T(8,128)S(1)} %maximum_bitcast_fusion), channel_id=1, source_target_pairs={{0,112},{16,0},{32,16},{48,32},{64,48},{80,64},{96,80},{112,96},{1... | collective-permute-start | bytes 129608 | tf_op jit(solution)/shard_map/ppermute | solution.py:223
  61.1 7.0 %collective-permute-start.19 = (f32[50,3,72]{2,0,1:T(8,128)S(1)}, f32[50,3,72]{2,0,1:T(8,128)S(1)}, u32[]{:S(2)}, u32[]{:S(2)}) collective-permute-start(f32[50,3,72]{2,0,1:T(8,128)S(1)} %maximum_bitcast_fusion.1), channel_id=1, source_target_pairs={{0,16},{16,32},{32,48},{48,64},{64,80},{80,96},{96,112},{112,0},{1... | collective-permute-start | bytes 129608 | tf_op jit(solution)/shard_map/ppermute | solution.py:224

commit v4 on v3

--- a/solution.py
+++ b/solution.py
@@ -200,33 +200,31 @@
     rows_all = jnp.concatenate([north, gap, from_below], axis=1)
     rows5 = rows_all.reshape(fields + 1, levels, PAD_ROWS, w)
 
-    work_first = adjoint[:, :, :, :HALO] * land_mask[None, :, :, :HALO].astype(jnp.float32)
-    work_last = adjoint[:, :, :, w - HALO :] * land_mask[None, :, :, w - HALO :].astype(jnp.float32)
-    first = jnp.concatenate(
-        [
-            jnp.concatenate([work_first.reshape(n_work, h, HALO), diffusivity[:, :, :HALO]], 0),
-            rows_all[:, :, :HALO],
-        ],
-        axis=1,
-    )
-    last = jnp.concatenate(
-        [
-            jnp.concatenate([work_last.reshape(n_work, h, HALO), diffusivity[:, :, w - HALO :]], 0),
-            rows_all[:, :, w - HALO :],
-        ],
-        axis=1,
-    )
+    lane = lax.broadcasted_iota(jnp.int32, (PAD_LANES, PAD_ROWS), 0)
+    slot = lax.broadcasted_iota(jnp.int32, (PAD_LANES, PAD_ROWS), 1)
+    take_first = (slot < HALO) & (lane == slot)
+    take_last = (slot >= PAD_ROWS - HALO) & (lane == slot + PAD_LANES - PAD_ROWS)
+
+    def edges(block):
+        pick = lambda part, sel: jnp.einsum(
+            "nyx,xc->ncy", part, sel.astype(jnp.float32), precision=lax.Precision.HIGHEST
+        )
+        return pick(block[..., :PAD_LANES], take_first) + pick(block[..., w - PAD_LANES :], take_last)
+
+    wet_edges = edges(land_mask.astype(jnp.float32))
+    adj_edges = edges(adjoint.reshape(n_work, h, w)).reshape(fields, levels, PAD_ROWS, h)
+    work_edges = (adj_edges * wet_edges[None]).reshape(n_work, PAD_ROWS, h)
+    interior = jnp.concatenate([work_edges, edges(diffusivity)], axis=0)
+    col_msg = jnp.concatenate([interior, edges(rows_all)], axis=2)
     ring_west = [(i, (i - 1) % lon_count) for i in range(lon_count)]
     ring_east = [(i, (i + 1) % lon_count) for i in range(lon_count)]
-    first_t = jnp.swapaxes(first, 1, 2)
-    last_t = jnp.swapaxes(last, 1, 2)
-    east_halo = jnp.swapaxes(lax.ppermute(first_t, "lon", ring_west), 1, 2)
-    west_halo = jnp.swapaxes(lax.ppermute(last_t, "lon", ring_east), 1, 2)
-    hp = h + PAD_ROWS
-    middle = jnp.zeros((n_work + levels, hp, PAD_LANES - 2 * HALO), jnp.float32)
-    cols5 = jnp.concatenate([east_halo, middle, west_halo], axis=2).reshape(
-        fields + 1, levels, hp, PAD_LANES
-    )
+    from_east = lax.ppermute(col_msg, "lon", ring_west)
+    from_west = lax.ppermute(col_msg, "lon", ring_east)
+    halo_slot = lax.broadcasted_iota(jnp.int32, col_msg.shape, 1)
+    got_cols = jnp.where(halo_slot < HALO, from_east, from_west)
+    place = (take_first | take_last).astype(jnp.float32).T
+    cols5 = jnp.einsum("ncy,cl->nyl", got_cols, place, precision=lax.Precision.HIGHEST)
+    cols5 = cols5.reshape(fields + 1, levels, h + PAD_ROWS, PAD_LANES)
 
     mixed_wet = mix_call(adjoint, land_mask, diffusivity, rows5, cols5, coriolis)
 
@@ -252,10 +250,7 @@
     send_meta = jnp.swapaxes(send_meta, 1, 2).reshape(devices, 2 * CAP)
     send_meta = jnp.pad(send_meta, ((0, 0), (0, seg_width - 2 * CAP)))
     send = jnp.concatenate([send_values.reshape(devices, CAP * seg_width), send_meta], axis=1)
-    send = send.reshape(lon_count, lat_count, send.shape[1])
-    hop = lax.all_to_all(send, "lat", split_axis=1, concat_axis=1, tiled=True)
-    got = lax.all_to_all(hop, "lon", split_axis=0, concat_axis=0, tiled=True)
-    got = got.reshape(devices, got.shape[2])
+    got = lax.all_to_all(send, ("lon", "lat"), split_axis=0, concat_axis=0, tiled=True)
     got_values = got[:, : CAP * seg_width].reshape(devices * CAP, seg_width)
     got_meta = got[:, CAP * seg_width : CAP * seg_width + 2 * CAP].reshape(devices, 2, CAP)
     got_weight = got_meta[:, 0, :].reshape(devices * CAP)

time: 117 us -> 113 us (0.966)
  matrix products: 5.41 us -> 17.2 us
  local copies, waits for them, and re-layouts: 18.3 us -> 10.3 us
  other arithmetic: 14.8 us -> 8.55 us
  starting transfers between devices: 25.8 us -> 22.1 us
  waiting for transfers between devices: 10.5 us -> 13.1 us
    dot_general x0 -> x9, matrix products: none -> 11.8 us  [the longest x8 8.84 us: edges(): jnp.einsum('nyx,xc->ncy', part, sel.astype(jnp.float32), precision=lax.Pr...]
    unnamed x19 -> x25, local copies, waits for them, and re-layouts: 3.76 us -> 0.47 us
    concatenate x1, other arithmetic: 3.31 us -> 0.13 us  [per_device(): col_msg = jnp.concatenate([interior, edges(rows_all)], axis=2)]
    transpose x2 -> x0, local copies, waits for them, and re-layouts: 2.5 us -> none  [the longest x1 1.87 us: per_device(): west_halo = jnp.swapaxes(lax.ppermute(last_t, 'lon', ring_east), 1, 2)]
    mul x1 -> x0, other arithmetic: 2.47 us -> none  [per_device(): adjoint[:, :, :, :HALO] * land_mask[None, :, :, :HALO].astype(jnp.float32)]
    all_to_all x2 -> x1, starting transfers between devices: 12.4 us -> 10.2 us  [per_device(): lax.all_to_all(send, ('lon', 'lat'), split_axis=0, concat_axis=0, tiled=T...]
    ppermute x2, waiting for transfers between devices: 1.06 us -> 3.25 us  [the longest x1 2.19 us: per_device(): from_east = lax.ppermute(col_msg, 'lon', ring_west)]
    ppermute x2, starting transfers between devices: 3.71 us -> 1.53 us  [the longest x1 1.45 us: per_device(): from_east = lax.ppermute(col_msg, 'lon', ring_west)]
  transfers between devices with their start and end apart: 8 -> 7, of which waited for: 3 -> 4; matrix products, arithmetic and copies ran while one was open for 24% -> 20% of each run, Pallas kernels for 18% -> 19%
where the time goes in v4:
time: 113 us; the launch traced here: 111 us
  Pallas kernels  39 us (35%)
  starting transfers between devices  22.1 us (20%)
  matrix products  17.2 us (15%)
  waiting for transfers between devices  13.1 us (12%)
  local copies, waits for them, and re-layouts  10.3 us (9%)
  other arithmetic  8.55 us (8%)
    pallas_call x1, Pallas kernels, mix_call(): pl.pallas_call(mix_kernel, grid=(levels,), in_specs=[pl.BlockSpec((fields...  20.9 us
    pallas_call x1, Pallas kernels, obs_call(): pl.pallas_call(obs_kernel, grid_spec=pltpu.PrefetchScalarGridSpec(num_sca...  18.1 us
    all_to_all x1, starting transfers between devices, per_device(): lax.all_to_all(send, ('lon', 'lat'), split_axis=0, concat_axis=0, tiled=T...  10.2 us
    dot_general x8, matrix products, edges(): jnp.einsum('nyx,xc->ncy', part, sel.astype(jnp.float32), precision=lax.Pr...  8.84 us
    ppermute x1, waiting for transfers between devices, run(): got_a = lax.ppermute(msg, ('lon', 'lat'), pairs_a)  6.38 us
    dot_general x3, matrix products, exact_dot(): lax.dot_general(left, right, (((left_dim,), (0,)), ((), ())), precision=l...  4.34 us
    ppermute x1, waiting for transfers between devices, run(): got_b = lax.ppermute(msg, ('lon', 'lat'), pairs_b)  3.47 us
    ppermute x1, starting transfers between devices, run(): got_b = lax.ppermute(msg, ('lon', 'lat'), pairs_b)  3.34 us
  transfers between devices with their start and end apart: 7, of which 4 were waited for; matrix products, arithmetic and copies ran while one was open for 20% of the time, Pallas kernels for 19%

profile of v4, /device:TPU:95, one launch (start us, length us, event | category | flops | bytes accessed | tf_op | source)
XLA Modules:
  0.0 111.4 jit_solution(12319278907978606347)
XLA Ops:
  0.0 0.7 convert_element_type.78
  0.7 1.1 fusion.21
  2.5 1.5 %fusion = f32[1024,2]{0,1:T(2,128)S(1)} fusion(s32[512]{0:T(512)S(1)} %bitcast.76, f32[512,1]{0,1:T(1,128)S(1)} %bitcast.78, f32[512,1]{0,1:T(1,128)} %bitcast.80), kind=kOutput, calls=%fused_computation.10 | convolution fusion | flops 13108224 | bytes 14336 | tf_op jit(solution)/shard_map/dot_general | solution.py:18
  4.3 1.9 %fusion.1 = f32[1024,128]{1,0:T(8,128)S(1)} fusion(f32[512,128]{1,0:T(8,128)S(1)} %copy-done, s32[512]{0:T(512)S(1)} %bitcast.77), kind=kOutput, calls=%fused_computation.11 | convolution fusion | flops 805830656 | bytes 788480 | tf_op jit(solution)/shard_map/dot_general | solution.py:18
  6.2 0.9 reshape_reshape.3
  7.1 1.2 %select_maximum_fusion = f32[128,1152]{1,0:T(8,128)S(1)} fusion(f32[128,16]{1,0:T(8,128)S(1)} %copy.84, f32[128,1024]{1,0:T(8,128)} %reshape_reshape.3), kind=kLoop, calls=%fused_computation.35 | loop fusion | flops 442368 | bytes 1122304 | tf_op jit(solution)/shard_map/concatenate | solution.py:252
  8.3 1.2 %all_to_all.8 = f32[128,1,1152]{2,1,0:T(1,128)} reshape(f32[128,1152]{1,0:T(8,128)S(1)} %select_maximum_fusion) | data formatting | bytes 1179648 | tf_op jit(solution)/shard_map/all_to_all | solution.py:253
  9.6 10.2 %all-to-all-start = ((f32[128,1,1152]{2,1,0:T(1,128)}), f32[128,1,1152]{2,1,0:T(1,128)S(1)}, u32[]{:S(2)}, u32[]{:S(2)}) async-start(f32[128,1,1152]{2,1,0:T(1,128)} %all_to_all.8), calls=%async_computation | async-start | bytes 1179648 | tf_op jit(solution)/shard_map/all_to_all | solution.py:253
  19.9 2.3 %broadcast_multiply_fusion = (f32[4,10,3,512]{3,2,1,0:T(4,128)}, f32[4,10,3,512]{3,2,1,0:T(4,128)S(1)}, f32[4,10,3,512]{3,2,1,0:T(4,128)S(1)}) fusion(f32[4]{0:T(128)} %constant.144.clone, f32[10,3,512]{2,1,0:T(4,128)S(1)} %get-tuple-element.34, f32[4,10,64,512]{3,2,1,0:T(8,128)} %adj_ref.1, f32[10,3,512]{2,1,0:T(4,128)S(1)} %get-tuple-element.33), kind=kLoop, calls=%fused_computation.62 | loop fusion | flops 184320 | bytes 1351696 | tf_op jit(solution)/shard_map/mul | solution.py:192
  22.2 0.8 pad_maximum_fusion.11
  23.0 3.0 %collective-permute-start.16 = (f32[50,3,512]{2,0,1:T(8,128)}, f32[50,3,512]{2,0,1:T(8,128)}, u32[]{:S(2)}, u32[]{:S(2)}) collective-permute-start(f32[50,3,512]{2,0,1:T(8,128)} %pad_maximum_fusion.11), channel_id=1, source_target_pairs={{1,0},{2,1},{3,2},{4,3},{5,4},{6,5},{7,6},{8,7},{9,8},{10,9},{11,1... | collective-permute-start | bytes 921608 | tf_op jit(solution)/shard_map/ppermute | solution.py:190
  26.1 0.8 pad_maximum_fusion.12
  26.9 1.3 %collective-permute-start.17 = (f32[50,3,512]{2,0,1:T(8,128)}, f32[50,3,512]{2,0,1:T(8,128)}, u32[]{:S(2)}, u32[]{:S(2)}) collective-permute-start(f32[50,3,512]{2,0,1:T(8,128)} %pad_maximum_fusion.12), channel_id=1, source_target_pairs={{0,1},{1,2},{2,3},{3,4},{4,5},{5,6},{6,7},{7,8},{8,9},{9,10},{10,1... | collective-permute-start | bytes 921608 | tf_op jit(solution)/shard_map/ppermute | solution.py:189
  28.2 1.2 %slice.70 = s32[1]{0:T(128)} slice(s32[512]{0:T(512)} %param.28), slice={[0:1]} | slice | bytes 8 | tf_op jit(solution)/shard_map/slice | solution.py:133
  31.8 3.0 %fusion.5 = f32[8,40,64]{2,0,1:T(8,128)S(1)} fusion(f32[40,64,512]{2,1,0:T(8,128)} %bitcast.61, s32[8]{0:T(128)S(1)} %iota_add_fusion, pred[8]{0:T(512)(128)(4,1)S(1)} %get-tuple-element.41), kind=kOutput, calls=%fused_computation.14 | convolution fusion | flops 31459328 | bytes 1392680 | tf_op jit(solution)/shard_map/nyx,xc->ncy/dot_general | solution.py:209
  35.4 3.0 %fusion.18 = f32[40,8,64]{2,1,0:T(8,128)S(1)} fusion(f32[40,8,64]{2,1,0:T(8,128)S(1)} %bitcast.71, f32[8,40,64]{2,0,1:T(8,128)S(1)} %fusion.5, f32[40,64,512]{2,1,0:T(8,128)} %bitcast.62, pred[8]{0:T(512)(128)(4,1)S(1)} %copy-done.5), kind=kOutput, calls=%fused_computation.22 | convolution fusion | flops 31500288 | bytes 1556488 | tf_op jit(solution)/shard_map/nyx,xc->ncy/dot_general | solution.py:209
  39.0 16.8 %conditional.1 = (f32[50,3,1024]{2,0,1:T(8,128)S(1)}) conditional(s32[]{:T(128)} %clamp.3, f32[50,3,512]{2,1,0:T(4,128)S(1)} %fusion.27, f32[50,3,512]{2,1,0:T(4,128)S(1)} %fusion.27, f32[50,3,512]{2,1,0:T(4,128)S(1)} %fusion.27, f32[50,3,512]{2,1,0:T(4,128)S(1)} %fusion.27, f32[50,3,512]{2,1,0:T(4,128)S(1)} %fusion.27, ...), branch_computations={%region_1.2_spmd, %region_2.3_spmd, %region_3.4_spmd, %region_4.5_... | conditional | flops 153600 | bytes 4915288 | solution.py:152
  39.0 3.3 %collective-permute-start.3 = (f32[50,3,512]{2,1,0:T(4,128)S(1)}, f32[50,3,512]{2,1,0:T(4,128)S(1)}, u32[]{:S(2)}, u32[]{:S(2)}) collective-permute-start(f32[50,3,512]{2,1,0:T(4,128)S(1)} %param.1), channel_id=1, source_target_pairs={{31,15},{15,31},{127,47},{111,63},{95,79},{79,95},{63,111},{47,127}} | collective-permute-start | bytes 921608 | tf_op jit(solution)/shard_map/cond/branch_1_fun/ppermute | solution.py:147
  42.4 2.8 %collective-permute-start.2 = (f32[50,3,512]{2,1,0:T(4,128)S(1)}, f32[50,3,512]{2,1,0:T(4,128)S(1)}, u32[]{:S(2)}, u32[]{:S(2)}) collective-permute-start(f32[50,3,512]{2,1,0:T(4,128)S(1)} %param.1), channel_id=1, source_target_pairs={{15,15},{127,31},{111,47},{95,63},{79,79},{63,95},{47,111},{31,127}} | collective-permute-start | bytes 921608 | tf_op jit(solution)/shard_map/cond/branch_1_fun/ppermute | solution.py:146
  45.1 3.5 %collective-permute-done.3 = f32[50,3,512]{2,1,0:T(4,128)S(1)} collective-permute-done((f32[50,3,512]{2,1,0:T(4,128)S(1)}, f32[50,3,512]{2,1,0:T(4,128)S(1)}, u32[]{:S(2)}, u32[]{:S(2)}) %collective-permute-start.3) | collective-permute-done | bytes 307232 | tf_op jit(solution)/shard_map/cond/branch_1_fun/ppermute | solution.py:147
  48.6 6.4 %collective-permute-done.2 = f32[50,3,512]{2,1,0:T(4,128)S(1)} collective-permute-done((f32[50,3,512]{2,1,0:T(4,128)S(1)}, f32[50,3,512]{2,1,0:T(4,128)S(1)}, u32[]{:S(2)}, u32[]{:S(2)}) %collective-permute-start.2) | collective-permute-done | bytes 307232 | tf_op jit(solution)/shard_map/cond/branch_1_fun/ppermute | solution.py:146
  55.8 0.9 fusion.9
  56.8 1.1 %pad_maximum_fusion.8 = f32[50,8,512]{2,0,1:T(8,128)S(1)} fusion(f32[50,3,512]{2,0,1:T(8,128)} %collective-permute-done.17, f32[50,3,512]{2,0,1:T(8,128)S(1)} %fusion.9, f32[8]{0:T(128)S(1)} %pad.25.clone), kind=kLoop, calls=%fused_computation.32 | loop fusion | flops 409600 | bytes 1433632 | tf_op jit(solution)/shard_map/concatenate | solution.py:200
  59.2 1.5 %collective-permute-start.18 = (f32[50,8,72]{2,1,0:T(8,128)S(1)}, f32[50,8,72]{2,1,0:T(8,128)S(1)}, u32[]{:S(2)}, u32[]{:S(2)}) collective-permute-start(f32[50,8,72]{2,1,0:T(8,128)S(1)} %pad_maximum_fusion.13), channel_id=1, source_target_pairs={{0,112},{16,0},{32,16},{48,32},{64,48},{80,64},{96,80},{112,96},{1... | collective-permute-start | bytes 345608 | tf_op jit(solution)/shard_map/ppermute | solution.py:221
  60.6 0.7 copy.71.cor_ref
  61.3 1.4 %copy.67 = f32[50,8,512]{2,1,0:T(8,128)} copy(f32[50,8,512]{2,0,1:T(8,128)S(1)} %pad_maximum_fusion.8) | data formatting | bytes 1638400 | tf_op jit(solution)/shard_map/concatenate | solution.py:200
  62.7 1.1 collective-permute-done.19
  63.8 2.2 %collective-permute-done.18 = f32[50,8,72]{2,1,0:T(8,128)S(1)} collective-permute-done((f32[50,8,72]{2,1,0:T(8,128)S(1)}, f32[50,8,72]{2,1,0:T(8,128)S(1)}, u32[]{:S(2)}, u32[]{:S(2)}) %collective-permute-start.18) | collective-permute-done | bytes 115232 | tf_op jit(solution)/shard_map/ppermute | solution.py:221
  66.0 2.9 %fusion.41 = f32[50,72,128]{2,1,0:T(8,128)} fusion(f32[50,8,72]{2,1,0:T(8,128)S(1)} %collective-permute-done.18, f32[50,8,72]{2,1,0:T(8,128)S(1)} %collective-permute-done.19, pred[8]{0:T(512)(128)(4,1)S(1)} %copy-done.5, s32[8]{0:T(128)S(1)} %copy-done.7, pred[8]{0:T(512)(128)(4,1)S(1)} %copy-done.9), kind=kOutput, calls=%fused_computation.60 | convolution fusion | flops 44270720 | bytes 2073648 | tf_op jit(solution)/shard_map/ncy,cl->nyl/dot_general | solution.py:226
  68.9 20.9 %shard_map.109 = f32[4,10,64,512]{3,2,1,0:T(8,128)} custom-call(f32[4,10,64,512]{3,2,1,0:T(8,128)} %adj_ref.1, s32[10,64,512]{2,1,0:T(8,128)} %mask_ref.3, f32[10,64,512]{2,1,0:T(8,128)} %diff_ref.1, f32[5,10,8,512]{3,2,1,0:T(8,128)} %bitcast.65, f32[5,10,72,128]{3,2,1,0:T(8,128)} %bitcast.63, f32[64,1]{1,0:T(8,128)} %copy.71.cor_ref), custom_call_target="tpu_custom_call" | custom-call | tf_op jit(solution)/shard_map/pallas_call | solution.py:60
  90.7 0.9 reshape.306.vals_ref
  93.3 18.1 %shard_map.110 = f32[40,64,512]{2,1,0:T(8,128)} custom-call(s32[5,1024]{1,0:T(8,128)} %stack.20.where_ref, f32[1024]{0:T(1024)} %reshape_squeeze.4.weight_ref, f32[1024,128]{1,0:T(8,128)} %reshape.306.vals_ref, f32[40,64,512]{2,1,0:T(8,128)} %bitcast.64, s32[10,64,512]{2,1,0:T(8,128)} %mask_ref.3, f32[40,64,512]{2,1,0:T(8,128)} %bitcast.60), custom_call_target="tpu_custom_call" | custom-call | tf_op jit(solution)/shard_map/pallas_call | solution.py:109
  (68 shorter events, 8.7 us)
Async XLA Ops:
  0.0 4.3 %copy-start = (f32[512,128]{1,0:T(8,128)S(1)}, f32[512,128]{1,0:T(8,128)}, u32[]{:S(2)}) copy-start(f32[512,128]{1,0:T(8,128)} %param.24) | copy-start | bytes 786436
  7.1 12.7 %copy-start.2 = (f32[10,64,512]{2,1,0:T(8,128)S(1)}, f32[10,64,512]{2,1,0:T(8,128)}, u32[]{:S(2)}) copy-start(f32[10,64,512]{2,1,0:T(8,128)} %diff_ref.1) | copy-start | bytes 3932164
  7.1 12.8 %copy-start.1 = (s32[10,64,512]{2,1,0:T(8,128)S(1)}, s32[10,64,512]{2,1,0:T(8,128)}, u32[]{:S(2)}) copy-start(s32[10,64,512]{2,1,0:T(8,128)} %mask_ref.3) | copy-start | bytes 3932164
  9.6 80.2 %all-to-all-start = ((f32[128,1,1152]{2,1,0:T(1,128)}), f32[128,1,1152]{2,1,0:T(1,128)S(1)}, u32[]{:S(2)}, u32[]{:S(2)}) async-start(f32[128,1,1152]{2,1,0:T(1,128)} %all_to_all.8), calls=%async_computation | async-start | bytes 1179648 | tf_op jit(solution)/shard_map/all_to_all | solution.py:253
  23.0 32.8 %collective-permute-start.16 = (f32[50,3,512]{2,0,1:T(8,128)}, f32[50,3,512]{2,0,1:T(8,128)}, u32[]{:S(2)}, u32[]{:S(2)}) collective-permute-start(f32[50,3,512]{2,0,1:T(8,128)} %pad_maximum_fusion.11), channel_id=1, source_target_pairs={{1,0},{2,1},{3,2},{4,3},{5,4},{6,5},{7,6},{8,7},{9,8},{10,9},{11,1... | collective-permute-start | bytes 921608 | tf_op jit(solution)/shard_map/ppermute | solution.py:190
  26.9 29.9 %collective-permute-start.17 = (f32[50,3,512]{2,0,1:T(8,128)}, f32[50,3,512]{2,0,1:T(8,128)}, u32[]{:S(2)}, u32[]{:S(2)}) collective-permute-start(f32[50,3,512]{2,0,1:T(8,128)} %pad_maximum_fusion.12), channel_id=1, source_target_pairs={{0,1},{1,2},{2,3},{3,4},{4,5},{5,6},{6,7},{7,8},{8,9},{9,10},{10,1... | collective-permute-start | bytes 921608 | tf_op jit(solution)/shard_map/ppermute | solution.py:189
  30.0 1.0 copy-start.3
  30.1 4.7 %copy-start.6 = (s32[8]{0:T(128)}, s32[8]{0:T(128)S(1)}, u32[]{:S(2)}) copy-start(s32[8]{0:T(128)S(1)} %iota_add_fusion) | copy-start | bytes 100
  30.1 1.2 %copy-start.4 = (pred[8]{0:T(512)(128)(4,1)}, pred[8]{0:T(512)(128)(4,1)S(1)}, u32[]{:S(2)}) copy-start(pred[8]{0:T(512)(128)(4,1)S(1)} %get-tuple-element.42) | copy-start | bytes 28
  30.1 4.7 %copy-start.8 = (pred[8]{0:T(512)(128)(4,1)}, pred[8]{0:T(512)(128)(4,1)S(1)}, u32[]{:S(2)}) copy-start(pred[8]{0:T(512)(128)(4,1)S(1)} %get-tuple-element.41) | copy-start | bytes 28
  31.8 3.6 %copy-start.5 = (pred[8]{0:T(512)(128)(4,1)S(1)}, pred[8]{0:T(512)(128)(4,1)}, u32[]{:S(2)}) copy-start(pred[8]{0:T(512)(128)(4,1)} %copy-done.4) | copy-start | bytes 28
  35.3 3.0 %copy-start.7 = (s32[8]{0:T(128)S(1)}, s32[8]{0:T(128)}, u32[]{:S(2)}) copy-start(s32[8]{0:T(128)} %copy-done.6) | copy-start | bytes 100
  35.3 3.0 %copy-start.9 = (pred[8]{0:T(512)(128)(4,1)S(1)}, pred[8]{0:T(512)(128)(4,1)}, u32[]{:S(2)}) copy-start(pred[8]{0:T(512)(128)(4,1)} %copy-done.8) | copy-start | bytes 28
  39.0 9.6 %collective-permute-start.3 = (f32[50,3,512]{2,1,0:T(4,128)S(1)}, f32[50,3,512]{2,1,0:T(4,128)S(1)}, u32[]{:S(2)}, u32[]{:S(2)}) collective-permute-start(f32[50,3,512]{2,1,0:T(4,128)S(1)} %param.1), channel_id=1, source_target_pairs={{31,15},{15,31},{127,47},{111,63},{95,79},{79,95},{63,111},{47,127}} | collective-permute-start | bytes 921608 | tf_op jit(solution)/shard_map/cond/branch_1_fun/ppermute | solution.py:147
  42.4 12.6 %collective-permute-start.2 = (f32[50,3,512]{2,1,0:T(4,128)S(1)}, f32[50,3,512]{2,1,0:T(4,128)S(1)}, u32[]{:S(2)}, u32[]{:S(2)}) collective-permute-start(f32[50,3,512]{2,1,0:T(4,128)S(1)} %param.1), channel_id=1, source_target_pairs={{15,15},{127,31},{111,47},{95,63},{79,79},{63,95},{47,111},{31,127}} | collective-permute-start | bytes 921608 | tf_op jit(solution)/shard_map/cond/branch_1_fun/ppermute | solution.py:146
  56.7 3.9 %copy-start.10 = (f32[64]{0:T(128)S(1)}, f32[64]{0:T(128)}, u32[]{:S(2)}) copy-start(f32[64]{0:T(128)} %param.23) | copy-start | bytes 772
  59.1 4.7 %collective-permute-start.19 = (f32[50,8,72]{2,1,0:T(8,128)S(1)}, f32[50,8,72]{2,1,0:T(8,128)S(1)}, u32[]{:S(2)}, u32[]{:S(2)}) collective-permute-start(f32[50,8,72]{2,1,0:T(8,128)S(1)} %pad_maximum_fusion.13), channel_id=1, source_target_pairs={{0,16},{16,32},{32,48},{48,64},{64,80},{80,96},{96,112},{112,0},{1... | collective-permute-start | bytes 345608 | tf_op jit(solution)/shard_map/ppermute | solution.py:222
  59.2 6.8 %collective-permute-start.18 = (f32[50,8,72]{2,1,0:T(8,128)S(1)}, f32[50,8,72]{2,1,0:T(8,128)S(1)}, u32[]{:S(2)}, u32[]{:S(2)}) collective-permute-start(f32[50,8,72]{2,1,0:T(8,128)S(1)} %pad_maximum_fusion.13), channel_id=1, source_target_pairs={{0,112},{16,0},{32,16},{48,32},{64,48},{80,64},{96,80},{112,96},{1... | collective-permute-start | bytes 345608 | tf_op jit(solution)/shard_map/ppermute | solution.py:221

commit v5 on v4

--- a/solution.py
+++ b/solution.py
@@ -1,5 +1,3 @@
-import functools
-
 import jax
 import jax.numpy as jnp
 from jax import lax
@@ -24,11 +22,21 @@
     )
 
 
-def mix_kernel(adj_ref, mask_ref, diff_ref, rows_ref, cols_ref, cor_ref, out_ref, xs, ds):
+def step_kernel(
+    where_ref, weight_ref, adj_ref, mask_ref, diff_ref, rows_ref, cols_ref, cor_ref, vals_ref,
+    traj_hbm, out_ref, xs, ds, traj_ref, sem
+):
     fields = adj_ref.shape[0]
     h, w = adj_ref.shape[2], adj_ref.shape[3]
     hp, wp = xs.shape[1], xs.shape[2]
-    wet = mask_ref[0].astype(jnp.float32)
+    k = pl.program_id(0)
+    last = pl.num_programs(0) - 1
+
+    @pl.when(k == 0)
+    def _():
+        pltpu.make_async_copy(traj_hbm, traj_ref, sem).start()
+
+    wet = mask_ref[k].astype(jnp.float32)
     for f in range(fields):
         xs[f, 0:h, 0:w] = adj_ref[f, 0] * wet
         xs[f, h:hp, 0:w] = rows_ref[f, 0]
@@ -48,39 +56,33 @@
             x = x + d * (east + west + north + south - 4.0 * x)
         done.append(x[0:h, 0:w])
     rot = cor_ref[...]
-    out_ref[0, 0] = wet * done[0]
-    out_ref[1, 0] = wet * done[1]
-    out_ref[2, 0] = wet * (done[2] - rot * done[3])
-    out_ref[3, 0] = wet * (done[3] + rot * done[2])
-
-
-def mix_call(adjoint, land_mask, diffusivity, rows5, cols5, coriolis):
-    fields, levels, h, w = adjoint.shape
-    hp, wp = h + PAD_ROWS, w + PAD_LANES
-    return pl.pallas_call(
-        mix_kernel,
-        grid=(levels,),
-        in_specs=[
-            pl.BlockSpec((fields, 1, h, w), lambda k: (0, k, 0, 0)),
-            pl.BlockSpec((1, h, w), lambda k: (k, 0, 0)),
-            pl.BlockSpec((1, h, w), lambda k: (k, 0, 0)),
-            pl.BlockSpec((fields + 1, 1, PAD_ROWS, w), lambda k: (0, k, 0, 0)),
-            pl.BlockSpec((fields + 1, 1, hp, PAD_LANES), lambda k: (0, k, 0, 0)),
-            pl.BlockSpec((h, 1), lambda k: (0, 0)),
-        ],
-        out_specs=pl.BlockSpec((fields, 1, h, w), lambda k: (0, k, 0, 0)),
-        out_shape=jax.ShapeDtypeStruct(adjoint.shape, jnp.float32),
-        scratch_shapes=[
-            pltpu.VMEM((fields, hp, wp), jnp.float32),
-            pltpu.VMEM((hp, wp), jnp.float32),
-        ],
-    )(adjoint, land_mask, diffusivity, rows5, cols5, coriolis.reshape(h, 1))
-
-
-def obs_kernel(where_ref, weight_ref, vals_ref, traj_ref, mask_ref, base_ref, out_ref):
-    out_ref[...] = base_ref[...]
+    out_ref[0, k] = wet * done[0]
+    out_ref[1, k] = wet * done[1]
+    out_ref[2, k] = wet * (done[2] - rot * done[3])
+    out_ref[3, k] = wet * (done[3] + rot * done[2])
+
+    @pl.when(k == last)
+    def _():
+        pltpu.make_async_copy(traj_hbm, traj_ref, sem).wait()
+        add_forcing(where_ref, weight_ref, vals_ref, traj_ref, mask_ref, out_ref)
+
+
+def add_forcing(where_ref, weight_ref, vals_ref, traj_ref, mask_ref, out_ref):
     seg_width = vals_ref.shape[1]
     sub = lax.broadcasted_iota(jnp.int32, (8, seg_width), 0)
+
+    def add_row(i, value):
+        layer = where_ref[0, i]
+        rows = pl.ds(pl.multiple_of(where_ref[1, i], 8), 8)
+        cols = pl.ds(pl.multiple_of(where_ref[2, i], seg_width), seg_width)
+        level = where_ref[3, i]
+        field = where_ref[5, i]
+        sampled = traj_ref[layer, rows, cols]
+        misfit = weight_ref[i] * (sampled - value)
+        wet = mask_ref[level, rows, cols].astype(jnp.float32)
+        hit = sub == where_ref[4, i]
+        cur = out_ref[field, level, rows, cols]
+        out_ref[field, level, rows, cols] = cur + jnp.where(hit, wet * misfit, 0.0)
 
     def body(o, carry):
         first = pl.multiple_of(o * 8, 8)
@@ -89,39 +91,39 @@
             add_row(first + j, vals8[j : j + 1, :])
         return carry
 
-    def add_row(i, value):
-        layer = where_ref[0, i]
-        rows = pl.ds(pl.multiple_of(where_ref[1, i], 8), 8)
-        cols = pl.ds(pl.multiple_of(where_ref[2, i], seg_width), seg_width)
-        level = where_ref[3, i]
-        sampled = traj_ref[layer, rows, cols]
-        misfit = weight_ref[i] * (sampled - value)
-        wet = mask_ref[level, rows, cols].astype(jnp.float32)
-        hit = sub == where_ref[4, i]
-        cur = out_ref[layer, rows, cols]
-        out_ref[layer, rows, cols] = cur + jnp.where(hit, wet * misfit, 0.0)
-
     lax.fori_loop(0, vals_ref.shape[0] // 8, body, 0)
 
 
-def obs_call(where, weight, values, traj3, land_mask, base3):
-    whole = lambda shape: pl.BlockSpec(shape, lambda i, *_: (0,) * len(shape))
+def step_call(where, weight, adjoint, land_mask, diffusivity, rows5, cols5, coriolis, values, traj3):
+    fields, levels, h, w = adjoint.shape
+    hp, wp = h + PAD_ROWS, w + PAD_LANES
+    whole = lambda shape: pl.BlockSpec(shape, lambda k, *_: (0,) * len(shape))
     return pl.pallas_call(
-        obs_kernel,
+        step_kernel,
         grid_spec=pltpu.PrefetchScalarGridSpec(
             num_scalar_prefetch=2,
-            grid=(1,),
+            grid=(levels,),
             in_specs=[
+                pl.BlockSpec((fields, 1, h, w), lambda k, *_: (0, k, 0, 0)),
+                whole(land_mask.shape),
+                pl.BlockSpec((1, h, w), lambda k, *_: (k, 0, 0)),
+                pl.BlockSpec((fields + 1, 1, PAD_ROWS, w), lambda k, *_: (0, k, 0, 0)),
+                pl.BlockSpec((fields + 1, 1, hp, PAD_LANES), lambda k, *_: (0, k, 0, 0)),
+                whole((h, 1)),
                 whole(values.shape),
-                whole(traj3.shape),
-                whole(land_mask.shape),
-                whole(base3.shape),
+                pl.BlockSpec(memory_space=pl.ANY),
             ],
-            out_specs=whole(base3.shape),
+            out_specs=whole(adjoint.shape),
+            scratch_shapes=[
+                pltpu.VMEM((fields, hp, wp), jnp.float32),
+                pltpu.VMEM((hp, wp), jnp.float32),
+                pltpu.VMEM(traj3.shape, jnp.float32),
+                pltpu.SemaphoreType.DMA(()),
+            ],
         ),
-        out_shape=jax.ShapeDtypeStruct(base3.shape, jnp.float32),
+        out_shape=jax.ShapeDtypeStruct(adjoint.shape, jnp.float32),
         compiler_params=pltpu.CompilerParams(vmem_limit_bytes=60 * 1024 * 1024),
-    )(where, weight, values, traj3, land_mask, base3)
+    )(where, weight, adjoint, land_mask, diffusivity, rows5, cols5, coriolis.reshape(h, 1), values, traj3)
 
 
 def fold_rows(top_msg, fold_partner, width):
@@ -226,7 +228,6 @@
     cols5 = jnp.einsum("ncy,cl->nyl", got_cols, place, precision=lax.Precision.HIGHEST)
     cols5 = cols5.reshape(fields + 1, levels, h + PAD_ROWS, PAD_LANES)
 
-    mixed_wet = mix_call(adjoint, land_mask, diffusivity, rows5, cols5, coriolis)
 
     devices = lon_count * lat_count
     seg_width = obs_values.shape[1]
@@ -262,17 +263,28 @@
     row_local = rest % h
     layer = rest // h
     where = jnp.stack(
-        [layer, row_local // 8 * 8, seg_local * seg_width, layer % levels, row_local % 8], axis=0
-    )
-    out3 = obs_call(
+        [
+            layer,
+            row_local // 8 * 8,
+            seg_local * seg_width,
+            layer % levels,
+            row_local % 8,
+            layer // levels,
+        ],
+        axis=0,
+    )
+    return step_call(
         where,
         got_weight,
+        adjoint,
+        land_mask,
+        diffusivity,
+        rows5,
+        cols5,
+        coriolis,
         got_values,
         trajectory.reshape(n_work, h, w),
-        land_mask,
-        mixed_wet.reshape(n_work, h, w),
-    )
-    return out3.reshape(adjoint.shape)
+    )
 
 
 def solution(mesh):

time: 113 us -> 108 us (0.956); the launches traced: 111 us -> 108 us
  starting transfers between devices: 22.1 us -> 26.3 us
  Pallas kernels: 39 us -> 35.1 us
  waiting for transfers between devices: 13.1 us -> 10.6 us
    ppermute x1, starting transfers between devices: 0.07 us -> 6.67 us  [per_device(): from_west = lax.ppermute(col_msg, 'lon', ring_east)]
    ppermute x1, waiting for transfers between devices: 6.38 us -> 1.23 us  [run(): got_a = lax.ppermute(msg, ('lon', 'lat'), pairs_a)]
    pallas_call x2 -> x1, Pallas kernels: 39 us -> 35.1 us  [step_call(): pl.pallas_call(step_kernel, grid_spec=pltpu.PrefetchScalarGridSpec(num_sc...]
    ppermute x1, waiting for transfers between devices: 2.19 us -> 4.01 us  [per_device(): from_east = lax.ppermute(col_msg, 'lon', ring_west)]
    ppermute x1, starting transfers between devices: 1.45 us -> 0.01 us  [per_device(): from_east = lax.ppermute(col_msg, 'lon', ring_west)]
    ppermute x1, waiting for transfers between devices: 3.47 us -> 4.68 us  [run(): got_b = lax.ppermute(msg, ('lon', 'lat'), pairs_b)]
    ppermute x1, starting transfers between devices: 3.34 us -> 2.14 us  [run(): got_b = lax.ppermute(msg, ('lon', 'lat'), pairs_b)]
    concatenate x1, other arithmetic: 1.23 us -> 0.04 us  [per_device(): jnp.concatenate([send_values.reshape(devices, CAP * seg_width), send_meta...]
  transfers between devices with their start and end apart: 7 -> 7, of which waited for: 4 -> 4; matrix products, arithmetic and copies ran while one was open for 20% -> 21% of each run, Pallas kernels for 19% -> 0%
where the time goes in v5:
time: 108 us
  Pallas kernels  35.1 us (32%)
  starting transfers between devices  26.3 us (24%)
  matrix products  17.2 us (16%)
  waiting for transfers between devices  10.6 us (10%)
  local copies, waits for them, and re-layouts  9.52 us (9%)
  other arithmetic  7.44 us (7%)
  between operations  1.22 us (1%)
    pallas_call x1, Pallas kernels, step_call(): pl.pallas_call(step_kernel, grid_spec=pltpu.PrefetchScalarGridSpec(num_sc...  35.1 us
    all_to_all x1, starting transfers between devices, per_device(): lax.all_to_all(send, ('lon', 'lat'), split_axis=0, concat_axis=0, tiled=T...  10.2 us
    dot_general x8, matrix products, edges(): jnp.einsum('nyx,xc->ncy', part, sel.astype(jnp.float32), precision=lax.Pr...  8.84 us
    ppermute x1, starting transfers between devices, per_device(): from_west = lax.ppermute(col_msg, 'lon', ring_east)  6.67 us
    ppermute x1, waiting for transfers between devices, run(): got_b = lax.ppermute(msg, ('lon', 'lat'), pairs_b)  4.68 us
    dot_general x3, matrix products, exact_dot(): lax.dot_general(left, right, (((left_dim,), (0,)), ((), ())), precision=l...  4.34 us
    ppermute x1, waiting for transfers between devices, per_device(): from_east = lax.ppermute(col_msg, 'lon', ring_west)  4.01 us
    ppermute x1, starting transfers between devices, run(): got_a = lax.ppermute(msg, ('lon', 'lat'), pairs_a)  3.07 us
  transfers between devices with their start and end apart: 7, of which 4 were waited for; matrix products, arithmetic and copies ran while one was open for 21% of the time, Pallas kernels for 0%

profile of v5, /device:TPU:95, one launch (start us, length us, event | category | flops | bytes accessed | tf_op | source)
XLA Modules:
  0.0 107.6 jit_solution(6885408445171444369)
XLA Ops:
  0.0 0.7 convert_element_type.82
  0.7 1.1 fusion.21
  1.8 0.7 multiply_add_fusion
  2.5 1.5 %fusion = f32[1024,2]{0,1:T(2,128)S(1)} fusion(s32[512]{0:T(512)S(1)} %bitcast.73, f32[512,1]{0,1:T(1,128)S(1)} %bitcast.75, f32[512,1]{0,1:T(1,128)} %bitcast.77), kind=kOutput, calls=%fused_computation.10 | convolution fusion | flops 13108224 | bytes 14336 | tf_op jit(solution)/shard_map/dot_general | solution.py:16
  4.3 1.9 %fusion.1 = f32[1024,128]{1,0:T(8,128)S(1)} fusion(f32[512,128]{1,0:T(8,128)S(1)} %copy-done, s32[512]{0:T(512)S(1)} %bitcast.74), kind=kOutput, calls=%fused_computation.11 | convolution fusion | flops 805830656 | bytes 788480 | tf_op jit(solution)/shard_map/dot_general | solution.py:16
  6.4 1.2 %all_to_all.8 = f32[128,1,1152]{2,1,0:T(1,128)} reshape(f32[128,1152]{1,0:T(8,128)S(1)} %select_maximum_fusion) | data formatting | bytes 1179648 | tf_op jit(solution)/shard_map/all_to_all | solution.py:254
  7.6 10.2 %all-to-all-start = ((f32[128,1,1152]{2,1,0:T(1,128)}), f32[128,1,1152]{2,1,0:T(1,128)S(1)}, u32[]{:S(2)}, u32[]{:S(2)}) async-start(f32[128,1,1152]{2,1,0:T(1,128)} %all_to_all.8), calls=%async_computation | async-start | bytes 1179648 | tf_op jit(solution)/shard_map/all_to_all | solution.py:254
  17.9 2.3 %broadcast_multiply_fusion = (f32[4,10,3,512]{3,2,1,0:T(4,128)}, f32[4,10,3,512]{3,2,1,0:T(4,128)S(1)}, f32[4,10,3,512]{3,2,1,0:T(4,128)S(1)}) fusion(f32[4]{0:T(128)} %constant.148.clone, f32[10,3,512]{2,1,0:T(4,128)S(1)} %get-tuple-element.34, f32[4,10,64,512]{3,2,1,0:T(8,128)} %adj_ref.1, f32[10,3,512]{2,1,0:T(4,128)S(1)} %get-tuple-element.33), kind=kLoop, calls=%fused_computation.62 | loop fusion | flops 184320 | bytes 1351696 | tf_op jit(solution)/shard_map/mul | solution.py:194
  20.3 0.8 pad_maximum_fusion.11
  21.1 3.0 %collective-permute-start.16 = (f32[50,3,512]{2,0,1:T(8,128)}, f32[50,3,512]{2,0,1:T(8,128)}, u32[]{:S(2)}, u32[]{:S(2)}) collective-permute-start(f32[50,3,512]{2,0,1:T(8,128)} %pad_maximum_fusion.11), channel_id=1, source_target_pairs={{1,0},{2,1},{3,2},{4,3},{5,4},{6,5},{7,6},{8,7},{9,8},{10,9},{11,1... | collective-permute-start | bytes 921608 | tf_op jit(solution)/shard_map/ppermute | solution.py:192
  24.2 0.8 pad_maximum_fusion.12
  24.9 1.3 %collective-permute-start.17 = (f32[50,3,512]{2,0,1:T(8,128)}, f32[50,3,512]{2,0,1:T(8,128)}, u32[]{:S(2)}, u32[]{:S(2)}) collective-permute-start(f32[50,3,512]{2,0,1:T(8,128)} %pad_maximum_fusion.12), channel_id=1, source_target_pairs={{0,1},{1,2},{2,3},{3,4},{4,5},{5,6},{6,7},{7,8},{8,9},{9,10},{10,1... | collective-permute-start | bytes 921608 | tf_op jit(solution)/shard_map/ppermute | solution.py:191
  26.2 1.2 %slice.69 = s32[1]{0:T(128)} slice(s32[512]{0:T(512)} %param.28), slice={[0:1]} | slice | bytes 8 | tf_op jit(solution)/shard_map/slice | solution.py:135
  29.9 3.0 %fusion.5 = f32[8,40,64]{2,0,1:T(8,128)S(1)} fusion(f32[40,64,512]{2,1,0:T(8,128)} %bitcast.58, s32[8]{0:T(128)S(1)} %iota_add_fusion, pred[8]{0:T(512)(128)(4,1)S(1)} %get-tuple-element.41), kind=kOutput, calls=%fused_computation.14 | convolution fusion | flops 31459328 | bytes 1392680 | tf_op jit(solution)/shard_map/nyx,xc->ncy/dot_general | solution.py:211
  33.5 3.0 %fusion.18 = f32[40,8,64]{2,1,0:T(8,128)S(1)} fusion(f32[40,8,64]{2,1,0:T(8,128)S(1)} %bitcast.68, f32[8,40,64]{2,0,1:T(8,128)S(1)} %fusion.5, f32[40,64,512]{2,1,0:T(8,128)} %bitcast.59, pred[8]{0:T(512)(128)(4,1)S(1)} %copy-done.5), kind=kOutput, calls=%fused_computation.22 | convolution fusion | flops 31500288 | bytes 1556488 | tf_op jit(solution)/shard_map/nyx,xc->ncy/dot_general | solution.py:211
  37.1 11.9 %conditional.1 = (f32[50,3,1024]{2,0,1:T(8,128)S(1)}) conditional(s32[]{:T(128)} %clamp.3, f32[50,3,512]{2,1,0:T(4,128)S(1)} %fusion.27, f32[50,3,512]{2,1,0:T(4,128)S(1)} %fusion.27, f32[50,3,512]{2,1,0:T(4,128)S(1)} %fusion.27, f32[50,3,512]{2,1,0:T(4,128)S(1)} %fusion.27, f32[50,3,512]{2,1,0:T(4,128)S(1)} %fusion.27, ...), branch_computations={%region_1.2_spmd, %region_2.3_spmd, %region_3.4_spmd, %region_4.5_... | conditional | flops 153600 | bytes 4915288 | solution.py:154
  37.1 2.1 %collective-permute-start.7 = (f32[50,3,512]{2,1,0:T(4,128)S(1)}, f32[50,3,512]{2,1,0:T(4,128)S(1)}, u32[]{:S(2)}, u32[]{:S(2)}) collective-permute-start(f32[50,3,512]{2,1,0:T(4,128)S(1)} %param.3), channel_id=1, source_target_pairs={{63,15},{47,31},{31,47},{15,63},{127,79},{111,95},{95,111},{79,127}} | collective-permute-start | bytes 921608 | tf_op jit(solution)/shard_map/cond/branch_3_fun/ppermute | solution.py:149
  39.3 3.1 %collective-permute-start.6 = (f32[50,3,512]{2,1,0:T(4,128)S(1)}, f32[50,3,512]{2,1,0:T(4,128)S(1)}, u32[]{:S(2)}, u32[]{:S(2)}) collective-permute-start(f32[50,3,512]{2,1,0:T(4,128)S(1)} %param.3), channel_id=1, source_target_pairs={{47,15},{31,31},{15,47},{127,63},{111,79},{95,95},{79,111},{63,127}} | collective-permute-start | bytes 921608 | tf_op jit(solution)/shard_map/cond/branch_3_fun/ppermute | solution.py:148
  42.3 4.7 %collective-permute-done.7 = f32[50,3,512]{2,1,0:T(4,128)S(1)} collective-permute-done((f32[50,3,512]{2,1,0:T(4,128)S(1)}, f32[50,3,512]{2,1,0:T(4,128)S(1)}, u32[]{:S(2)}, u32[]{:S(2)}) %collective-permute-start.7) | collective-permute-done | bytes 307232 | tf_op jit(solution)/shard_map/cond/branch_3_fun/ppermute | solution.py:149
  47.0 1.2 %collective-permute-done.6 = f32[50,3,512]{2,1,0:T(4,128)S(1)} collective-permute-done((f32[50,3,512]{2,1,0:T(4,128)S(1)}, f32[50,3,512]{2,1,0:T(4,128)S(1)}, u32[]{:S(2)}, u32[]{:S(2)}) %collective-permute-start.6) | collective-permute-done | bytes 307232 | tf_op jit(solution)/shard_map/cond/branch_3_fun/ppermute | solution.py:148
  49.1 0.9 fusion.9
  50.0 1.1 %pad_maximum_fusion.8 = f32[50,8,512]{2,0,1:T(8,128)S(1)} fusion(f32[50,3,512]{2,0,1:T(8,128)} %collective-permute-done.17, f32[50,3,512]{2,0,1:T(8,128)S(1)} %fusion.9, f32[8]{0:T(128)S(1)} %pad.25.clone), kind=kLoop, calls=%fused_computation.32 | loop fusion | flops 409600 | bytes 1433632 | tf_op jit(solution)/shard_map/concatenate | solution.py:202
  52.3 6.7 %collective-permute-start.19 = (f32[50,8,72]{2,1,0:T(8,128)S(1)}, f32[50,8,72]{2,1,0:T(8,128)S(1)}, u32[]{:S(2)}, u32[]{:S(2)}) collective-permute-start(f32[50,8,72]{2,1,0:T(8,128)S(1)} %pad_maximum_fusion.13), channel_id=1, source_target_pairs={{0,16},{16,32},{32,48},{48,64},{64,80},{80,96},{96,112},{112,0},{1... | collective-permute-start | bytes 345608 | tf_op jit(solution)/shard_map/ppermute | solution.py:224
  59.0 0.7 copy.71.cor_ref
  59.7 1.4 %copy.66 = f32[50,8,512]{2,1,0:T(8,128)} copy(f32[50,8,512]{2,0,1:T(8,128)S(1)} %pad_maximum_fusion.8) | data formatting | bytes 1638400 | tf_op jit(solution)/shard_map/concatenate | solution.py:202
  61.7 4.0 %collective-permute-done.18 = f32[50,8,72]{2,1,0:T(8,128)S(1)} collective-permute-done((f32[50,8,72]{2,1,0:T(8,128)S(1)}, f32[50,8,72]{2,1,0:T(8,128)S(1)}, u32[]{:S(2)}, u32[]{:S(2)}) %collective-permute-start.18) | collective-permute-done | bytes 115232 | tf_op jit(solution)/shard_map/ppermute | solution.py:223
  65.7 3.0 %fusion.41 = f32[50,72,128]{2,1,0:T(8,128)} fusion(f32[50,8,72]{2,1,0:T(8,128)S(1)} %collective-permute-done.18, f32[50,8,72]{2,1,0:T(8,128)S(1)} %collective-permute-done.19, pred[8]{0:T(512)(128)(4,1)S(1)} %copy-done.5, s32[8]{0:T(128)S(1)} %copy-done.7, pred[8]{0:T(512)(128)(4,1)S(1)} %copy-done.9), kind=kOutput, calls=%fused_computation.60 | convolution fusion | flops 44270720 | bytes 2073648 | tf_op jit(solution)/shard_map/ncy,cl->nyl/dot_general | solution.py:228
  68.7 0.7 copy.57
  69.6 0.9 reshape.329.vals_ref
  70.6 0.7 reshape_squeeze.4.weight_ref
  71.7 0.6 stack.21.where_ref
  72.3 35.1 %shard_map.109 = f32[4,10,64,512]{3,2,1,0:T(8,128)} custom-call(s32[6,1024]{1,0:T(8,128)} %stack.21.where_ref, f32[1024]{0:T(1024)} %reshape_squeeze.4.weight_ref, f32[4,10,64,512]{3,2,1,0:T(8,128)} %adj_ref.1, s32[10,64,512]{2,1,0:T(8,128)} %mask_ref.1, f32[10,64,512]{2,1,0:T(8,128)} %diff_ref.1, f32[5,10,8,512]{3,2,1,0:T(8,128)} %bitcast.62, ...), custom_call_target="tpu_custom_call" | custom-call | tf_op jit(solution)/shard_map/pallas_call | solution.py:101
  (69 shorter events, 6.7 us)
Async XLA Ops:
  0.0 4.3 %copy-start = (f32[512,128]{1,0:T(8,128)S(1)}, f32[512,128]{1,0:T(8,128)}, u32[]{:S(2)}) copy-start(f32[512,128]{1,0:T(8,128)} %param.24) | copy-start | bytes 786436
  6.3 11.4 %copy-start.1 = (s32[10,64,512]{2,1,0:T(8,128)S(1)}, s32[10,64,512]{2,1,0:T(8,128)}, u32[]{:S(2)}) copy-start(s32[10,64,512]{2,1,0:T(8,128)} %mask_ref.1) | copy-start | bytes 3932164
  6.4 11.5 %copy-start.2 = (f32[10,64,512]{2,1,0:T(8,128)S(1)}, f32[10,64,512]{2,1,0:T(8,128)}, u32[]{:S(2)}) copy-start(f32[10,64,512]{2,1,0:T(8,128)} %diff_ref.1) | copy-start | bytes 3932164
  7.6 61.1 %all-to-all-start = ((f32[128,1,1152]{2,1,0:T(1,128)}), f32[128,1,1152]{2,1,0:T(1,128)S(1)}, u32[]{:S(2)}, u32[]{:S(2)}) async-start(f32[128,1,1152]{2,1,0:T(1,128)} %all_to_all.8), calls=%async_computation | async-start | bytes 1179648 | tf_op jit(solution)/shard_map/all_to_all | solution.py:254
  21.1 28.0 %collective-permute-start.16 = (f32[50,3,512]{2,0,1:T(8,128)}, f32[50,3,512]{2,0,1:T(8,128)}, u32[]{:S(2)}, u32[]{:S(2)}) collective-permute-start(f32[50,3,512]{2,0,1:T(8,128)} %pad_maximum_fusion.11), channel_id=1, source_target_pairs={{1,0},{2,1},{3,2},{4,3},{5,4},{6,5},{7,6},{8,7},{9,8},{10,9},{11,1... | collective-permute-start | bytes 921608 | tf_op jit(solution)/shard_map/ppermute | solution.py:192
  24.9 25.1 %collective-permute-start.17 = (f32[50,3,512]{2,0,1:T(8,128)}, f32[50,3,512]{2,0,1:T(8,128)}, u32[]{:S(2)}, u32[]{:S(2)}) collective-permute-start(f32[50,3,512]{2,0,1:T(8,128)} %pad_maximum_fusion.12), channel_id=1, source_target_pairs={{0,1},{1,2},{2,3},{3,4},{4,5},{5,6},{6,7},{7,8},{8,9},{9,10},{10,1... | collective-permute-start | bytes 921608 | tf_op jit(solution)/shard_map/ppermute | solution.py:191
  28.1 4.8 %copy-start.6 = (s32[8]{0:T(128)}, s32[8]{0:T(128)S(1)}, u32[]{:S(2)}) copy-start(s32[8]{0:T(128)S(1)} %iota_add_fusion) | copy-start | bytes 100
  28.1 1.3 %copy-start.4 = (pred[8]{0:T(512)(128)(4,1)}, pred[8]{0:T(512)(128)(4,1)S(1)}, u32[]{:S(2)}) copy-start(pred[8]{0:T(512)(128)(4,1)S(1)} %get-tuple-element.42) | copy-start | bytes 28
  28.1 4.8 %copy-start.8 = (pred[8]{0:T(512)(128)(4,1)}, pred[8]{0:T(512)(128)(4,1)S(1)}, u32[]{:S(2)}) copy-start(pred[8]{0:T(512)(128)(4,1)S(1)} %get-tuple-element.41) | copy-start | bytes 28
  28.2 1.0 copy-start.3
  29.9 3.6 %copy-start.5 = (pred[8]{0:T(512)(128)(4,1)S(1)}, pred[8]{0:T(512)(128)(4,1)}, u32[]{:S(2)}) copy-start(pred[8]{0:T(512)(128)(4,1)} %copy-done.4) | copy-start | bytes 28
  33.4 3.0 %copy-start.7 = (s32[8]{0:T(128)S(1)}, s32[8]{0:T(128)}, u32[]{:S(2)}) copy-start(s32[8]{0:T(128)} %copy-done.6) | copy-start | bytes 100
  33.4 3.0 %copy-start.9 = (pred[8]{0:T(512)(128)(4,1)S(1)}, pred[8]{0:T(512)(128)(4,1)}, u32[]{:S(2)}) copy-start(pred[8]{0:T(512)(128)(4,1)} %copy-done.8) | copy-start | bytes 28
  37.1 9.9 %collective-permute-start.7 = (f32[50,3,512]{2,1,0:T(4,128)S(1)}, f32[50,3,512]{2,1,0:T(4,128)S(1)}, u32[]{:S(2)}, u32[]{:S(2)}) collective-permute-start(f32[50,3,512]{2,1,0:T(4,128)S(1)} %param.3), channel_id=1, source_target_pairs={{63,15},{47,31},{31,47},{15,63},{127,79},{111,95},{95,111},{79,127}} | collective-permute-start | bytes 921608 | tf_op jit(solution)/shard_map/cond/branch_3_fun/ppermute | solution.py:149
  39.3 9.0 %collective-permute-start.6 = (f32[50,3,512]{2,1,0:T(4,128)S(1)}, f32[50,3,512]{2,1,0:T(4,128)S(1)}, u32[]{:S(2)}, u32[]{:S(2)}) collective-permute-start(f32[50,3,512]{2,1,0:T(4,128)S(1)} %param.3), channel_id=1, source_target_pairs={{47,15},{31,31},{15,47},{127,63},{111,79},{95,95},{79,111},{63,127}} | collective-permute-start | bytes 921608 | tf_op jit(solution)/shard_map/cond/branch_3_fun/ppermute | solution.py:148
  50.0 9.0 %copy-start.10 = (f32[64]{0:T(128)S(1)}, f32[64]{0:T(128)}, u32[]{:S(2)}) copy-start(f32[64]{0:T(128)} %param.23) | copy-start | bytes 772
  52.3 9.4 %collective-permute-start.19 = (f32[50,8,72]{2,1,0:T(8,128)S(1)}, f32[50,8,72]{2,1,0:T(8,128)S(1)}, u32[]{:S(2)}, u32[]{:S(2)}) collective-permute-start(f32[50,8,72]{2,1,0:T(8,128)S(1)} %pad_maximum_fusion.13), channel_id=1, source_target_pairs={{0,16},{16,32},{32,48},{48,64},{64,80},{80,96},{96,112},{112,0},{1... | collective-permute-start | bytes 345608 | tf_op jit(solution)/shard_map/ppermute | solution.py:224
  59.0 6.7 %collective-permute-start.18 = (f32[50,8,72]{2,1,0:T(8,128)S(1)}, f32[50,8,72]{2,1,0:T(8,128)S(1)}, u32[]{:S(2)}, u32[]{:S(2)}) collective-permute-start(f32[50,8,72]{2,1,0:T(8,128)S(1)} %pad_maximum_fusion.13), channel_id=1, source_target_pairs={{0,112},{16,0},{32,16},{48,32},{64,48},{80,64},{96,80},{112,96},{1... | collective-permute-start | bytes 345608 | tf_op jit(solution)/shard_map/ppermute | solution.py:223

commit v6 on v5

--- a/solution.py
+++ b/solution.py
@@ -230,6 +230,9 @@
 
 
     devices = lon_count * lat_count
+    _, _, obs_values, obs_weight, obs_owner, obs_offset = lax.optimization_barrier(
+        (top_msg, bot_msg, obs_values, obs_weight, obs_owner, obs_offset)
+    )
     seg_width = obs_values.shape[1]
     rows_sent = obs_values.shape[0]
     owner_index = obs_owner[:, 0]

time: 108 us -> 114 us (1.056)
  local copies, waits for them, and re-layouts: 9.52 us -> 14 us
  waiting for transfers between devices: 10.6 us -> 14.9 us
  other arithmetic: 7.44 us -> 5.62 us
    ppermute x1, waiting for transfers between devices: 1.23 us -> 10.3 us  [run(): got_a = lax.ppermute(msg, ('lon', 'lat'), pairs_a)]
    ppermute x1, waiting for transfers between devices: 4.68 us -> 0.01 us  [run(): got_b = lax.ppermute(msg, ('lon', 'lat'), pairs_b)]
    ppermute x1, starting transfers between devices: 6.67 us -> 3.07 us  [per_device(): from_west = lax.ppermute(col_msg, 'lon', ring_east)]
    all_to_all x1, starting transfers between devices: 10.2 us -> 13 us  [per_device(): lax.all_to_all(send, ('lon', 'lat'), split_axis=0, concat_axis=0, tiled=T...]
    unnamed x25 -> x33, local copies, waits for them, and re-layouts: 0.52 us -> 2.87 us
    ppermute x1, starting transfers between devices: 3.07 us -> 4.81 us  [run(): got_a = lax.ppermute(msg, ('lon', 'lat'), pairs_a)]
    concatenate x2 -> x0, other arithmetic: 1.53 us -> none  [the longest x1 0.77 us: per_device(): jnp.concatenate([bot_work.reshape(n_work, HALO, w), bot_diff], axis=0)]
    ppermute x1, starting transfers between devices: 2.14 us -> 0.68 us  [run(): got_b = lax.ppermute(msg, ('lon', 'lat'), pairs_b)]
  transfers between devices with their start and end apart: 7 -> 7, of which waited for: 4 -> 3; matrix products, arithmetic and copies ran while one was open for 21% -> 21% of each run, Pallas kernels for 0% -> 0%
where the time goes in v6:
time: 114 us
  Pallas kernels  35.1 us (31%)
  starting transfers between devices  26.1 us (23%)
  matrix products  16.5 us (14%)
  waiting for transfers between devices  14.9 us (13%)
  local copies, waits for them, and re-layouts  14 us (12%)
  other arithmetic  5.62 us (5%)
  between operations  1.19 us (1%)
    pallas_call x1, Pallas kernels, step_call(): pl.pallas_call(step_kernel, grid_spec=pltpu.PrefetchScalarGridSpec(num_sc...  35.1 us
    all_to_all x1, starting transfers between devices, per_device(): lax.all_to_all(send, ('lon', 'lat'), split_axis=0, concat_axis=0, tiled=T...  13 us
    ppermute x1, waiting for transfers between devices, run(): got_a = lax.ppermute(msg, ('lon', 'lat'), pairs_a)  10.3 us
    dot_general x8, matrix products, edges(): jnp.einsum('nyx,xc->ncy', part, sel.astype(jnp.float32), precision=lax.Pr...  9.55 us
    ppermute x1, starting transfers between devices, run(): got_a = lax.ppermute(msg, ('lon', 'lat'), pairs_a)  4.81 us
    ppermute x1, waiting for transfers between devices, per_device(): from_east = lax.ppermute(col_msg, 'lon', ring_west)  4.01 us
    dot_general x3, matrix products, exact_dot(): lax.dot_general(left, right, (((left_dim,), (0,)), ((), ())), precision=l...  3.66 us
    ppermute x1, starting transfers between devices, per_device(): from_above = lax.ppermute(bot_msg, 'lat', down)  3.3 us
  transfers between devices with their start and end apart: 7, of which 3 were waited for; matrix products, arithmetic and copies ran while one was open for 21% of the time, Pallas kernels for 0%

profile of v6, /device:TPU:95, one launch (start us, length us, event | category | flops | bytes accessed | tf_op | source)
XLA Modules:
  0.0 113.7 jit_solution(5216508122297936797)
XLA Ops:
  0.0 1.1 slice_convert_fusion
  1.1 1.0 fusion.75
  2.1 2.3 %broadcast_multiply_fusion = (f32[4,10,3,512]{3,2,1,0:T(4,128)}, f32[4,10,3,512]{3,2,1,0:T(4,128)S(1)}, f32[4,10,3,512]{3,2,1,0:T(4,128)S(1)}) fusion(f32[4]{0:T(128)} %constant.148.clone, f32[10,3,512]{2,1,0:T(4,128)S(1)} %get-tuple-element.44, f32[4,10,64,512]{3,2,1,0:T(8,128)} %adj_ref.1, f32[10,3,512]{2,1,0:T(4,128)S(1)} %get-tuple-element.43), kind=kLoop, calls=%fused_computation.62 | loop fusion | flops 184320 | bytes 1351696 | tf_op jit(solution)/shard_map/mul | solution.py:194
  4.4 0.8 copy_dynamic-update-slice_fusion
  5.2 0.7 copy_dynamic-update-slice_fusion.2
  5.9 3.3 %collective-permute-start.16 = (f32[50,3,512]{2,0,1:T(8,128)}, f32[50,3,512]{2,0,1:T(8,128)}, u32[]{:S(2)}, u32[]{:S(2)}) collective-permute-start(f32[50,3,512]{2,0,1:T(8,128)} %copy_dynamic-update-slice_fusion.2), channel_id=1, source_target_pairs={{1,0},{2,1},{3,2},{4,3},{5,4},{6,5},{7,6},{8,7},{9,8},{10,9},{11,1... | collective-permute-start | bytes 921608 | tf_op jit(solution)/shard_map/ppermute | solution.py:192
  9.2 0.8 copy_dynamic-update-slice_fusion.1
  9.9 0.7 copy_dynamic-update-slice_fusion.3
  10.6 1.3 %collective-permute-start.17 = (f32[50,3,512]{2,0,1:T(8,128)}, f32[50,3,512]{2,0,1:T(8,128)}, u32[]{:S(2)}, u32[]{:S(2)}) collective-permute-start(f32[50,3,512]{2,0,1:T(8,128)} %copy_dynamic-update-slice_fusion.3), channel_id=1, source_target_pairs={{0,1},{1,2},{2,3},{3,4},{4,5},{5,6},{6,7},{7,8},{8,9},{9,10},{10,1... | collective-permute-start | bytes 921608 | tf_op jit(solution)/shard_map/ppermute | solution.py:191
  12.3 0.8 fusion
  13.4 1.9 %fusion.1 = f32[1024,128]{1,0:T(8,128)S(1)} fusion(f32[512,128]{1,0:T(8,128)S(1)} %copy-done, s32[512]{0:T(512)S(1)} %bitcast.74), kind=kOutput, calls=%fused_computation.11 | convolution fusion | flops 805830656 | bytes 788480 | tf_op jit(solution)/shard_map/dot_general | solution.py:16
  15.4 1.2 %all_to_all.8 = f32[128,1,1152]{2,1,0:T(1,128)} reshape(f32[128,1152]{1,0:T(8,128)S(1)} %select_maximum_fusion) | data formatting | bytes 1179648 | tf_op jit(solution)/shard_map/all_to_all | solution.py:257
  16.7 13.0 %all-to-all-start = ((f32[128,1,1152]{2,1,0:T(1,128)}), f32[128,1,1152]{2,1,0:T(1,128)S(1)}, u32[]{:S(2)}, u32[]{:S(2)}) async-start(f32[128,1,1152]{2,1,0:T(1,128)} %all_to_all.8), calls=%async_computation | async-start | bytes 1179648 | tf_op jit(solution)/shard_map/all_to_all | solution.py:257
  29.7 1.2 %slice.75 = s32[1]{0:T(128)} slice(s32[512]{0:T(512)} %param.28), slice={[0:1]} | slice | bytes 8 | tf_op jit(solution)/shard_map/slice | solution.py:135
  31.7 1.1 %copy-done.2 = f32[10,64,512]{2,1,0:T(8,128)S(1)} copy-done((f32[10,64,512]{2,1,0:T(8,128)S(1)}, f32[10,64,512]{2,1,0:T(8,128)}, u32[]{:S(2)}) %copy-start.2) | copy-done | bytes 1310744
  34.2 3.0 %fusion.5 = f32[8,40,64]{2,0,1:T(8,128)S(1)} fusion(f32[40,64,512]{2,1,0:T(8,128)} %bitcast.58, s32[8]{0:T(128)S(1)} %iota_add_fusion, pred[8]{0:T(512)(128)(4,1)S(1)} %get-tuple-element.49), kind=kOutput, calls=%fused_computation.14 | convolution fusion | flops 31459328 | bytes 1392680 | tf_op jit(solution)/shard_map/nyx,xc->ncy/dot_general | solution.py:211
  37.8 3.7 %fusion.18 = f32[40,8,64]{2,1,0:T(8,128)} fusion(f32[40,8,64]{2,1,0:T(8,128)S(1)} %bitcast.68, f32[8,40,64]{2,0,1:T(8,128)S(1)} %fusion.5, f32[40,64,512]{2,1,0:T(8,128)} %bitcast.59, pred[8]{0:T(512)(128)(4,1)S(1)} %copy-done.6), kind=kOutput, calls=%fused_computation.22 | convolution fusion | flops 31500288 | bytes 1556488 | tf_op jit(solution)/shard_map/nyx,xc->ncy/dot_general | solution.py:211
  42.1 16.6 %conditional.1 = (f32[50,3,1024]{2,0,1:T(8,128)S(1)}) conditional(s32[]{:T(128)} %clamp.3, f32[50,3,512]{2,1,0:T(4,128)S(1)} %fusion.27, f32[50,3,512]{2,1,0:T(4,128)S(1)} %fusion.27, f32[50,3,512]{2,1,0:T(4,128)S(1)} %fusion.27, f32[50,3,512]{2,1,0:T(4,128)S(1)} %fusion.27, f32[50,3,512]{2,1,0:T(4,128)S(1)} %fusion.27, ...), branch_computations={%region_1.2_spmd, %region_2.3_spmd, %region_3.4_spmd, %region_4.5_... | conditional | flops 153600 | bytes 4915288 | solution.py:154
  42.1 0.7 collective-permute-start.13
  42.7 4.8 %collective-permute-start.12 = (f32[50,3,512]{2,1,0:T(4,128)S(1)}, f32[50,3,512]{2,1,0:T(4,128)S(1)}, u32[]{:S(2)}, u32[]{:S(2)}) collective-permute-start(f32[50,3,512]{2,1,0:T(4,128)S(1)} %param.6), channel_id=1, source_target_pairs={{95,15},{79,31},{63,47},{47,63},{31,79},{15,95},{127,111},{111,127}} | collective-permute-start | bytes 921608 | tf_op jit(solution)/shard_map/cond/branch_6_fun/ppermute | solution.py:148
  47.6 10.3 %collective-permute-done.12 = f32[50,3,512]{2,1,0:T(4,128)S(1)} collective-permute-done((f32[50,3,512]{2,1,0:T(4,128)S(1)}, f32[50,3,512]{2,1,0:T(4,128)S(1)}, u32[]{:S(2)}, u32[]{:S(2)}) %collective-permute-start.12) | collective-permute-done | bytes 307232 | tf_op jit(solution)/shard_map/cond/branch_6_fun/ppermute | solution.py:148
  58.6 0.9 fusion.9
  59.6 1.2 %pad_maximum_fusion.8 = f32[50,8,512]{2,0,1:T(8,128)S(1)} fusion(f32[50,3,512]{2,0,1:T(8,128)} %collective-permute-done.17, f32[50,3,512]{2,0,1:T(8,128)S(1)} %fusion.9, f32[8]{0:T(128)S(1)} %pad.25.clone), kind=kLoop, calls=%fused_computation.32 | loop fusion | flops 409600 | bytes 1433632 | tf_op jit(solution)/shard_map/concatenate | solution.py:202
  62.0 3.1 %collective-permute-start.19 = (f32[50,8,72]{2,1,0:T(8,128)S(1)}, f32[50,8,72]{2,1,0:T(8,128)S(1)}, u32[]{:S(2)}, u32[]{:S(2)}) collective-permute-start(f32[50,8,72]{2,1,0:T(8,128)S(1)} %pad_maximum_fusion.11), channel_id=1, source_target_pairs={{0,16},{16,32},{32,48},{48,64},{64,80},{80,96},{96,112},{112,0},{1... | collective-permute-start | bytes 345608 | tf_op jit(solution)/shard_map/ppermute | solution.py:224
  65.1 0.7 copy.71.cor_ref
  65.8 1.4 %copy.66 = f32[50,8,512]{2,1,0:T(8,128)} copy(f32[50,8,512]{2,0,1:T(8,128)S(1)} %pad_maximum_fusion.8) | data formatting | bytes 1638400 | tf_op jit(solution)/shard_map/concatenate | solution.py:202
  67.8 4.0 %collective-permute-done.18 = f32[50,8,72]{2,1,0:T(8,128)S(1)} collective-permute-done((f32[50,8,72]{2,1,0:T(8,128)S(1)}, f32[50,8,72]{2,1,0:T(8,128)S(1)}, u32[]{:S(2)}, u32[]{:S(2)}) %collective-permute-start.18) | collective-permute-done | bytes 115232 | tf_op jit(solution)/shard_map/ppermute | solution.py:223
  71.8 3.0 %fusion.41 = f32[50,72,128]{2,1,0:T(8,128)} fusion(f32[50,8,72]{2,1,0:T(8,128)S(1)} %collective-permute-done.18, f32[50,8,72]{2,1,0:T(8,128)S(1)} %collective-permute-done.19, pred[8]{0:T(512)(128)(4,1)S(1)} %copy-done.6, s32[8]{0:T(128)S(1)} %copy-done.8, pred[8]{0:T(512)(128)(4,1)S(1)} %copy-done.10), kind=kOutput, calls=%fused_computation.60 | convolution fusion | flops 44270720 | bytes 2073648 | tf_op jit(solution)/shard_map/ncy,cl->nyl/dot_general | solution.py:228
  74.8 0.7 copy.61
  75.7 0.9 reshape.329.vals_ref
  76.7 0.7 reshape_squeeze.4.weight_ref
  78.4 35.1 %shard_map.109 = f32[4,10,64,512]{3,2,1,0:T(8,128)} custom-call(s32[6,1024]{1,0:T(8,128)} %stack.21.where_ref, f32[1024]{0:T(1024)} %reshape_squeeze.4.weight_ref, f32[4,10,64,512]{3,2,1,0:T(8,128)} %adj_ref.1, s32[10,64,512]{2,1,0:T(8,128)} %mask_ref.1, f32[10,64,512]{2,1,0:T(8,128)} %diff_ref.1, f32[5,10,8,512]{3,2,1,0:T(8,128)} %bitcast.62, ...), custom_call_target="tpu_custom_call" | custom-call | tf_op jit(solution)/shard_map/pallas_call | solution.py:101
  (75 shorter events, 7.1 us)
Async XLA Ops:
  0.0 13.4 %copy-start = (f32[512,128]{1,0:T(8,128)S(1)}, f32[512,128]{1,0:T(8,128)}, u32[]{:S(2)}) copy-start(f32[512,128]{1,0:T(8,128)} %param.24) | copy-start | bytes 786436
  2.1 9.8 %copy-start.12 = (s32[512]{0:T(512)S(1)}, s32[512]{0:T(512)}, u32[]{:S(2)}) copy-start(s32[512]{0:T(512)} %param.27) | copy-start | bytes 6148
  2.1 9.8 %copy-start.11 = (s32[512,1]{0,1:T(1,128)S(1)}, s32[512,1]{0,1:T(1,128)}, u32[]{:S(2)}) copy-start(s32[512,1]{0,1:T(1,128)} %param.26) | copy-start | bytes 6148
  4.4 7.8 %copy-start.14 = (f32[512]{0:T(512)S(1)}, f32[512]{0:T(512)}, u32[]{:S(2)}) copy-start(f32[512]{0:T(512)} %param.25) | copy-start | bytes 6148
  5.9 52.8 %collective-permute-start.16 = (f32[50,3,512]{2,0,1:T(8,128)}, f32[50,3,512]{2,0,1:T(8,128)}, u32[]{:S(2)}, u32[]{:S(2)}) collective-permute-start(f32[50,3,512]{2,0,1:T(8,128)} %copy_dynamic-update-slice_fusion.2), channel_id=1, source_target_pairs={{1,0},{2,1},{3,2},{4,3},{5,4},{6,5},{7,6},{8,7},{9,8},{10,9},{11,1... | collective-permute-start | bytes 921608 | tf_op jit(solution)/shard_map/ppermute | solution.py:192
  10.6 49.0 %collective-permute-start.17 = (f32[50,3,512]{2,0,1:T(8,128)}, f32[50,3,512]{2,0,1:T(8,128)}, u32[]{:S(2)}, u32[]{:S(2)}) collective-permute-start(f32[50,3,512]{2,0,1:T(8,128)} %copy_dynamic-update-slice_fusion.3), channel_id=1, source_target_pairs={{0,1},{1,2},{2,3},{3,4},{4,5},{5,6},{6,7},{7,8},{8,9},{9,10},{10,1... | collective-permute-start | bytes 921608 | tf_op jit(solution)/shard_map/ppermute | solution.py:191
  15.4 16.1 %copy-start.1 = (s32[10,64,512]{2,1,0:T(8,128)S(1)}, s32[10,64,512]{2,1,0:T(8,128)}, u32[]{:S(2)}) copy-start(s32[10,64,512]{2,1,0:T(8,128)} %mask_ref.1) | copy-start | bytes 3932164
  16.7 58.1 %all-to-all-start = ((f32[128,1,1152]{2,1,0:T(1,128)}), f32[128,1,1152]{2,1,0:T(1,128)S(1)}, u32[]{:S(2)}, u32[]{:S(2)}) async-start(f32[128,1,1152]{2,1,0:T(1,128)} %all_to_all.8), calls=%async_computation | async-start | bytes 1179648 | tf_op jit(solution)/shard_map/all_to_all | solution.py:257
  31.5 5.7 %copy-start.7 = (s32[8]{0:T(128)}, s32[8]{0:T(128)S(1)}, u32[]{:S(2)}) copy-start(s32[8]{0:T(128)S(1)} %iota_add_fusion) | copy-start | bytes 100
  31.5 2.2 %copy-start.5 = (pred[8]{0:T(512)(128)(4,1)}, pred[8]{0:T(512)(128)(4,1)S(1)}, u32[]{:S(2)}) copy-start(pred[8]{0:T(512)(128)(4,1)S(1)} %get-tuple-element.50) | copy-start | bytes 28
  31.5 5.6 %copy-start.9 = (pred[8]{0:T(512)(128)(4,1)}, pred[8]{0:T(512)(128)(4,1)S(1)}, u32[]{:S(2)}) copy-start(pred[8]{0:T(512)(128)(4,1)S(1)} %get-tuple-element.49) | copy-start | bytes 28
  31.5 1.3 %copy-start.2 = (f32[10,64,512]{2,1,0:T(8,128)S(1)}, f32[10,64,512]{2,1,0:T(8,128)}, u32[]{:S(2)}) copy-start(f32[10,64,512]{2,1,0:T(8,128)} %diff_ref.1) | copy-start | bytes 3932164
  31.5 1.8 %copy-start.3 = (f32[4,10,3,512]{3,2,1,0:T(4,128)S(1)}, f32[4,10,3,512]{3,2,1,0:T(4,128)}, u32[]{:S(2)}) copy-start(f32[4,10,3,512]{3,2,1,0:T(4,128)} %get-tuple-element.31) | copy-start | bytes 737284
  34.2 3.6 %copy-start.6 = (pred[8]{0:T(512)(128)(4,1)S(1)}, pred[8]{0:T(512)(128)(4,1)}, u32[]{:S(2)}) copy-start(pred[8]{0:T(512)(128)(4,1)} %copy-done.5) | copy-start | bytes 28
  37.7 3.7 %copy-start.8 = (s32[8]{0:T(128)S(1)}, s32[8]{0:T(128)}, u32[]{:S(2)}) copy-start(s32[8]{0:T(128)} %copy-done.7) | copy-start | bytes 100
  37.7 3.7 %copy-start.10 = (pred[8]{0:T(512)(128)(4,1)S(1)}, pred[8]{0:T(512)(128)(4,1)}, u32[]{:S(2)}) copy-start(pred[8]{0:T(512)(128)(4,1)} %copy-done.9) | copy-start | bytes 28
  42.1 5.5 %collective-permute-start.13 = (f32[50,3,512]{2,1,0:T(4,128)S(1)}, f32[50,3,512]{2,1,0:T(4,128)S(1)}, u32[]{:S(2)}, u32[]{:S(2)}) collective-permute-start(f32[50,3,512]{2,1,0:T(4,128)S(1)} %param.6), channel_id=1, source_target_pairs={{111,15},{95,31},{79,47},{63,63},{47,79},{31,95},{15,111},{127,127}} | collective-permute-start | bytes 921608 | tf_op jit(solution)/shard_map/cond/branch_6_fun/ppermute | solution.py:149
  42.7 15.1 %collective-permute-start.12 = (f32[50,3,512]{2,1,0:T(4,128)S(1)}, f32[50,3,512]{2,1,0:T(4,128)S(1)}, u32[]{:S(2)}, u32[]{:S(2)}) collective-permute-start(f32[50,3,512]{2,1,0:T(4,128)S(1)} %param.6), channel_id=1, source_target_pairs={{95,15},{79,31},{63,47},{47,63},{31,79},{15,95},{127,111},{111,127}} | collective-permute-start | bytes 921608 | tf_op jit(solution)/shard_map/cond/branch_6_fun/ppermute | solution.py:148
  59.6 2.3 %copy-start.4 = (f32[40,8,64]{2,1,0:T(8,128)S(1)}, f32[40,8,64]{2,1,0:T(8,128)}, u32[]{:S(2)}) copy-start(f32[40,8,64]{2,1,0:T(8,128)} %fusion.18) | copy-start | bytes 245764
  59.6 5.5 %copy-start.13 = (f32[64]{0:T(128)S(1)}, f32[64]{0:T(128)}, u32[]{:S(2)}) copy-start(f32[64]{0:T(128)} %param.23) | copy-start | bytes 772
  62.0 5.8 %collective-permute-start.19 = (f32[50,8,72]{2,1,0:T(8,128)S(1)}, f32[50,8,72]{2,1,0:T(8,128)S(1)}, u32[]{:S(2)}, u32[]{:S(2)}) collective-permute-start(f32[50,8,72]{2,1,0:T(8,128)S(1)} %pad_maximum_fusion.11), channel_id=1, source_target_pairs={{0,16},{16,32},{32,48},{48,64},{64,80},{80,96},{96,112},{112,0},{1... | collective-permute-start | bytes 345608 | tf_op jit(solution)/shard_map/ppermute | solution.py:224
  65.1 6.7 %collective-permute-start.18 = (f32[50,8,72]{2,1,0:T(8,128)S(1)}, f32[50,8,72]{2,1,0:T(8,128)S(1)}, u32[]{:S(2)}, u32[]{:S(2)}) collective-permute-start(f32[50,8,72]{2,1,0:T(8,128)S(1)} %pad_maximum_fusion.11), channel_id=1, source_target_pairs={{0,112},{16,0},{32,16},{48,32},{64,48},{80,64},{96,80},{112,96},{1... | collective-permute-start | bytes 345608 | tf_op jit(solution)/shard_map/ppermute | solution.py:223

commit v7 on v5

--- a/solution.py
+++ b/solution.py
@@ -23,6 +23,7 @@
 
 
 def step_kernel(
+    tiles_ref,
     where_ref, weight_ref, adj_ref, mask_ref, diff_ref, rows_ref, cols_ref, cor_ref, vals_ref,
     traj_hbm, out_ref, xs, ds, traj_ref, sem
 ):
@@ -64,10 +65,10 @@
     @pl.when(k == last)
     def _():
         pltpu.make_async_copy(traj_hbm, traj_ref, sem).wait()
-        add_forcing(where_ref, weight_ref, vals_ref, traj_ref, mask_ref, out_ref)
-
-
-def add_forcing(where_ref, weight_ref, vals_ref, traj_ref, mask_ref, out_ref):
+        add_forcing(tiles_ref[0], where_ref, weight_ref, vals_ref, traj_ref, mask_ref, out_ref)
+
+
+def add_forcing(tiles, where_ref, weight_ref, vals_ref, traj_ref, mask_ref, out_ref):
     seg_width = vals_ref.shape[1]
     sub = lax.broadcasted_iota(jnp.int32, (8, seg_width), 0)
 
@@ -91,17 +92,17 @@
             add_row(first + j, vals8[j : j + 1, :])
         return carry
 
-    lax.fori_loop(0, vals_ref.shape[0] // 8, body, 0)
-
-
-def step_call(where, weight, adjoint, land_mask, diffusivity, rows5, cols5, coriolis, values, traj3):
+    lax.fori_loop(0, tiles, body, 0)
+
+
+def step_call(tiles, where, weight, adjoint, land_mask, diffusivity, rows5, cols5, coriolis, values, traj3):
     fields, levels, h, w = adjoint.shape
     hp, wp = h + PAD_ROWS, w + PAD_LANES
     whole = lambda shape: pl.BlockSpec(shape, lambda k, *_: (0,) * len(shape))
     return pl.pallas_call(
         step_kernel,
         grid_spec=pltpu.PrefetchScalarGridSpec(
-            num_scalar_prefetch=2,
+            num_scalar_prefetch=3,
             grid=(levels,),
             in_specs=[
                 pl.BlockSpec((fields, 1, h, w), lambda k, *_: (0, k, 0, 0)),
@@ -123,7 +124,7 @@
         ),
         out_shape=jax.ShapeDtypeStruct(adjoint.shape, jnp.float32),
         compiler_params=pltpu.CompilerParams(vmem_limit_bytes=60 * 1024 * 1024),
-    )(where, weight, adjoint, land_mask, diffusivity, rows5, cols5, coriolis.reshape(h, 1), values, traj3)
+    )(tiles, where, weight, adjoint, land_mask, diffusivity, rows5, cols5, coriolis.reshape(h, 1), values, traj3)
 
 
 def fold_rows(top_msg, fold_partner, width):
@@ -255,7 +256,25 @@
     got_values = got[:, : CAP * seg_width].reshape(devices * CAP, seg_width)
     got_meta = got[:, CAP * seg_width : CAP * seg_width + 2 * CAP].reshape(devices, 2, CAP)
     got_weight = got_meta[:, 0, :].reshape(devices * CAP)
-    got_offset = got_meta[:, 1, :].reshape(devices * CAP).astype(jnp.int32)
+    got_offset = got_meta[:, 1, :].reshape(devices * CAP)
+    n_slots = devices * CAP
+    filled = got_weight != 0.0
+    slot_order = jnp.arange(n_slots, dtype=jnp.int32)
+    earlier_slots = (slot_order[None, :] < slot_order[:, None]).astype(jnp.bfloat16)
+    packed_at = lax.dot_general(
+        earlier_slots,
+        filled.astype(jnp.bfloat16)[:, None],
+        (((1,), (0,)), ((), ())),
+        preferred_element_type=jnp.float32,
+    )[:, 0].astype(jnp.int32)
+    pack = ((packed_at[None, :] == slot_order[:, None]) & filled[None, :]).astype(jnp.float32)
+    payload = jnp.concatenate([got_values, got_weight[:, None], got_offset[:, None]], axis=1)
+    packed = exact_dot(pack, payload, 1)
+    got_values = packed[:, :seg_width]
+    got_weight = packed[:, seg_width]
+    got_offset = packed[:, seg_width + 1].astype(jnp.int32)
+    n_filled = jnp.sum(filled.astype(jnp.int32))
+    tiles = ((n_filled + 7) // 8).reshape(1)
 
     segments = w // seg_width
     seg_local = got_offset % segments
@@ -274,6 +293,7 @@
         axis=0,
     )
     return step_call(
+        tiles,
         where,
         got_weight,
         adjoint,

time: 108 us -> 112 us (1.037)
  the two profiles are of different devices: /device:TPU:95 before, /device:TPU:123 now
where the time goes in v7:
time: 112 us
  Pallas kernels  35.1 us (31%)
  starting transfers between devices  21.5 us (19%)
  matrix products  20.3 us (18%)
  waiting for transfers between devices  12.3 us (11%)
  local copies, waits for them, and re-layouts  11 us (10%)
  other arithmetic  9.24 us (8%)
  between operations  1.92 us (2%)
    pallas_call x1, Pallas kernels, step_call(): pl.pallas_call(step_kernel, grid_spec=pltpu.PrefetchScalarGridSpec(num_sc...  35.1 us
    all_to_all x1, starting transfers between devices, per_device(): lax.all_to_all(send, ('lon', 'lat'), split_axis=0, concat_axis=0, tiled=T...  10 us
    dot_general x8, matrix products, edges(): jnp.einsum('nyx,xc->ncy', part, sel.astype(jnp.float32), precision=lax.Pr...  8.84 us
    dot_general x4, matrix products, exact_dot(): lax.dot_general(left, right, (((left_dim,), (0,)), ((), ())), precision=l...  7.04 us
    ppermute x1, waiting for transfers between devices, run(): got_a = lax.ppermute(msg, ('lon', 'lat'), pairs_a)  6.48 us
    ppermute x1, waiting for transfers between devices, run(): got_b = lax.ppermute(msg, ('lon', 'lat'), pairs_b)  4.64 us
    ppermute x1, starting transfers between devices, run(): got_b = lax.ppermute(msg, ('lon', 'lat'), pairs_b)  3.72 us
    ppermute x1, starting transfers between devices, per_device(): from_above = lax.ppermute(bot_msg, 'lat', down)  2.99 us
  transfers between devices with their start and end apart: 7, of which 4 were waited for; matrix products, arithmetic and copies ran while one was open for 20% of the time, Pallas kernels for 0%

profile of v7, /device:TPU:123, one launch (start us, length us, event | category | flops | bytes accessed | tf_op | source)
XLA Modules:
  0.0 111.6 jit_solution(15611483771836556494)
XLA Ops:
  0.0 0.7 convert_element_type.94
  0.7 1.1 fusion.27
  1.8 0.7 multiply_add_fusion
  2.5 1.5 %fusion.5 = f32[1024,2]{0,1:T(2,128)S(1)} fusion(s32[512]{0:T(512)S(1)} %bitcast.90, f32[512,1]{0,1:T(1,128)S(1)} %bitcast.92, f32[512,1]{0,1:T(1,128)} %bitcast.94), kind=kOutput, calls=%fused_computation.16 | convolution fusion | flops 13108224 | bytes 14336 | tf_op jit(solution)/shard_map/dot_general | solution.py:16
  4.3 1.9 %fusion.6 = f32[1024,128]{1,0:T(8,128)S(1)} fusion(f32[512,128]{1,0:T(8,128)S(1)} %copy-done, s32[512]{0:T(512)S(1)} %bitcast.91), kind=kOutput, calls=%fused_computation.17 | convolution fusion | flops 805830656 | bytes 788480 | tf_op jit(solution)/shard_map/dot_general | solution.py:16
  6.2 0.9 reshape_reshape.3
  7.1 1.2 %select_maximum_fusion = f32[128,1152]{1,0:T(8,128)S(1)} fusion(f32[128,16]{1,0:T(8,128)S(1)} %copy.115, f32[128,1024]{1,0:T(8,128)} %reshape_reshape.3), kind=kLoop, calls=%fused_computation.47 | loop fusion | flops 442368 | bytes 1122304 | tf_op jit(solution)/shard_map/concatenate | solution.py:254
  8.3 1.2 %all_to_all.8 = f32[128,1,1152]{2,1,0:T(1,128)} reshape(f32[128,1152]{1,0:T(8,128)S(1)} %select_maximum_fusion) | data formatting | bytes 1179648 | tf_op jit(solution)/shard_map/all_to_all | solution.py:255
  9.5 10.0 %all-to-all-start = ((f32[128,1,1152]{2,1,0:T(1,128)}), f32[128,1,1152]{2,1,0:T(1,128)S(1)}, u32[]{:S(2)}, u32[]{:S(2)}) async-start(f32[128,1,1152]{2,1,0:T(1,128)} %all_to_all.8), calls=%async_computation | async-start | bytes 1179648 | tf_op jit(solution)/shard_map/all_to_all | solution.py:255
  19.7 2.3 %broadcast_multiply_fusion = (f32[4,10,3,512]{3,2,1,0:T(4,128)}, f32[4,10,3,512]{3,2,1,0:T(4,128)S(1)}, f32[4,10,3,512]{3,2,1,0:T(4,128)S(1)}) fusion(f32[4]{0:T(128)} %constant.156.clone, f32[10,3,512]{2,1,0:T(4,128)S(1)} %get-tuple-element.36, f32[4,10,64,512]{3,2,1,0:T(8,128)} %adj_ref.1, f32[10,3,512]{2,1,0:T(4,128)S(1)} %get-tuple-element.35), kind=kLoop, calls=%fused_computation.74 | loop fusion | flops 184320 | bytes 1351696 | tf_op jit(solution)/shard_map/mul | solution.py:195
  22.1 0.8 pad_maximum_fusion.11
  22.8 3.0 %collective-permute-start.16 = (f32[50,3,512]{2,0,1:T(8,128)}, f32[50,3,512]{2,0,1:T(8,128)}, u32[]{:S(2)}, u32[]{:S(2)}) collective-permute-start(f32[50,3,512]{2,0,1:T(8,128)} %pad_maximum_fusion.11), channel_id=1, source_target_pairs={{1,0},{2,1},{3,2},{4,3},{5,4},{6,5},{7,6},{8,7},{9,8},{10,9},{11,1... | collective-permute-start | bytes 921608 | tf_op jit(solution)/shard_map/ppermute | solution.py:193
  25.9 0.8 pad_maximum_fusion.12
  26.7 1.3 %collective-permute-start.17 = (f32[50,3,512]{2,0,1:T(8,128)}, f32[50,3,512]{2,0,1:T(8,128)}, u32[]{:S(2)}, u32[]{:S(2)}) collective-permute-start(f32[50,3,512]{2,0,1:T(8,128)} %pad_maximum_fusion.12), channel_id=1, source_target_pairs={{0,1},{1,2},{2,3},{3,4},{4,5},{5,6},{6,7},{7,8},{8,9},{9,10},{10,1... | collective-permute-start | bytes 921608 | tf_op jit(solution)/shard_map/ppermute | solution.py:192
  28.0 1.2 %slice.81 = s32[1]{0:T(128)} slice(s32[512]{0:T(512)} %param.28), slice={[0:1]} | slice | bytes 8 | tf_op jit(solution)/shard_map/slice | solution.py:136
  31.6 3.0 %fusion.11 = f32[8,40,64]{2,0,1:T(8,128)S(1)} fusion(f32[40,64,512]{2,1,0:T(8,128)} %bitcast.73, s32[8]{0:T(128)S(1)} %iota_add_fusion, pred[8]{0:T(512)(128)(4,1)S(1)} %get-tuple-element.43), kind=kOutput, calls=%fused_computation.21 | convolution fusion | flops 31459328 | bytes 1392680 | tf_op jit(solution)/shard_map/nyx,xc->ncy/dot_general | solution.py:212
  35.2 3.0 %fusion.24 = f32[40,8,64]{2,1,0:T(8,128)S(1)} fusion(f32[40,8,64]{2,1,0:T(8,128)S(1)} %bitcast.83, f32[8,40,64]{2,0,1:T(8,128)S(1)} %fusion.11, f32[40,64,512]{2,1,0:T(8,128)} %bitcast.74, pred[8]{0:T(512)(128)(4,1)S(1)} %copy-done.5), kind=kOutput, calls=%fused_computation.29 | convolution fusion | flops 31500288 | bytes 1556488 | tf_op jit(solution)/shard_map/nyx,xc->ncy/dot_general | solution.py:212
  38.8 17.6 %conditional.1 = (f32[50,3,1024]{2,0,1:T(8,128)S(1)}) conditional(s32[]{:T(128)} %clamp.3, f32[50,3,512]{2,1,0:T(4,128)S(1)} %fusion.38, f32[50,3,512]{2,1,0:T(4,128)S(1)} %fusion.38, f32[50,3,512]{2,1,0:T(4,128)S(1)} %fusion.38, f32[50,3,512]{2,1,0:T(4,128)S(1)} %fusion.38, f32[50,3,512]{2,1,0:T(4,128)S(1)} %fusion.38, ...), branch_computations={%region_2.3_spmd, %region_3.4_spmd, %region_4.5_spmd, %region_5.6_... | conditional | flops 153600 | bytes 4915288 | solution.py:155
  38.8 3.7 %collective-permute-start.9 = (f32[50,3,512]{2,1,0:T(4,128)S(1)}, f32[50,3,512]{2,1,0:T(4,128)S(1)}, u32[]{:S(2)}, u32[]{:S(2)}) collective-permute-start(f32[50,3,512]{2,1,0:T(4,128)S(1)} %param.4), channel_id=1, source_target_pairs={{79,15},{63,31},{47,47},{31,63},{15,79},{127,95},{111,111},{95,127}} | collective-permute-start | bytes 921608 | tf_op jit(solution)/shard_map/cond/branch_4_fun/ppermute | solution.py:150
  42.6 1.9 %collective-permute-start.8 = (f32[50,3,512]{2,1,0:T(4,128)S(1)}, f32[50,3,512]{2,1,0:T(4,128)S(1)}, u32[]{:S(2)}, u32[]{:S(2)}) collective-permute-start(f32[50,3,512]{2,1,0:T(4,128)S(1)} %param.4), channel_id=1, source_target_pairs={{63,15},{47,31},{31,47},{15,63},{127,79},{111,95},{95,111},{79,127}} | collective-permute-start | bytes 921608 | tf_op jit(solution)/shard_map/cond/branch_4_fun/ppermute | solution.py:149
  44.5 4.6 %collective-permute-done.9 = f32[50,3,512]{2,1,0:T(4,128)S(1)} collective-permute-done((f32[50,3,512]{2,1,0:T(4,128)S(1)}, f32[50,3,512]{2,1,0:T(4,128)S(1)}, u32[]{:S(2)}, u32[]{:S(2)}) %collective-permute-start.9) | collective-permute-done | bytes 307232 | tf_op jit(solution)/shard_map/cond/branch_4_fun/ppermute | solution.py:150
  49.1 6.5 %collective-permute-done.8 = f32[50,3,512]{2,1,0:T(4,128)S(1)} collective-permute-done((f32[50,3,512]{2,1,0:T(4,128)S(1)}, f32[50,3,512]{2,1,0:T(4,128)S(1)}, u32[]{:S(2)}, u32[]{:S(2)}) %collective-permute-start.8) | collective-permute-done | bytes 307232 | tf_op jit(solution)/shard_map/cond/branch_4_fun/ppermute | solution.py:149
  56.4 0.9 fusion.15
  57.4 1.1 %pad_maximum_fusion.8 = f32[50,8,512]{2,0,1:T(8,128)S(1)} fusion(f32[50,3,512]{2,0,1:T(8,128)} %collective-permute-done.17, f32[50,3,512]{2,0,1:T(8,128)S(1)} %fusion.15, f32[8]{0:T(128)S(1)} %pad.25.clone), kind=kLoop, calls=%fused_computation.44 | loop fusion | flops 409600 | bytes 1433632 | tf_op jit(solution)/shard_map/concatenate | solution.py:203
  59.8 1.5 %collective-permute-start.18 = (f32[50,8,72]{2,1,0:T(8,128)S(1)}, f32[50,8,72]{2,1,0:T(8,128)S(1)}, u32[]{:S(2)}, u32[]{:S(2)}) collective-permute-start(f32[50,8,72]{2,1,0:T(8,128)S(1)} %pad_maximum_fusion.13), channel_id=1, source_target_pairs={{0,112},{16,0},{32,16},{48,32},{64,48},{80,64},{96,80},{112,96},{1... | collective-permute-start | bytes 345608 | tf_op jit(solution)/shard_map/ppermute | solution.py:224
  61.2 0.7 copy.101.cor_ref
  61.9 1.4 %copy.96 = f32[50,8,512]{2,1,0:T(8,128)} copy(f32[50,8,512]{2,0,1:T(8,128)S(1)} %pad_maximum_fusion.8) | data formatting | bytes 1638400 | tf_op jit(solution)/shard_map/concatenate | solution.py:203
  63.3 1.1 collective-permute-done.19
  64.5 2.9 %fusion.52 = f32[50,72,128]{2,1,0:T(8,128)} fusion(f32[50,8,72]{2,1,0:T(8,128)S(1)} %collective-permute-done.18, f32[50,8,72]{2,1,0:T(8,128)S(1)} %collective-permute-done.19, pred[8]{0:T(512)(128)(4,1)S(1)} %copy-done.5, s32[8]{0:T(128)S(1)} %copy-done.7, pred[8]{0:T(512)(128)(4,1)S(1)} %copy-done.9), kind=kOutput, calls=%fused_computation.72 | convolution fusion | flops 44270720 | bytes 2073648 | tf_op jit(solution)/shard_map/ncy,cl->nyl/dot_general | solution.py:229
  71.1 2.7 %fusion.1 = f32[1024,130]{0,1:T(8,128)S(1)} fusion(s32[1024]{0:T(1024)S(1)} %convert_element_type.96, pred[1024]{0:T(1024)(128)(4,1)S(1)} %ne.254, f32[1024,1]{1,0:T(8,128)S(1)} %broadcast_in_dim_reshape_squeeze.9, f32[1024,1]{1,0:T(8,128)S(1)} %broadcast_in_dim_reshape_squeeze.8, f32[1024,128]{1,0:T(8,128)S(1)} %reshape.341), kind=kOutput, calls=%fused_computation.11 | convolution fusion | flops 1638141952 | bytes 1070080 | tf_op jit(solution)/shard_map/dot_general | solution.py:16
  74.6 1.0 copy.114.vals_ref
  76.3 35.1 %shard_map.109 = f32[4,10,64,512]{3,2,1,0:T(8,128)} custom-call(s32[1]{0:T(128)} %bitcast.9.tiles_ref, s32[6,1024]{1,0:T(8,128)} %stack.21.where_ref, f32[1024]{0:T(1024)} %bitcast.86, f32[4,10,64,512]{3,2,1,0:T(8,128)} %adj_ref.1, s32[10,64,512]{2,1,0:T(8,128)} %mask_ref.1, f32[10,64,512]{2,1,0:T(8,128)} %diff_ref.1, f32[5,10,8,512]{3,2,1,0:T(8,128)} %bitcast.77, ...), custom_call_target="tpu_custom_call" | custom-call | tf_op jit(solution)/shard_map/pallas_call | solution.py:102
  (79 shorter events, 9.8 us)
Async XLA Ops:
  0.0 4.3 %copy-start = (f32[512,128]{1,0:T(8,128)S(1)}, f32[512,128]{1,0:T(8,128)}, u32[]{:S(2)}) copy-start(f32[512,128]{1,0:T(8,128)} %param.24) | copy-start | bytes 786436
  7.1 12.5 %copy-start.1 = (s32[10,64,512]{2,1,0:T(8,128)S(1)}, s32[10,64,512]{2,1,0:T(8,128)}, u32[]{:S(2)}) copy-start(s32[10,64,512]{2,1,0:T(8,128)} %mask_ref.1) | copy-start | bytes 3932164
  7.1 12.5 %copy-start.2 = (f32[10,64,512]{2,1,0:T(8,128)S(1)}, f32[10,64,512]{2,1,0:T(8,128)}, u32[]{:S(2)}) copy-start(f32[10,64,512]{2,1,0:T(8,128)} %diff_ref.1) | copy-start | bytes 3932164
  9.5 57.9 %all-to-all-start = ((f32[128,1,1152]{2,1,0:T(1,128)}), f32[128,1,1152]{2,1,0:T(1,128)S(1)}, u32[]{:S(2)}, u32[]{:S(2)}) async-start(f32[128,1,1152]{2,1,0:T(1,128)} %all_to_all.8), calls=%async_computation | async-start | bytes 1179648 | tf_op jit(solution)/shard_map/all_to_all | solution.py:255
  22.8 33.6 %collective-permute-start.16 = (f32[50,3,512]{2,0,1:T(8,128)}, f32[50,3,512]{2,0,1:T(8,128)}, u32[]{:S(2)}, u32[]{:S(2)}) collective-permute-start(f32[50,3,512]{2,0,1:T(8,128)} %pad_maximum_fusion.11), channel_id=1, source_target_pairs={{1,0},{2,1},{3,2},{4,3},{5,4},{6,5},{7,6},{8,7},{9,8},{10,9},{11,1... | collective-permute-start | bytes 921608 | tf_op jit(solution)/shard_map/ppermute | solution.py:193
  26.7 30.7 %collective-permute-start.17 = (f32[50,3,512]{2,0,1:T(8,128)}, f32[50,3,512]{2,0,1:T(8,128)}, u32[]{:S(2)}, u32[]{:S(2)}) collective-permute-start(f32[50,3,512]{2,0,1:T(8,128)} %pad_maximum_fusion.12), channel_id=1, source_target_pairs={{0,1},{1,2},{2,3},{3,4},{4,5},{5,6},{6,7},{7,8},{8,9},{9,10},{10,1... | collective-permute-start | bytes 921608 | tf_op jit(solution)/shard_map/ppermute | solution.py:192
  29.9 1.0 copy-start.3
  29.9 4.7 %copy-start.6 = (s32[8]{0:T(128)}, s32[8]{0:T(128)S(1)}, u32[]{:S(2)}) copy-start(s32[8]{0:T(128)S(1)} %iota_add_fusion) | copy-start | bytes 100
  29.9 1.2 %copy-start.4 = (pred[8]{0:T(512)(128)(4,1)}, pred[8]{0:T(512)(128)(4,1)S(1)}, u32[]{:S(2)}) copy-start(pred[8]{0:T(512)(128)(4,1)S(1)} %get-tuple-element.44) | copy-start | bytes 28
  29.9 4.7 %copy-start.8 = (pred[8]{0:T(512)(128)(4,1)}, pred[8]{0:T(512)(128)(4,1)S(1)}, u32[]{:S(2)}) copy-start(pred[8]{0:T(512)(128)(4,1)S(1)} %get-tuple-element.43) | copy-start | bytes 28
  31.6 3.6 %copy-start.5 = (pred[8]{0:T(512)(128)(4,1)S(1)}, pred[8]{0:T(512)(128)(4,1)}, u32[]{:S(2)}) copy-start(pred[8]{0:T(512)(128)(4,1)} %copy-done.4) | copy-start | bytes 28
  35.2 3.0 %copy-start.7 = (s32[8]{0:T(128)S(1)}, s32[8]{0:T(128)}, u32[]{:S(2)}) copy-start(s32[8]{0:T(128)} %copy-done.6) | copy-start | bytes 100
  35.2 3.0 %copy-start.9 = (pred[8]{0:T(512)(128)(4,1)S(1)}, pred[8]{0:T(512)(128)(4,1)}, u32[]{:S(2)}) copy-start(pred[8]{0:T(512)(128)(4,1)} %copy-done.8) | copy-start | bytes 28
  38.8 10.3 %collective-permute-start.9 = (f32[50,3,512]{2,1,0:T(4,128)S(1)}, f32[50,3,512]{2,1,0:T(4,128)S(1)}, u32[]{:S(2)}, u32[]{:S(2)}) collective-permute-start(f32[50,3,512]{2,1,0:T(4,128)S(1)} %param.4), channel_id=1, source_target_pairs={{79,15},{63,31},{47,47},{31,63},{15,79},{127,95},{111,111},{95,127}} | collective-permute-start | bytes 921608 | tf_op jit(solution)/shard_map/cond/branch_4_fun/ppermute | solution.py:150
  42.6 13.0 %collective-permute-start.8 = (f32[50,3,512]{2,1,0:T(4,128)S(1)}, f32[50,3,512]{2,1,0:T(4,128)S(1)}, u32[]{:S(2)}, u32[]{:S(2)}) collective-permute-start(f32[50,3,512]{2,1,0:T(4,128)S(1)} %param.4), channel_id=1, source_target_pairs={{63,15},{47,31},{31,47},{15,63},{127,79},{111,95},{95,111},{79,127}} | collective-permute-start | bytes 921608 | tf_op jit(solution)/shard_map/cond/branch_4_fun/ppermute | solution.py:149
  57.4 3.9 %copy-start.10 = (f32[64]{0:T(128)S(1)}, f32[64]{0:T(128)}, u32[]{:S(2)}) copy-start(f32[64]{0:T(128)} %param.23) | copy-start | bytes 772
  59.7 4.7 %collective-permute-start.19 = (f32[50,8,72]{2,1,0:T(8,128)S(1)}, f32[50,8,72]{2,1,0:T(8,128)S(1)}, u32[]{:S(2)}, u32[]{:S(2)}) collective-permute-start(f32[50,8,72]{2,1,0:T(8,128)S(1)} %pad_maximum_fusion.13), channel_id=1, source_target_pairs={{0,16},{16,32},{32,48},{48,64},{64,80},{80,96},{96,112},{112,0},{1... | collective-permute-start | bytes 345608 | tf_op jit(solution)/shard_map/ppermute | solution.py:225
  59.8 4.7 %collective-permute-start.18 = (f32[50,8,72]{2,1,0:T(8,128)S(1)}, f32[50,8,72]{2,1,0:T(8,128)S(1)}, u32[]{:S(2)}, u32[]{:S(2)}) collective-permute-start(f32[50,8,72]{2,1,0:T(8,128)S(1)} %pad_maximum_fusion.13), channel_id=1, source_target_pairs={{0,112},{16,0},{32,16},{48,32},{64,48},{80,64},{96,80},{112,96},{1... | collective-permute-start | bytes 345608 | tf_op jit(solution)/shard_map/ppermute | solution.py:224

commit v8 on v5

--- a/solution.py
+++ b/solution.py
@@ -24,17 +24,19 @@
 
 def step_kernel(
     where_ref, weight_ref, adj_ref, mask_ref, diff_ref, rows_ref, cols_ref, cor_ref, vals_ref,
-    traj_hbm, out_ref, xs, ds, traj_ref, sem
+    traj_ref, out_ref, xs, ds
 ):
     fields = adj_ref.shape[0]
     h, w = adj_ref.shape[2], adj_ref.shape[3]
     hp, wp = xs.shape[1], xs.shape[2]
     k = pl.program_id(0)
-    last = pl.num_programs(0) - 1
+    per_step = vals_ref.shape[0] // pl.num_programs(0)
 
     @pl.when(k == 0)
     def _():
-        pltpu.make_async_copy(traj_hbm, traj_ref, sem).start()
+        out_ref[...] = jnp.zeros(out_ref.shape, jnp.float32)
+
+    add_forcing(k * per_step, per_step, where_ref, weight_ref, vals_ref, traj_ref, mask_ref, out_ref)
 
     wet = mask_ref[k].astype(jnp.float32)
     for f in range(fields):
@@ -56,18 +58,13 @@
             x = x + d * (east + west + north + south - 4.0 * x)
         done.append(x[0:h, 0:w])
     rot = cor_ref[...]
-    out_ref[0, k] = wet * done[0]
-    out_ref[1, k] = wet * done[1]
-    out_ref[2, k] = wet * (done[2] - rot * done[3])
-    out_ref[3, k] = wet * (done[3] + rot * done[2])
-
-    @pl.when(k == last)
-    def _():
-        pltpu.make_async_copy(traj_hbm, traj_ref, sem).wait()
-        add_forcing(where_ref, weight_ref, vals_ref, traj_ref, mask_ref, out_ref)
-
-
-def add_forcing(where_ref, weight_ref, vals_ref, traj_ref, mask_ref, out_ref):
+    out_ref[0, k] = out_ref[0, k] + wet * done[0]
+    out_ref[1, k] = out_ref[1, k] + wet * done[1]
+    out_ref[2, k] = out_ref[2, k] + wet * (done[2] - rot * done[3])
+    out_ref[3, k] = out_ref[3, k] + wet * (done[3] + rot * done[2])
+
+
+def add_forcing(start, count, where_ref, weight_ref, vals_ref, traj_ref, mask_ref, out_ref):
     seg_width = vals_ref.shape[1]
     sub = lax.broadcasted_iota(jnp.int32, (8, seg_width), 0)
 
@@ -84,19 +81,22 @@
         cur = out_ref[field, level, rows, cols]
         out_ref[field, level, rows, cols] = cur + jnp.where(hit, wet * misfit, 0.0)
 
-    def body(o, carry):
-        first = pl.multiple_of(o * 8, 8)
+    for t in range(count // 8):
+        first = pl.multiple_of(start + 8 * t, 8)
         vals8 = vals_ref[pl.ds(first, 8), :]
         for j in range(8):
             add_row(first + j, vals8[j : j + 1, :])
-        return carry
-
-    lax.fori_loop(0, vals_ref.shape[0] // 8, body, 0)
 
 
 def step_call(where, weight, adjoint, land_mask, diffusivity, rows5, cols5, coriolis, values, traj3):
     fields, levels, h, w = adjoint.shape
     hp, wp = h + PAD_ROWS, w + PAD_LANES
+    rows_in = values.shape[0]
+    per_step = -(-(-(-rows_in // levels)) // 8) * 8
+    extra = per_step * levels - rows_in
+    values = jnp.pad(values, ((0, extra), (0, 0)))
+    weight = jnp.pad(weight, (0, extra))
+    where = jnp.pad(where, ((0, 0), (0, extra)))
     whole = lambda shape: pl.BlockSpec(shape, lambda k, *_: (0,) * len(shape))
     return pl.pallas_call(
         step_kernel,
@@ -111,14 +111,12 @@
                 pl.BlockSpec((fields + 1, 1, hp, PAD_LANES), lambda k, *_: (0, k, 0, 0)),
                 whole((h, 1)),
                 whole(values.shape),
-                pl.BlockSpec(memory_space=pl.ANY),
+                whole(traj3.shape),
             ],
             out_specs=whole(adjoint.shape),
             scratch_shapes=[
                 pltpu.VMEM((fields, hp, wp), jnp.float32),
                 pltpu.VMEM((hp, wp), jnp.float32),
-                pltpu.VMEM(traj3.shape, jnp.float32),
-                pltpu.SemaphoreType.DMA(()),
             ],
         ),
         out_shape=jax.ShapeDtypeStruct(adjoint.shape, jnp.float32),

time: 108 us -> 104 us (0.963)
  starting transfers between devices: 26.3 us -> 22.1 us
  waiting for transfers between devices: 10.6 us -> 14.3 us
  Pallas kernels: 35.1 us -> 31.7 us
    ppermute x1, waiting for transfers between devices: 1.23 us -> 7.45 us  [run(): got_a = lax.ppermute(msg, ('lon', 'lat'), pairs_a)]
    ppermute x1, starting transfers between devices: 6.67 us -> 1.2 us  [per_device(): from_west = lax.ppermute(col_msg, 'lon', ring_east)]
    pallas_call x1, Pallas kernels: 35.1 us -> 31.7 us  [step_call(): pl.pallas_call(step_kernel, grid_spec=pltpu.PrefetchScalarGridSpec(num_sc...]
    ppermute x1, waiting for transfers between devices: 4.68 us -> 2.57 us  [run(): got_b = lax.ppermute(msg, ('lon', 'lat'), pairs_b)]
    pad x0 -> x3, local copies, waits for them, and re-layouts: none -> 2.06 us  [the longest x1 0.84 us: step_call(): values = jnp.pad(values, ((0, extra), (0, 0)))]
  transfers between devices with their start and end apart: 7 -> 7, of which waited for: 4 -> 4; matrix products, arithmetic and copies ran while one was open for 21% -> 22% of each run, Pallas kernels for 0% -> 0%
where the time goes in v8:
time: 104 us
  Pallas kernels  31.7 us (30%)
  starting transfers between devices  22.1 us (21%)
  matrix products  17.2 us (17%)
  waiting for transfers between devices  14.3 us (14%)
  local copies, waits for them, and re-layouts  9.57 us (9%)
  other arithmetic  7.42 us (7%)
    pallas_call x1, Pallas kernels, step_call(): pl.pallas_call(step_kernel, grid_spec=pltpu.PrefetchScalarGridSpec(num_sc...  31.7 us
    all_to_all x1, starting transfers between devices, per_device(): lax.all_to_all(send, ('lon', 'lat'), split_axis=0, concat_axis=0, tiled=T...  10.2 us
    dot_general x8, matrix products, edges(): jnp.einsum('nyx,xc->ncy', part, sel.astype(jnp.float32), precision=lax.Pr...  8.84 us
    ppermute x1, waiting for transfers between devices, run(): got_a = lax.ppermute(msg, ('lon', 'lat'), pairs_a)  7.45 us
    dot_general x3, matrix products, exact_dot(): lax.dot_general(left, right, (((left_dim,), (0,)), ((), ())), precision=l...  4.34 us
    ppermute x1, starting transfers between devices, run(): got_a = lax.ppermute(msg, ('lon', 'lat'), pairs_a)  3.64 us
    ppermute x1, waiting for transfers between devices, per_device(): from_east = lax.ppermute(col_msg, 'lon', ring_west)  3.24 us
    ppermute x1, starting transfers between devices, per_device(): from_above = lax.ppermute(bot_msg, 'lat', down)  2.99 us
  transfers between devices with their start and end apart: 7, of which 4 were waited for; matrix products, arithmetic and copies ran while one was open for 22% of the time, Pallas kernels for 0%

profile of v8, /device:TPU:95, one launch (start us, length us, event | category | flops | bytes accessed | tf_op | source)
XLA Modules:
  0.0 103.5 jit_solution(185191492777012512)
XLA Ops:
  0.0 0.7 convert_element_type.86
  0.7 1.1 %fusion.21 = f32[512]{0:T(512)S(1)} fusion(s32[512]{0:T(512)} %bitcast.72), kind=kOutput, calls=%fused_computation.23 | convolution fusion | flops 67763712 | bytes 4096 | tf_op jit(solution)/shard_map/dot_general | solution.py:239
  1.8 0.7 multiply_add_fusion
  2.5 1.5 %fusion = f32[1024,2]{0,1:T(2,128)S(1)} fusion(s32[512]{0:T(512)S(1)} %bitcast.73, f32[512,1]{0,1:T(1,128)S(1)} %bitcast.75, f32[512,1]{0,1:T(1,128)} %bitcast.77), kind=kOutput, calls=%fused_computation.10 | convolution fusion | flops 13108224 | bytes 14336 | tf_op jit(solution)/shard_map/dot_general | solution.py:16
  4.3 1.9 %fusion.1 = f32[1024,128]{1,0:T(8,128)S(1)} fusion(f32[512,128]{1,0:T(8,128)S(1)} %copy-done, s32[512]{0:T(512)S(1)} %bitcast.74), kind=kOutput, calls=%fused_computation.11 | convolution fusion | flops 805830656 | bytes 788480 | tf_op jit(solution)/shard_map/dot_general | solution.py:16
  6.4 1.2 %all_to_all.8 = f32[128,1,1152]{2,1,0:T(1,128)} reshape(f32[128,1152]{1,0:T(8,128)S(1)} %select_maximum_fusion) | data formatting | bytes 1179648 | tf_op jit(solution)/shard_map/all_to_all | solution.py:252
  7.6 10.2 %all-to-all-start = ((f32[128,1,1152]{2,1,0:T(1,128)}), f32[128,1,1152]{2,1,0:T(1,128)S(1)}, u32[]{:S(2)}, u32[]{:S(2)}) async-start(f32[128,1,1152]{2,1,0:T(1,128)} %all_to_all.8), calls=%async_computation | async-start | bytes 1179648 | tf_op jit(solution)/shard_map/all_to_all | solution.py:252
  17.9 2.3 %broadcast_multiply_fusion = (f32[4,10,3,512]{3,2,1,0:T(4,128)}, f32[4,10,3,512]{3,2,1,0:T(4,128)S(1)}, f32[4,10,3,512]{3,2,1,0:T(4,128)S(1)}) fusion(f32[4]{0:T(128)} %constant.148.clone, f32[10,3,512]{2,1,0:T(4,128)S(1)} %get-tuple-element.34, f32[4,10,64,512]{3,2,1,0:T(8,128)} %adj_ref.1, f32[10,3,512]{2,1,0:T(4,128)S(1)} %get-tuple-element.33), kind=kLoop, calls=%fused_computation.62 | loop fusion | flops 184320 | bytes 1351696 | tf_op jit(solution)/shard_map/mul | solution.py:192
  20.3 0.8 pad_maximum_fusion.11
  21.0 3.0 %collective-permute-start.16 = (f32[50,3,512]{2,0,1:T(8,128)}, f32[50,3,512]{2,0,1:T(8,128)}, u32[]{:S(2)}, u32[]{:S(2)}) collective-permute-start(f32[50,3,512]{2,0,1:T(8,128)} %pad_maximum_fusion.11), channel_id=1, source_target_pairs={{1,0},{2,1},{3,2},{4,3},{5,4},{6,5},{7,6},{8,7},{9,8},{10,9},{11,1... | collective-permute-start | bytes 921608 | tf_op jit(solution)/shard_map/ppermute | solution.py:190
  24.1 0.8 pad_maximum_fusion.12
  24.9 1.3 %collective-permute-start.17 = (f32[50,3,512]{2,0,1:T(8,128)}, f32[50,3,512]{2,0,1:T(8,128)}, u32[]{:S(2)}, u32[]{:S(2)}) collective-permute-start(f32[50,3,512]{2,0,1:T(8,128)} %pad_maximum_fusion.12), channel_id=1, source_target_pairs={{0,1},{1,2},{2,3},{3,4},{4,5},{5,6},{6,7},{7,8},{8,9},{9,10},{10,1... | collective-permute-start | bytes 921608 | tf_op jit(solution)/shard_map/ppermute | solution.py:189
  26.2 1.2 %slice.69 = s32[1]{0:T(128)} slice(s32[512]{0:T(512)} %param.28), slice={[0:1]} | slice | bytes 8 | tf_op jit(solution)/shard_map/slice | solution.py:133
  29.8 3.0 %fusion.5 = f32[8,40,64]{2,0,1:T(8,128)S(1)} fusion(f32[40,64,512]{2,1,0:T(8,128)} %bitcast.58, s32[8]{0:T(128)S(1)} %iota_add_fusion, pred[8]{0:T(512)(128)(4,1)S(1)} %get-tuple-element.40), kind=kOutput, calls=%fused_computation.14 | convolution fusion | flops 31459328 | bytes 1392680 | tf_op jit(solution)/shard_map/nyx,xc->ncy/dot_general | solution.py:209
  33.4 3.0 %fusion.18 = f32[40,8,64]{2,1,0:T(8,128)S(1)} fusion(f32[40,8,64]{2,1,0:T(8,128)S(1)} %bitcast.68, f32[8,40,64]{2,0,1:T(8,128)S(1)} %fusion.5, f32[40,64,512]{2,1,0:T(8,128)} %bitcast.59, pred[8]{0:T(512)(128)(4,1)S(1)} %copy-done.5), kind=kOutput, calls=%fused_computation.22 | convolution fusion | flops 31500288 | bytes 1556488 | tf_op jit(solution)/shard_map/nyx,xc->ncy/dot_general | solution.py:209
  37.0 16.9 %conditional.1 = (f32[50,3,1024]{2,0,1:T(8,128)S(1)}) conditional(s32[]{:T(128)} %clamp.3, f32[50,3,512]{2,1,0:T(4,128)S(1)} %fusion.27, f32[50,3,512]{2,1,0:T(4,128)S(1)} %fusion.27, f32[50,3,512]{2,1,0:T(4,128)S(1)} %fusion.27, f32[50,3,512]{2,1,0:T(4,128)S(1)} %fusion.27, f32[50,3,512]{2,1,0:T(4,128)S(1)} %fusion.27, ...), branch_computations={%region_1.2_spmd, %region_2.3_spmd, %region_3.4_spmd, %region_4.5_... | conditional | flops 153600 | bytes 4915288 | solution.py:152
  37.0 2.5 %collective-permute-start.11 = (f32[50,3,512]{2,1,0:T(4,128)S(1)}, f32[50,3,512]{2,1,0:T(4,128)S(1)}, u32[]{:S(2)}, u32[]{:S(2)}) collective-permute-start(f32[50,3,512]{2,1,0:T(4,128)S(1)} %param.5), channel_id=1, source_target_pairs={{95,15},{79,31},{63,47},{47,63},{31,79},{15,95},{127,111},{111,127}} | collective-permute-start | bytes 921608 | tf_op jit(solution)/shard_map/cond/branch_5_fun/ppermute | solution.py:147
  39.5 3.6 %collective-permute-start.10 = (f32[50,3,512]{2,1,0:T(4,128)S(1)}, f32[50,3,512]{2,1,0:T(4,128)S(1)}, u32[]{:S(2)}, u32[]{:S(2)}) collective-permute-start(f32[50,3,512]{2,1,0:T(4,128)S(1)} %param.5), channel_id=1, source_target_pairs={{79,15},{63,31},{47,47},{31,63},{15,79},{127,95},{111,111},{95,127}} | collective-permute-start | bytes 921608 | tf_op jit(solution)/shard_map/cond/branch_5_fun/ppermute | solution.py:146
  43.1 2.6 %collective-permute-done.11 = f32[50,3,512]{2,1,0:T(4,128)S(1)} collective-permute-done((f32[50,3,512]{2,1,0:T(4,128)S(1)}, f32[50,3,512]{2,1,0:T(4,128)S(1)}, u32[]{:S(2)}, u32[]{:S(2)}) %collective-permute-start.11) | collective-permute-done | bytes 307232 | tf_op jit(solution)/shard_map/cond/branch_5_fun/ppermute | solution.py:147
  45.7 7.5 %collective-permute-done.10 = f32[50,3,512]{2,1,0:T(4,128)S(1)} collective-permute-done((f32[50,3,512]{2,1,0:T(4,128)S(1)}, f32[50,3,512]{2,1,0:T(4,128)S(1)}, u32[]{:S(2)}, u32[]{:S(2)}) %collective-permute-start.10) | collective-permute-done | bytes 307232 | tf_op jit(solution)/shard_map/cond/branch_5_fun/ppermute | solution.py:146
  53.9 0.9 fusion.9
  54.9 1.1 %pad_maximum_fusion.8 = f32[50,8,512]{2,0,1:T(8,128)S(1)} fusion(f32[50,3,512]{2,0,1:T(8,128)} %collective-permute-done.17, f32[50,3,512]{2,0,1:T(8,128)S(1)} %fusion.9, f32[8]{0:T(128)S(1)} %pad.40.clone), kind=kLoop, calls=%fused_computation.32 | loop fusion | flops 409600 | bytes 1433632 | tf_op jit(solution)/shard_map/concatenate | solution.py:200
  57.2 1.2 %collective-permute-start.19 = (f32[50,8,72]{2,1,0:T(8,128)S(1)}, f32[50,8,72]{2,1,0:T(8,128)S(1)}, u32[]{:S(2)}, u32[]{:S(2)}) collective-permute-start(f32[50,8,72]{2,1,0:T(8,128)S(1)} %pad_maximum_fusion.13), channel_id=1, source_target_pairs={{0,16},{16,32},{32,48},{48,64},{64,80},{80,96},{96,112},{112,0},{1... | collective-permute-start | bytes 345608 | tf_op jit(solution)/shard_map/ppermute | solution.py:222
  58.8 0.7 copy.71.cor_ref
  59.5 1.4 %copy.66 = f32[50,8,512]{2,1,0:T(8,128)} copy(f32[50,8,512]{2,0,1:T(8,128)S(1)} %pad_maximum_fusion.8) | data formatting | bytes 1638400 | tf_op jit(solution)/shard_map/concatenate | solution.py:200
  60.9 1.1 %collective-permute-done.19 = f32[50,8,72]{2,1,0:T(8,128)S(1)} collective-permute-done((f32[50,8,72]{2,1,0:T(8,128)S(1)}, f32[50,8,72]{2,1,0:T(8,128)S(1)}, u32[]{:S(2)}, u32[]{:S(2)}) %collective-permute-start.19) | collective-permute-done | bytes 115232 | tf_op jit(solution)/shard_map/ppermute | solution.py:222
  61.9 3.2 %collective-permute-done.18 = f32[50,8,72]{2,1,0:T(8,128)S(1)} collective-permute-done((f32[50,8,72]{2,1,0:T(8,128)S(1)}, f32[50,8,72]{2,1,0:T(8,128)S(1)}, u32[]{:S(2)}, u32[]{:S(2)}) %collective-permute-start.18) | collective-permute-done | bytes 115232 | tf_op jit(solution)/shard_map/ppermute | solution.py:221
  65.2 3.0 %fusion.41 = f32[50,72,128]{2,1,0:T(8,128)} fusion(f32[50,8,72]{2,1,0:T(8,128)S(1)} %collective-permute-done.18, f32[50,8,72]{2,1,0:T(8,128)S(1)} %collective-permute-done.19, pred[8]{0:T(512)(128)(4,1)S(1)} %copy-done.5, s32[8]{0:T(128)S(1)} %copy-done.7, pred[8]{0:T(512)(128)(4,1)S(1)} %copy-done.9), kind=kOutput, calls=%fused_computation.60 | convolution fusion | flops 44270720 | bytes 2073648 | tf_op jit(solution)/shard_map/ncy,cl->nyl/dot_general | solution.py:226
  68.1 0.7 copy.57
  69.2 0.8 pad.19.vals_ref
  71.2 0.6 pad.17.where_ref
  71.8 31.7 %shard_map.109 = f32[4,10,64,512]{3,2,1,0:T(8,128)} custom-call(s32[6,1040]{1,0:T(8,128)} %pad.17.where_ref, f32[1040]{0:T(1024)} %pad.18.weight_ref, f32[4,10,64,512]{3,2,1,0:T(8,128)} %adj_ref.1, s32[10,64,512]{2,1,0:T(8,128)} %mask_ref.1, f32[10,64,512]{2,1,0:T(8,128)} %diff_ref.1, f32[5,10,8,512]{3,2,1,0:T(8,128)} %bitcast.62, ...), custom_call_target="tpu_custom_call" | custom-call | tf_op jit(solution)/shard_map/pallas_call | solution.py:101
  (72 shorter events, 7.3 us)
Async XLA Ops:
  0.0 4.3 %copy-start = (f32[512,128]{1,0:T(8,128)S(1)}, f32[512,128]{1,0:T(8,128)}, u32[]{:S(2)}) copy-start(f32[512,128]{1,0:T(8,128)} %param.24) | copy-start | bytes 786436
  6.3 11.4 %copy-start.1 = (s32[10,64,512]{2,1,0:T(8,128)S(1)}, s32[10,64,512]{2,1,0:T(8,128)}, u32[]{:S(2)}) copy-start(s32[10,64,512]{2,1,0:T(8,128)} %mask_ref.1) | copy-start | bytes 3932164
  6.4 11.5 %copy-start.2 = (f32[10,64,512]{2,1,0:T(8,128)S(1)}, f32[10,64,512]{2,1,0:T(8,128)}, u32[]{:S(2)}) copy-start(f32[10,64,512]{2,1,0:T(8,128)} %diff_ref.1) | copy-start | bytes 3932164
  7.6 60.5 %all-to-all-start = ((f32[128,1,1152]{2,1,0:T(1,128)}), f32[128,1,1152]{2,1,0:T(1,128)S(1)}, u32[]{:S(2)}, u32[]{:S(2)}) async-start(f32[128,1,1152]{2,1,0:T(1,128)} %all_to_all.8), calls=%async_computation | async-start | bytes 1179648 | tf_op jit(solution)/shard_map/all_to_all | solution.py:252
  21.0 32.9 %collective-permute-start.16 = (f32[50,3,512]{2,0,1:T(8,128)}, f32[50,3,512]{2,0,1:T(8,128)}, u32[]{:S(2)}, u32[]{:S(2)}) collective-permute-start(f32[50,3,512]{2,0,1:T(8,128)} %pad_maximum_fusion.11), channel_id=1, source_target_pairs={{1,0},{2,1},{3,2},{4,3},{5,4},{6,5},{7,6},{8,7},{9,8},{10,9},{11,1... | collective-permute-start | bytes 921608 | tf_op jit(solution)/shard_map/ppermute | solution.py:190
  24.9 30.0 %collective-permute-start.17 = (f32[50,3,512]{2,0,1:T(8,128)}, f32[50,3,512]{2,0,1:T(8,128)}, u32[]{:S(2)}, u32[]{:S(2)}) collective-permute-start(f32[50,3,512]{2,0,1:T(8,128)} %pad_maximum_fusion.12), channel_id=1, source_target_pairs={{0,1},{1,2},{2,3},{3,4},{4,5},{5,6},{6,7},{7,8},{8,9},{9,10},{10,1... | collective-permute-start | bytes 921608 | tf_op jit(solution)/shard_map/ppermute | solution.py:189
  28.0 4.8 %copy-start.6 = (s32[8]{0:T(128)}, s32[8]{0:T(128)S(1)}, u32[]{:S(2)}) copy-start(s32[8]{0:T(128)S(1)} %iota_add_fusion) | copy-start | bytes 100
  28.0 1.3 %copy-start.4 = (pred[8]{0:T(512)(128)(4,1)}, pred[8]{0:T(512)(128)(4,1)S(1)}, u32[]{:S(2)}) copy-start(pred[8]{0:T(512)(128)(4,1)S(1)} %get-tuple-element.41) | copy-start | bytes 28
  28.0 4.8 %copy-start.8 = (pred[8]{0:T(512)(128)(4,1)}, pred[8]{0:T(512)(128)(4,1)S(1)}, u32[]{:S(2)}) copy-start(pred[8]{0:T(512)(128)(4,1)S(1)} %get-tuple-element.40) | copy-start | bytes 28
  28.0 1.0 copy-start.3
  29.8 3.6 %copy-start.5 = (pred[8]{0:T(512)(128)(4,1)S(1)}, pred[8]{0:T(512)(128)(4,1)}, u32[]{:S(2)}) copy-start(pred[8]{0:T(512)(128)(4,1)} %copy-done.4) | copy-start | bytes 28
  33.3 3.0 %copy-start.7 = (s32[8]{0:T(128)S(1)}, s32[8]{0:T(128)}, u32[]{:S(2)}) copy-start(s32[8]{0:T(128)} %copy-done.6) | copy-start | bytes 100
  33.3 3.0 %copy-start.9 = (pred[8]{0:T(512)(128)(4,1)S(1)}, pred[8]{0:T(512)(128)(4,1)}, u32[]{:S(2)}) copy-start(pred[8]{0:T(512)(128)(4,1)} %copy-done.8) | copy-start | bytes 28
  37.0 8.7 %collective-permute-start.11 = (f32[50,3,512]{2,1,0:T(4,128)S(1)}, f32[50,3,512]{2,1,0:T(4,128)S(1)}, u32[]{:S(2)}, u32[]{:S(2)}) collective-permute-start(f32[50,3,512]{2,1,0:T(4,128)S(1)} %param.5), channel_id=1, source_target_pairs={{95,15},{79,31},{63,47},{47,63},{31,79},{15,95},{127,111},{111,127}} | collective-permute-start | bytes 921608 | tf_op jit(solution)/shard_map/cond/branch_5_fun/ppermute | solution.py:147
  39.5 13.7 %collective-permute-start.10 = (f32[50,3,512]{2,1,0:T(4,128)S(1)}, f32[50,3,512]{2,1,0:T(4,128)S(1)}, u32[]{:S(2)}, u32[]{:S(2)}) collective-permute-start(f32[50,3,512]{2,1,0:T(4,128)S(1)} %param.5), channel_id=1, source_target_pairs={{79,15},{63,31},{47,47},{31,63},{15,79},{127,95},{111,111},{95,127}} | collective-permute-start | bytes 921608 | tf_op jit(solution)/shard_map/cond/branch_5_fun/ppermute | solution.py:146
  54.9 3.9 %copy-start.10 = (f32[64]{0:T(128)S(1)}, f32[64]{0:T(128)}, u32[]{:S(2)}) copy-start(f32[64]{0:T(128)} %param.23) | copy-start | bytes 772
  57.2 4.7 %collective-permute-start.19 = (f32[50,8,72]{2,1,0:T(8,128)S(1)}, f32[50,8,72]{2,1,0:T(8,128)S(1)}, u32[]{:S(2)}, u32[]{:S(2)}) collective-permute-start(f32[50,8,72]{2,1,0:T(8,128)S(1)} %pad_maximum_fusion.13), channel_id=1, source_target_pairs={{0,16},{16,32},{32,48},{48,64},{64,80},{80,96},{96,112},{112,0},{1... | collective-permute-start | bytes 345608 | tf_op jit(solution)/shard_map/ppermute | solution.py:222
  58.4 6.7 %collective-permute-start.18 = (f32[50,8,72]{2,1,0:T(8,128)S(1)}, f32[50,8,72]{2,1,0:T(8,128)S(1)}, u32[]{:S(2)}, u32[]{:S(2)}) collective-permute-start(f32[50,8,72]{2,1,0:T(8,128)S(1)} %pad_maximum_fusion.13), channel_id=1, source_target_pairs={{0,112},{16,0},{32,16},{48,32},{64,48},{80,64},{96,80},{112,96},{1... | collective-permute-start | bytes 345608 | tf_op jit(solution)/shard_map/ppermute | solution.py:221

commit v9 on v8

--- a/solution.py
+++ b/solution.py
@@ -20,6 +20,16 @@
         precision=lax.Precision.HIGHEST,
         preferred_element_type=jnp.float32,
     )
+
+
+def exact_pick(spec, data, onehot):
+    hi = data.astype(jnp.bfloat16)
+    rest = data - hi.astype(jnp.float32)
+    mid = rest.astype(jnp.bfloat16)
+    lo = (rest - mid.astype(jnp.float32)).astype(jnp.bfloat16)
+    sel = onehot.astype(jnp.bfloat16)
+    part = lambda piece: jnp.einsum(spec, piece, sel, preferred_element_type=jnp.float32)
+    return (part(hi) + part(mid)) + part(lo)
 
 
 def step_kernel(
@@ -152,8 +162,8 @@
     both = lax.switch(shift_tiles, [branch(q) for q in range(lon_count)], top_msg)
     source = lax.broadcasted_iota(jnp.int32, (2 * width, width), 0)
     target = lax.broadcasted_iota(jnp.int32, (2 * width, width), 1)
-    pick = (source == width - 1 - target + shift_in).astype(jnp.float32)
-    return exact_dot(both, pick, 2)
+    pick = source == width - 1 - target + shift_in
+    return exact_pick("nmc,cl->nml", both, pick)
 
 
 def per_device(
@@ -206,9 +216,7 @@
     take_last = (slot >= PAD_ROWS - HALO) & (lane == slot + PAD_LANES - PAD_ROWS)
 
     def edges(block):
-        pick = lambda part, sel: jnp.einsum(
-            "nyx,xc->ncy", part, sel.astype(jnp.float32), precision=lax.Precision.HIGHEST
-        )
+        pick = lambda part, sel: exact_pick("nyx,xc->ncy", part, sel)
         return pick(block[..., :PAD_LANES], take_first) + pick(block[..., w - PAD_LANES :], take_last)
 
     wet_edges = edges(land_mask.astype(jnp.float32))
@@ -223,7 +231,7 @@
     halo_slot = lax.broadcasted_iota(jnp.int32, col_msg.shape, 1)
     got_cols = jnp.where(halo_slot < HALO, from_east, from_west)
     place = (take_first | take_last).astype(jnp.float32).T
-    cols5 = jnp.einsum("ncy,cl->nyl", got_cols, place, precision=lax.Precision.HIGHEST)
+    cols5 = exact_pick("ncy,cl->nyl", got_cols, place)
     cols5 = cols5.reshape(fields + 1, levels, h + PAD_ROWS, PAD_LANES)
 
 

time: 104 us -> 130 us (1.25)
  the two profiles are of different devices: /device:TPU:95 before, /device:TPU:1 now
where the time goes in v9:
time: 130 us; the launch traced here: 129 us
  matrix products  33.4 us (26%)
  Pallas kernels  31.7 us (24%)
  starting transfers between devices  30.3 us (23%)
  local copies, waits for them, and re-layouts  12.7 us (10%)
  other arithmetic  10.5 us (8%)
  waiting for transfers between devices  9.07 us (7%)
    pallas_call x1, Pallas kernels, step_call(): pl.pallas_call(step_kernel, grid_spec=pltpu.PrefetchScalarGridSpec(num_sc...  31.7 us
    dot_general x30, matrix products, exact_pick(): jnp.einsum(spec, piece, sel, preferred_element_type=jnp.float32)  29.6 us
    all_to_all x1, starting transfers between devices, per_device(): lax.all_to_all(send, ('lon', 'lat'), split_axis=0, concat_axis=0, tiled=T...  16.5 us
    all_to_all x1, waiting for transfers between devices, per_device(): lax.all_to_all(send, ('lon', 'lat'), split_axis=0, concat_axis=0, tiled=T...  9.05 us
    ppermute x1, starting transfers between devices, per_device(): from_below = lax.ppermute(top_msg, 'lat', up)  5.47 us
    dot_general x2, matrix products, exact_dot(): lax.dot_general(left, right, (((left_dim,), (0,)), ((), ())), precision=l...  3.51 us
    ppermute x1, starting transfers between devices, per_device(): from_above = lax.ppermute(bot_msg, 'lat', down)  3.32 us
  transfers between devices with their start and end apart: 7, of which 1 were waited for; matrix products, arithmetic and copies ran while one was open for 33% of the time, Pallas kernels for 0%

profile of v9, /device:TPU:1, one launch (start us, length us, event | category | flops | bytes accessed | tf_op | source)
XLA Modules:
  0.0 128.9 jit_solution(255254748064855898)
XLA Ops:
  0.0 1.1 slice_convert_fusion.8
  1.1 1.0 fusion.153
  2.1 1.5 %broadcast_multiply_fusion = (f32[4,10,3,512]{3,2,1,0:T(4,128)S(1)}, f32[4,10,3,512]{3,2,1,0:T(4,128)S(1)}, f32[4,10,3,512]{3,2,1,0:T(4,128)S(1)}) fusion(f32[4]{0:T(128)} %constant.148.clone, f32[10,3,512]{2,1,0:T(4,128)S(1)} %get-tuple-element.55, f32[4,10,64,512]{3,2,1,0:T(8,128)} %adj_ref.1, f32[10,3,512]{2,1,0:T(4,128)S(1)} %get-tuple-element.54), kind=kLoop, calls=%fused_computation.110 | loop fusion | flops 184320 | bytes 1351696 | tf_op jit(solution)/shard_map/mul | solution.py:202
  4.5 3.3 %collective-permute-start.16 = (f32[50,3,512]{2,0,1:T(8,128)}, f32[50,3,512]{2,0,1:T(8,128)}, u32[]{:S(2)}, u32[]{:S(2)}) collective-permute-start(f32[50,3,512]{2,0,1:T(8,128)} %pad_maximum_fusion.3), channel_id=1, source_target_pairs={{1,0},{2,1},{3,2},{4,3},{5,4},{6,5},{7,6},{8,7},{9,8},{10,9},{11,1... | collective-permute-start | bytes 921608 | tf_op jit(solution)/shard_map/ppermute | solution.py:200
  8.7 5.5 %collective-permute-start.17 = (f32[50,3,512]{2,0,1:T(8,128)}, f32[50,3,512]{2,0,1:T(8,128)}, u32[]{:S(2)}, u32[]{:S(2)}) collective-permute-start(f32[50,3,512]{2,0,1:T(8,128)} %pad_maximum_fusion.4), channel_id=1, source_target_pairs={{0,1},{1,2},{2,3},{3,4},{4,5},{5,6},{6,7},{7,8},{8,9},{9,10},{10,1... | collective-permute-start | bytes 921608 | tf_op jit(solution)/shard_map/ppermute | solution.py:199
  14.2 1.2 slice.69
  16.4 0.9 fusion.135
  17.3 2.0 %fusion.143 = f32[8,40,64]{2,0,1:T(8,128)S(1)} fusion(s32[8]{0:T(128)S(1)} %iota_add_fusion, pred[8]{0:T(512)(128)(4,1)S(1)} %get-tuple-element.61, f32[40,64,512]{2,1,0:T(8,128)} %bitcast.81), kind=kOutput, calls=%fused_computation.203 | convolution fusion | flops 5244928 | bytes 737320 | tf_op jit(solution)/shard_map/nyx,xc->ncy/dot_general | solution.py:31
  19.4 2.7 %fusion.95 = f32[8,40,64]{2,0,1:T(8,128)} fusion(pred[8]{0:T(512)(128)(4,1)S(1)} %get-tuple-element.62, f32[40,64,512]{2,1,0:T(8,128)} %bitcast.82), kind=kOutput, calls=%fused_computation.165 | convolution fusion | flops 5244928 | bytes 737288 | tf_op jit(solution)/shard_map/nyx,xc->ncy/dot_general | solution.py:31
  24.9 1.0 convolution_add_fusion.5
  26.5 2.0 %convolution_add_fusion.1 = f32[8,40,64]{2,0,1:T(8,128)S(1)} fusion(f32[8,40,64]{2,0,1:T(8,128)S(1)} %fusion.143, f32[40,64,512]{2,1,0:T(8,128)} %bitcast.83, s32[8]{0:T(128)S(1)} %iota_add_fusion, pred[8]{0:T(512)(128)(4,1)S(1)} %get-tuple-element.61), kind=kOutput, calls=%fused_computation.36 | convolution fusion | flops 6576128 | bytes 1474600 | tf_op jit(solution)/shard_map/nyx,xc->ncy/dot_general | solution.py:31
  28.5 2.6 %convolution_add_fusion = f32[8,40,64]{2,0,1:T(8,128)} fusion(f32[8,40,64]{2,0,1:T(8,128)S(1)} %convolution_add_fusion.1, f32[40,64,512]{2,1,0:T(8,128)} %bitcast.84, s32[8]{0:T(128)S(1)} %iota_add_fusion, pred[8]{0:T(512)(128)(4,1)S(1)} %get-tuple-element.61), kind=kOutput, calls=%fused_computation.35 | convolution fusion | flops 7559168 | bytes 1474600 | tf_op jit(solution)/shard_map/nyx,xc->ncy/dot_general | solution.py:31
  31.2 1.9 %convolution_add_fusion.3 = f32[8,40,64]{2,0,1:T(8,128)S(1)} fusion(f32[8,40,64]{2,0,1:T(8,128)S(1)} %copy-done.4, f32[40,64,512]{2,1,0:T(8,128)} %bitcast.85, pred[8]{0:T(512)(128)(4,1)S(1)} %get-tuple-element.62), kind=kOutput, calls=%fused_computation.38 | convolution fusion | flops 6576128 | bytes 1474568 | tf_op jit(solution)/shard_map/nyx,xc->ncy/dot_general | solution.py:31
  33.1 1.1 fusion.33
  35.3 0.9 convolution_add_fusion.10
  36.3 2.7 %fusion.1 = f32[1024,128]{1,0:T(8,128)} fusion(f32[512,128]{1,0:T(8,128)S(1)} %copy-done, s32[512]{0:T(512)S(1)} %bitcast.100), kind=kOutput, calls=%fused_computation.19 | convolution fusion | flops 805830656 | bytes 788480 | tf_op jit(solution)/shard_map/dot_general | solution.py:16
  39.0 1.7 %fusion.25 = f32[10,8,64]{2,1,0:T(8,128)} fusion(f32[8,10,64]{2,0,1:T(8,128)} %convolution_add_fusion.10, f32[8,10,64]{2,0,1:T(8,128)} %convolution_add_fusion.9, f32[10,64,512]{2,1,0:T(8,128)S(1)} %convert_element_type.321, s32[8]{0:T(128)S(1)} %iota_add_fusion, pred[8]{0:T(512)(128)(4,1)S(1)} %get-tuple-element.61), kind=kOutput, calls=%fused_computation.51 | convolution fusion | flops 1896448 | bytes 390144 | tf_op jit(solution)/shard_map/nyx,xc->ncy/dot_general | solution.py:31
  40.6 4.7 %conditional.2 = (f32[50,3,1024]{2,1,0:T(4,128)}, bf16[50,3,1024]{2,1,0:T(4,128)(2,1)S(1)}, f32[50,3,1024]{2,1,0:T(4,128)S(1)}) conditional(s32[]{:T(128)} %clamp.3, f32[50,3,512]{2,1,0:T(4,128)S(1)} %copy-done.6, f32[50,3,512]{2,1,0:T(4,128)S(1)} %copy-done.6, f32[50,3,512]{2,1,0:T(4,128)S(1)} %copy-done.6, ...), branch_computations={%region_1.2_spmd, %region_2.3_spmd, %region_3.4_spmd, %region_4.5_... | conditional | flops 307200 | bytes 5427304
  43.7 1.4 %fusion.150 = (f32[50,3,1024]{2,1,0:T(4,128)S(1)}, bf16[50,3,1024]{2,1,0:T(4,128)(2,1)S(1)}) fusion(f32[50,3,1024]{2,1,0:T(4,128)} %constant_dynamic-update-slice_fusion.10), kind=kLoop, calls=%fused_computation.209 | loop fusion | flops 307200 | bytes 1536000 | tf_op jit(solution)/shard_map/convert_element_type | solution.py:27
  46.1 1.5 %subtract_convert_fusion.2 = (bf16[50,3,1024]{2,1,0:T(4,128)(2,1)S(1)}, bf16[50,3,1024]{2,1,0:T(4,128)(2,1)S(1)}) fusion(f32[50,3,1024]{2,1,0:T(4,128)} %get-tuple-element.24, f32[50,3,1024]{2,1,0:T(4,128)S(1)} %get-tuple-element.25), kind=kLoop, calls=%fused_computation.64 | loop fusion | flops 768000 | bytes 1843200 | tf_op jit(solution)/shard_map/convert_element_type | solution.py:29
  48.6 1.3 %fusion.9 = f32[50,3,512]{2,0,1:T(8,128)} fusion(f32[50,3,512]{2,0,1:T(8,128)S(1)} %fusion.5, s32[512]{0:T(512)S(1)} %copy-done.13, bf16[50,3,1024]{2,1,0:T(4,128)(2,1)S(1)} %copy-done.8), kind=kOutput, calls=%fused_computation.31 | convolution fusion | flops 157887488 | bytes 923648 | tf_op jit(solution)/shard_map/nmc,cl->nml/dot_general | solution.py:31
  49.9 2.0 %fusion.20 = f32[40,8,64]{2,1,0:T(8,128)S(1)} fusion(f32[40,8,64]{2,1,0:T(8,128)S(1)} %bitcast.95, f32[8,40,64]{2,0,1:T(8,128)S(1)} %copy-done.3, f32[8,40,64]{2,0,1:T(8,128)S(1)} %convolution_add_fusion.3, f32[40,64,512]{2,1,0:T(8,128)} %bitcast.86, pred[8]{0:T(512)(128)(4,1)S(1)} %get-tuple-element.62), kind=kOutput, calls=%fused_computation.41 | convolution fusion | flops 7600128 | bytes 1638408 | tf_op jit(solution)/shard_map/nyx,xc->ncy/dot_general | solution.py:31
  53.6 1.5 %fusion.15 = f32[50,3,512]{2,0,1:T(8,128)S(1)} fusion(f32[50,3,512]{2,0,1:T(8,128)} %collective-permute-done.16, f32[50,3,512]{2,0,1:T(8,128)S(1)} %copy-done.17, s32[512]{0:T(512)S(1)} %copy-done.13, bf16[50,3,1024]{2,1,0:T(4,128)(2,1)S(1)} %get-tuple-element.52, pred[]{:T(512)S(6)} %eq.116), kind=kOutput, calls=%fused_computation.33 | convolution fusion | flops 157964288 | bytes 1230849 | tf_op jit(solution)/shard_map/nmc,cl->nml/dot_general | solution.py:31
  55.1 1.1 pad_maximum_fusion
  58.0 1.3 collective-permute-start.19
  59.3 2.4 %collective-permute-start.18 = (f32[50,8,72]{2,1,0:T(8,128)S(1)}, f32[50,8,72]{2,1,0:T(8,128)S(1)}, u32[]{:S(2)}, u32[]{:S(2)}) collective-permute-start(f32[50,8,72]{2,1,0:T(8,128)S(1)} %pad_maximum_fusion.5), channel_id=1, source_target_pairs={{0,112},{16,0},{32,16},{48,32},{64,48},{80,64},{96,80},{112,96},{1... | collective-permute-start | bytes 345608 | tf_op jit(solution)/shard_map/ppermute | solution.py:229
  61.7 1.2 all_to_all.8
  62.9 16.5 %all-to-all-start = ((f32[128,1,1152]{2,1,0:T(1,128)}), f32[128,1,1152]{2,1,0:T(1,128)S(1)}, u32[]{:S(2)}, u32[]{:S(2)}) async-start(f32[128,1,1152]{2,1,0:T(1,128)} %all_to_all.8), calls=%async_computation | async-start | bytes 1179648 | tf_op jit(solution)/shard_map/all_to_all | solution.py:260
  80.1 1.4 %copy.86 = f32[50,8,512]{2,1,0:T(8,128)} copy(f32[50,8,512]{2,0,1:T(8,128)S(1)} %pad_maximum_fusion) | data formatting | bytes 1638400 | tf_op jit(solution)/shard_map/concatenate | solution.py:210
  82.6 1.8 %add_add_fusion = f32[50,72,128]{2,1,0:T(8,128)} fusion(f32[50,72,128]{2,1,0:T(8,128)S(1)} %fusion.51, f32[50,72,128]{2,1,0:T(8,128)S(1)} %fusion.53, f32[50,8,72]{2,1,0:T(8,128)S(1)} %broadcast_select_fusion, s32[8]{0:T(128)S(1)} %iota_add_fusion, pred[8]{0:T(512)(128)(4,1)S(1)} %get-tuple-element.61, pred[8]{0:T(512)(128)(4,1)S(1)} %get-tuple-element.62), kind=kOutput, calls=%fused_computation.24 | convolution fusion | flops 8503168 | bytes 5644848 | tf_op jit(solution)/shard_map/ncy,cl->nyl/dot_general | solution.py:31
  84.5 9.1 %all-to-all-done = f32[128,1,1152]{2,1,0:T(1,128)S(1)} async-done(((f32[128,1,1152]{2,1,0:T(1,128)}), f32[128,1,1152]{2,1,0:T(1,128)S(1)}, u32[]{:S(2)}, u32[]{:S(2)}) %all-to-all-start) | async-done | bytes 589856 | tf_op jit(solution)/shard_map/all_to_all | solution.py:260
  97.2 31.7 %shard_map.109 = f32[4,10,64,512]{3,2,1,0:T(8,128)} custom-call(s32[6,1040]{1,0:T(8,128)} %pad.17.where_ref, f32[1040]{0:T(1024)} %pad.18.weight_ref, f32[4,10,64,512]{3,2,1,0:T(8,128)} %adj_ref.1, s32[10,64,512]{2,1,0:T(8,128)} %mask_ref.1, f32[10,64,512]{2,1,0:T(8,128)} %diff_ref.1, f32[5,10,8,512]{3,2,1,0:T(8,128)} %bitcast.89, ...), custom_call_target="tpu_custom_call" | custom-call | tf_op jit(solution)/shard_map/pallas_call | solution.py:111
  (109 shorter events, 20.1 us)
Async XLA Ops:
  0.0 36.3 %copy-start = (f32[512,128]{1,0:T(8,128)S(1)}, f32[512,128]{1,0:T(8,128)}, u32[]{:S(2)}) copy-start(f32[512,128]{1,0:T(8,128)} %param.24) | copy-start | bytes 786436
  3.7 12.4 %copy-start.1 = (f32[10,64,512]{2,1,0:T(8,128)S(1)}, f32[10,64,512]{2,1,0:T(8,128)}, u32[]{:S(2)}) copy-start(f32[10,64,512]{2,1,0:T(8,128)} %diff_ref.1) | copy-start | bytes 3932164
  4.5 49.0 %collective-permute-start.16 = (f32[50,3,512]{2,0,1:T(8,128)}, f32[50,3,512]{2,0,1:T(8,128)}, u32[]{:S(2)}, u32[]{:S(2)}) collective-permute-start(f32[50,3,512]{2,0,1:T(8,128)} %pad_maximum_fusion.3), channel_id=1, source_target_pairs={{1,0},{2,1},{3,2},{4,3},{5,4},{6,5},{7,6},{8,7},{9,8},{10,9},{11,1... | collective-permute-start | bytes 921608 | tf_op jit(solution)/shard_map/ppermute | solution.py:200
  8.7 46.4 %collective-permute-start.17 = (f32[50,3,512]{2,0,1:T(8,128)}, f32[50,3,512]{2,0,1:T(8,128)}, u32[]{:S(2)}, u32[]{:S(2)}) collective-permute-start(f32[50,3,512]{2,0,1:T(8,128)} %pad_maximum_fusion.4), channel_id=1, source_target_pairs={{0,1},{1,2},{2,3},{3,4},{4,5},{5,6},{6,7},{7,8},{8,9},{9,10},{10,1... | collective-permute-start | bytes 921608 | tf_op jit(solution)/shard_map/ppermute | solution.py:199
  17.3 4.7 %copy-start.2 = (s32[10,64,512]{2,1,0:T(8,128)S(1)}, s32[10,64,512]{2,1,0:T(8,128)}, u32[]{:S(2)}) copy-start(s32[10,64,512]{2,1,0:T(8,128)} %mask_ref.1) | copy-start | bytes 3932164
  22.0 2.5 %copy-start.12 = (s32[512,1]{0,1:T(1,128)S(1)}, s32[512,1]{0,1:T(1,128)}, u32[]{:S(2)}) copy-start(s32[512,1]{0,1:T(1,128)} %param.26) | copy-start | bytes 6148
  26.5 4.7 %copy-start.4 = (f32[8,40,64]{2,0,1:T(8,128)S(1)}, f32[8,40,64]{2,0,1:T(8,128)}, u32[]{:S(2)}) copy-start(f32[8,40,64]{2,0,1:T(8,128)} %fusion.95) | copy-start | bytes 245764
  31.2 3.0 %copy-start.11 = (f32[8,10,64]{2,0,1:T(8,128)S(1)}, f32[8,10,64]{2,0,1:T(8,128)}, u32[]{:S(2)}) copy-start(f32[8,10,64]{2,0,1:T(8,128)} %fusion.139) | copy-start | bytes 61444
  31.2 3.9 %copy-start.10 = (f32[8,10,64]{2,0,1:T(8,128)S(1)}, f32[8,10,64]{2,0,1:T(8,128)}, u32[]{:S(2)}) copy-start(f32[8,10,64]{2,0,1:T(8,128)} %fusion.91) | copy-start | bytes 61444
  34.2 4.8 %copy-start.6 = (f32[50,3,512]{2,1,0:T(4,128)S(1)}, f32[50,3,512]{2,1,0:T(4,128)}, u32[]{:S(2)}) copy-start(f32[50,3,512]{2,1,0:T(4,128)} %fusion.33) | copy-start | bytes 921604
  40.6 1.4 %collective-permute-start.10 = (f32[50,3,512]{2,1,0:T(4,128)S(1)}, f32[50,3,512]{2,1,0:T(4,128)S(1)}, u32[]{:S(2)}, u32[]{:S(2)}) collective-permute-start(f32[50,3,512]{2,1,0:T(4,128)S(1)} %param.5), channel_id=1, source_target_pairs={{79,15},{63,31},{47,47},{31,63},{15,79},{127,95},{111,111},{95,127}} | collective-permute-start | bytes 921608 | tf_op jit(solution)/shard_map/cond/branch_5_fun/ppermute | solution.py:156
  41.3 1.5 %collective-permute-start.11 = (f32[50,3,512]{2,1,0:T(4,128)S(1)}, f32[50,3,512]{2,1,0:T(4,128)S(1)}, u32[]{:S(2)}, u32[]{:S(2)}) collective-permute-start(f32[50,3,512]{2,1,0:T(4,128)S(1)} %param.5), channel_id=1, source_target_pairs={{95,15},{79,31},{63,47},{47,63},{31,79},{15,95},{127,111},{111,127}} | collective-permute-start | bytes 921608 | tf_op jit(solution)/shard_map/cond/branch_5_fun/ppermute | solution.py:157
  45.3 0.8 copy-start.7
  45.3 2.3 %copy-start.13 = (s32[512]{0:T(512)S(1)}, s32[512]{0:T(512)}, u32[]{:S(2)}) copy-start(s32[512]{0:T(512)} %subtract_add_fusion) | copy-start | bytes 6148
  47.6 1.0 copy-start.8
  47.6 2.3 %copy-start.9 = (f32[10,8,64]{2,1,0:T(8,128)S(1)}, f32[10,8,64]{2,1,0:T(8,128)}, u32[]{:S(2)}) copy-start(f32[10,8,64]{2,1,0:T(8,128)} %fusion.25) | copy-start | bytes 61444
  47.6 2.3 %copy-start.3 = (f32[8,40,64]{2,0,1:T(8,128)S(1)}, f32[8,40,64]{2,0,1:T(8,128)}, u32[]{:S(2)}) copy-start(f32[8,40,64]{2,0,1:T(8,128)} %convolution_add_fusion) | copy-start | bytes 245764
  49.9 2.3 %copy-start.14 = (s32[512]{0:T(512)S(1)}, s32[512]{0:T(512)}, u32[]{:S(2)}) copy-start(s32[512]{0:T(512)} %param.27) | copy-start | bytes 6148
  49.9 2.4 %copy-start.16 = (f32[512]{0:T(512)S(1)}, f32[512]{0:T(512)}, u32[]{:S(2)}) copy-start(f32[512]{0:T(512)} %param.25) | copy-start | bytes 6148
  49.9 3.5 %copy-start.5 = (f32[1024,128]{1,0:T(8,128)S(1)}, f32[1024,128]{1,0:T(8,128)}, u32[]{:S(2)}) copy-start(f32[1024,128]{1,0:T(8,128)} %fusion.1) | copy-start | bytes 1572868
  52.2 1.4 %copy-start.17 = (f32[50,3,512]{2,0,1:T(8,128)S(1)}, f32[50,3,512]{2,0,1:T(8,128)}, u32[]{:S(2)}) copy-start(f32[50,3,512]{2,0,1:T(8,128)} %fusion.9) | copy-start | bytes 921604
  58.0 23.5 %collective-permute-start.19 = (f32[50,8,72]{2,1,0:T(8,128)S(1)}, f32[50,8,72]{2,1,0:T(8,128)S(1)}, u32[]{:S(2)}, u32[]{:S(2)}) collective-permute-start(f32[50,8,72]{2,1,0:T(8,128)S(1)} %pad_maximum_fusion.5), channel_id=1, source_target_pairs={{0,16},{16,32},{32,48},{48,64},{64,80},{80,96},{96,112},{112,0},{1... | collective-permute-start | bytes 345608 | tf_op jit(solution)/shard_map/ppermute | solution.py:230
  59.3 22.2 %collective-permute-start.18 = (f32[50,8,72]{2,1,0:T(8,128)S(1)}, f32[50,8,72]{2,1,0:T(8,128)S(1)}, u32[]{:S(2)}, u32[]{:S(2)}) collective-permute-start(f32[50,8,72]{2,1,0:T(8,128)S(1)} %pad_maximum_fusion.5), channel_id=1, source_target_pairs={{0,112},{16,0},{32,16},{48,32},{64,48},{80,64},{96,80},{112,96},{1... | collective-permute-start | bytes 345608 | tf_op jit(solution)/shard_map/ppermute | solution.py:229
  61.7 17.7 %copy-start.15 = (f32[64]{0:T(128)S(1)}, f32[64]{0:T(128)}, u32[]{:S(2)}) copy-start(f32[64]{0:T(128)} %param.23) | copy-start | bytes 772
  62.9 30.6 %all-to-all-start = ((f32[128,1,1152]{2,1,0:T(1,128)}), f32[128,1,1152]{2,1,0:T(1,128)S(1)}, u32[]{:S(2)}, u32[]{:S(2)}) async-start(f32[128,1,1152]{2,1,0:T(1,128)} %all_to_all.8), calls=%async_computation | async-start | bytes 1179648 | tf_op jit(solution)/shard_map/all_to_all | solution.py:260

commit v10 on v8

--- a/solution.py
+++ b/solution.py
@@ -211,10 +211,21 @@
         )
         return pick(block[..., :PAD_LANES], take_first) + pick(block[..., w - PAD_LANES :], take_last)
 
-    wet_edges = edges(land_mask.astype(jnp.float32))
-    adj_edges = edges(adjoint.reshape(n_work, h, w)).reshape(fields, levels, PAD_ROWS, h)
-    work_edges = (adj_edges * wet_edges[None]).reshape(n_work, PAD_ROWS, h)
-    interior = jnp.concatenate([work_edges, edges(diffusivity)], axis=0)
+    def end_tiles(lanes):
+        work = adjoint[..., lanes] * land_mask[None, ..., lanes].astype(jnp.float32)
+        return jnp.concatenate([work.reshape(n_work, h, PAD_LANES), diffusivity[..., lanes]], axis=0)
+
+    interior = jnp.einsum(
+        "nyx,xc->ncy",
+        end_tiles(slice(0, PAD_LANES)),
+        take_first.astype(jnp.float32),
+        precision=lax.Precision.HIGHEST,
+    ) + jnp.einsum(
+        "nyx,xc->ncy",
+        end_tiles(slice(w - PAD_LANES, w)),
+        take_last.astype(jnp.float32),
+        precision=lax.Precision.HIGHEST,
+    )
     col_msg = jnp.concatenate([interior, edges(rows_all)], axis=2)
     ring_west = [(i, (i - 1) % lon_count) for i in range(lon_count)]
     ring_east = [(i, (i + 1) % lon_count) for i in range(lon_count)]

time: 104 us -> 105 us (level)
  matrix products: 17.2 us -> 13.3 us
  other arithmetic: 7.42 us -> 11.1 us
    dot_general x8 -> x2, matrix products: 8.84 us -> 0.84 us  [edges(): jnp.einsum('nyx,xc->ncy', part, sel.astype(jnp.float32), precision=lax.Pr...]
    dot_general x0 -> x2, matrix products: none -> 4.07 us  [the longest x1 2.04 us: per_device(): jnp.einsum('nyx,xc->ncy', end_tiles(slice(w - PAD_LANES, w)), take_last.a...]
    ppermute x1, waiting for transfers between devices: 7.45 us -> 10.3 us  [run(): got_a = lax.ppermute(msg, ('lon', 'lat'), pairs_a)]
    ppermute x1, waiting for transfers between devices: 2.57 us -> 0.01 us  [run(): got_b = lax.ppermute(msg, ('lon', 'lat'), pairs_b)]
    mul x0 -> x1, other arithmetic: none -> 2.07 us  [end_tiles(): work = adjoint[..., lanes] * land_mask[None, ..., lanes].astype(jnp.float32)]
    ppermute x1, starting transfers between devices: 1.2 us -> 3.07 us  [per_device(): from_west = lax.ppermute(col_msg, 'lon', ring_east)]
    ppermute x1, starting transfers between devices: 2.46 us -> 0.68 us  [run(): got_b = lax.ppermute(msg, ('lon', 'lat'), pairs_b)]
    ppermute x1, starting transfers between devices: 3.64 us -> 4.81 us  [run(): got_a = lax.ppermute(msg, ('lon', 'lat'), pairs_a)]
  transfers between devices with their start and end apart: 7 -> 7, of which waited for: 4 -> 3; matrix products, arithmetic and copies ran while one was open for 22% -> 22% of each run, Pallas kernels for 0% -> 0%
where the time goes in v10:
time: 105 us
  Pallas kernels  31.7 us (30%)
  starting transfers between devices  23 us (22%)
  waiting for transfers between devices  14.9 us (14%)
  matrix products  13.3 us (13%)
  other arithmetic  11.1 us (11%)
  local copies, waits for them, and re-layouts  10.2 us (10%)
  between operations  1.09 us (1%)
    pallas_call x1, Pallas kernels, step_call(): pl.pallas_call(step_kernel, grid_spec=pltpu.PrefetchScalarGridSpec(num_sc...  31.7 us
    ppermute x1, waiting for transfers between devices, run(): got_a = lax.ppermute(msg, ('lon', 'lat'), pairs_a)  10.3 us
    all_to_all x1, starting transfers between devices, per_device(): lax.all_to_all(send, ('lon', 'lat'), split_axis=0, concat_axis=0, tiled=T...  10.2 us
    ppermute x1, starting transfers between devices, run(): got_a = lax.ppermute(msg, ('lon', 'lat'), pairs_a)  4.81 us
    dot_general x3, matrix products, exact_dot(): lax.dot_general(left, right, (((left_dim,), (0,)), ((), ())), precision=l...  4.35 us
    ppermute x1, waiting for transfers between devices, per_device(): from_east = lax.ppermute(col_msg, 'lon', ring_west)  4.01 us
    ppermute x1, starting transfers between devices, per_device(): from_west = lax.ppermute(col_msg, 'lon', ring_east)  3.07 us
    ppermute x1, starting transfers between devices, per_device(): from_above = lax.ppermute(bot_msg, 'lat', down)  3 us
  transfers between devices with their start and end apart: 7, of which 3 were waited for; matrix products, arithmetic and copies ran while one was open for 22% of the time, Pallas kernels for 0%

profile of v10, /device:TPU:95, one launch (start us, length us, event | category | flops | bytes accessed | tf_op | source)
XLA Modules:
  0.0 105.5 jit_solution(2992412890734992183)
XLA Ops:
  0.0 0.7 convert_element_type.87
  0.7 1.1 %fusion.22 = f32[512]{0:T(512)S(1)} fusion(s32[512]{0:T(512)} %bitcast.61), kind=kOutput, calls=%fused_computation.28 | convolution fusion | flops 67763712 | bytes 4096 | tf_op jit(solution)/shard_map/dot_general | solution.py:250
  1.8 0.7 multiply_add_fusion
  2.5 1.5 %fusion = f32[1024,2]{0,1:T(2,128)S(1)} fusion(s32[512]{0:T(512)S(1)} %bitcast.62, f32[512,1]{0,1:T(1,128)S(1)} %bitcast.64, f32[512,1]{0,1:T(1,128)} %bitcast.66), kind=kOutput, calls=%fused_computation.10 | convolution fusion | flops 13108224 | bytes 14336 | tf_op jit(solution)/shard_map/dot_general | solution.py:16
  4.3 1.9 %fusion.1 = f32[1024,128]{1,0:T(8,128)S(1)} fusion(f32[512,128]{1,0:T(8,128)S(1)} %copy-done, s32[512]{0:T(512)S(1)} %bitcast.63), kind=kOutput, calls=%fused_computation.11 | convolution fusion | flops 805830656 | bytes 788480 | tf_op jit(solution)/shard_map/dot_general | solution.py:16
  6.4 1.2 %all_to_all.8 = f32[128,1,1152]{2,1,0:T(1,128)} reshape(f32[128,1152]{1,0:T(8,128)S(1)} %select_maximum_fusion) | data formatting | bytes 1179648 | tf_op jit(solution)/shard_map/all_to_all | solution.py:263
  7.6 10.2 %all-to-all-start = ((f32[128,1,1152]{2,1,0:T(1,128)}), f32[128,1,1152]{2,1,0:T(1,128)S(1)}, u32[]{:S(2)}, u32[]{:S(2)}) async-start(f32[128,1,1152]{2,1,0:T(1,128)} %all_to_all.8), calls=%async_computation | async-start | bytes 1179648 | tf_op jit(solution)/shard_map/all_to_all | solution.py:263
  17.9 2.3 %broadcast_multiply_fusion = (f32[4,10,3,512]{3,2,1,0:T(4,128)}, f32[4,10,3,512]{3,2,1,0:T(4,128)S(1)}, f32[4,10,3,512]{3,2,1,0:T(4,128)S(1)}) fusion(f32[4]{0:T(128)} %constant.148.clone, f32[10,3,512]{2,1,0:T(4,128)S(1)} %get-tuple-element.40, f32[4,10,64,512]{3,2,1,0:T(8,128)} %adj_ref.1, f32[10,3,512]{2,1,0:T(4,128)S(1)} %get-tuple-element.39), kind=kLoop, calls=%fused_computation.59 | loop fusion | flops 184320 | bytes 1351696 | tf_op jit(solution)/shard_map/mul | solution.py:192
  20.3 0.8 pad_maximum_fusion.11
  21.1 3.0 %collective-permute-start.16 = (f32[50,3,512]{2,0,1:T(8,128)}, f32[50,3,512]{2,0,1:T(8,128)}, u32[]{:S(2)}, u32[]{:S(2)}) collective-permute-start(f32[50,3,512]{2,0,1:T(8,128)} %pad_maximum_fusion.11), channel_id=1, source_target_pairs={{1,0},{2,1},{3,2},{4,3},{5,4},{6,5},{7,6},{8,7},{9,8},{10,9},{11,1... | collective-permute-start | bytes 921608 | tf_op jit(solution)/shard_map/ppermute | solution.py:190
  24.2 0.8 pad_maximum_fusion.12
  24.9 1.3 %collective-permute-start.17 = (f32[50,3,512]{2,0,1:T(8,128)}, f32[50,3,512]{2,0,1:T(8,128)}, u32[]{:S(2)}, u32[]{:S(2)}) collective-permute-start(f32[50,3,512]{2,0,1:T(8,128)} %pad_maximum_fusion.12), channel_id=1, source_target_pairs={{0,1},{1,2},{2,3},{3,4},{4,5},{5,6},{6,7},{7,8},{8,9},{9,10},{10,1... | collective-permute-start | bytes 921608 | tf_op jit(solution)/shard_map/ppermute | solution.py:189
  26.2 1.2 %slice.69 = s32[1]{0:T(128)} slice(s32[512]{0:T(512)} %param.28), slice={[0:1]} | slice | bytes 8 | tf_op jit(solution)/shard_map/slice | solution.py:133
  29.7 0.9 fusion.68
  31.0 2.1 %slice_multiply_fusion = (f32[4,10,64,128]{3,2,1,0:T(8,128)S(1)}, f32[4,10,64,128]{3,2,1,0:T(8,128)S(1)}) fusion(f32[4,10,64,512]{3,2,1,0:T(8,128)} %adj_ref.1, f32[10,64,128]{2,1,0:T(8,128)S(1)} %get-tuple-element.35, f32[10,64,128]{2,1,0:T(8,128)S(1)} %get-tuple-element.36), kind=kLoop, calls=%fused_computation.22 | loop fusion | flops 655360 | bytes 5898240 | tf_op jit(solution)/shard_map/mul | solution.py:215
  33.2 2.0 %fusion.5 = f32[8,50,64]{2,0,1:T(8,128)S(1)} fusion(f32[10,64,128]{2,1,0:T(8,128)S(1)} %copy-done.5, f32[40,64,128]{2,1,0:T(8,128)S(1)} %bitcast.51, pred[8]{0:T(512)(128)(4,1)S(1)} %copy-done.6), kind=kOutput, calls=%fused_computation.14 | convolution fusion | flops 39733248 | bytes 1740808 | tf_op jit(solution)/shard_map/nyx,xc->ncy/dot_general | solution.py:218
  35.2 2.0 %fusion.19 = f32[50,8,64]{2,1,0:T(8,128)S(1)} fusion(f32[8,50,64]{2,0,1:T(8,128)S(1)} %fusion.5, f32[10,64,128]{2,1,0:T(8,128)S(1)} %copy-done.3, f32[40,64,128]{2,1,0:T(8,128)S(1)} %bitcast.49, s32[8]{0:T(128)S(1)} %copy-done.8, pred[8]{0:T(512)(128)(4,1)S(1)} %copy-done.7), kind=kOutput, calls=%fused_computation.27 | convolution fusion | flops 39758848 | bytes 1843240 | tf_op jit(solution)/shard_map/nyx,xc->ncy/dot_general | solution.py:223
  37.4 16.6 %conditional.1 = (f32[50,3,1024]{2,0,1:T(8,128)S(1)}) conditional(s32[]{:T(128)} %clamp.3, f32[50,3,512]{2,1,0:T(4,128)S(1)} %fusion.26, f32[50,3,512]{2,1,0:T(4,128)S(1)} %fusion.26, f32[50,3,512]{2,1,0:T(4,128)S(1)} %fusion.26, f32[50,3,512]{2,1,0:T(4,128)S(1)} %fusion.26, f32[50,3,512]{2,1,0:T(4,128)S(1)} %fusion.26, ...), branch_computations={%region_1.2_spmd, %region_2.3_spmd, %region_3.4_spmd, %region_4.5_... | conditional | flops 153600 | bytes 4915288 | solution.py:152
  37.4 0.7 collective-permute-start.13
  38.1 4.8 %collective-permute-start.12 = (f32[50,3,512]{2,1,0:T(4,128)S(1)}, f32[50,3,512]{2,1,0:T(4,128)S(1)}, u32[]{:S(2)}, u32[]{:S(2)}) collective-permute-start(f32[50,3,512]{2,1,0:T(4,128)S(1)} %param.6), channel_id=1, source_target_pairs={{95,15},{79,31},{63,47},{47,63},{31,79},{15,95},{127,111},{111,127}} | collective-permute-start | bytes 921608 | tf_op jit(solution)/shard_map/cond/branch_6_fun/ppermute | solution.py:146
  42.9 10.3 %collective-permute-done.12 = f32[50,3,512]{2,1,0:T(4,128)S(1)} collective-permute-done((f32[50,3,512]{2,1,0:T(4,128)S(1)}, f32[50,3,512]{2,1,0:T(4,128)S(1)}, u32[]{:S(2)}, u32[]{:S(2)}) %collective-permute-start.12) | collective-permute-done | bytes 307232 | tf_op jit(solution)/shard_map/cond/branch_6_fun/ppermute | solution.py:146
  54.0 1.0 fusion.13
  55.0 1.1 %pad_maximum_fusion.8 = f32[50,8,512]{2,0,1:T(8,128)S(1)} fusion(f32[50,3,512]{2,0,1:T(8,128)} %collective-permute-done.17, f32[50,3,512]{2,0,1:T(8,128)S(1)} %fusion.13, f32[8]{0:T(128)S(1)} %pad.43.clone), kind=kLoop, calls=%fused_computation.33 | loop fusion | flops 409600 | bytes 1433632 | tf_op jit(solution)/shard_map/concatenate | solution.py:200
  57.3 3.1 %collective-permute-start.19 = (f32[50,8,72]{2,1,0:T(8,128)S(1)}, f32[50,8,72]{2,1,0:T(8,128)S(1)}, u32[]{:S(2)}, u32[]{:S(2)}) collective-permute-start(f32[50,8,72]{2,1,0:T(8,128)S(1)} %pad_maximum_fusion.13), channel_id=1, source_target_pairs={{0,16},{16,32},{32,48},{48,64},{64,80},{80,96},{96,112},{112,0},{1... | collective-permute-start | bytes 345608 | tf_op jit(solution)/shard_map/ppermute | solution.py:233
  60.3 0.7 copy.71.cor_ref
  61.0 1.4 %copy.66 = f32[50,8,512]{2,1,0:T(8,128)} copy(f32[50,8,512]{2,0,1:T(8,128)S(1)} %pad_maximum_fusion.8) | data formatting | bytes 1638400 | tf_op jit(solution)/shard_map/concatenate | solution.py:200
  62.4 0.6 collective-permute-done.19
  63.0 4.0 %collective-permute-done.18 = f32[50,8,72]{2,1,0:T(8,128)S(1)} collective-permute-done((f32[50,8,72]{2,1,0:T(8,128)S(1)}, f32[50,8,72]{2,1,0:T(8,128)S(1)}, u32[]{:S(2)}, u32[]{:S(2)}) %collective-permute-start.18) | collective-permute-done | bytes 115232 | tf_op jit(solution)/shard_map/ppermute | solution.py:232
  67.1 3.0 %fusion.34 = f32[50,72,128]{2,1,0:T(8,128)} fusion(f32[50,8,72]{2,1,0:T(8,128)S(1)} %collective-permute-done.18, f32[50,8,72]{2,1,0:T(8,128)S(1)} %collective-permute-done.19, pred[8]{0:T(512)(128)(4,1)S(1)} %copy-done.6, s32[8]{0:T(128)S(1)} %copy-done.8, pred[8]{0:T(512)(128)(4,1)S(1)} %copy-done.7), kind=kOutput, calls=%fused_computation.57 | convolution fusion | flops 44270720 | bytes 2073648 | tf_op jit(solution)/shard_map/ncy,cl->nyl/dot_general | solution.py:237
  70.0 0.7 copy.57
  71.1 0.9 pad.19.vals_ref
  73.7 31.7 %shard_map.109 = f32[4,10,64,512]{3,2,1,0:T(8,128)} custom-call(s32[6,1040]{1,0:T(8,128)} %pad.17.where_ref, f32[1040]{0:T(1024)} %pad.18.weight_ref, f32[4,10,64,512]{3,2,1,0:T(8,128)} %adj_ref.1, s32[10,64,512]{2,1,0:T(8,128)} %mask_ref.1, f32[10,64,512]{2,1,0:T(8,128)} %diff_ref.1, f32[5,10,8,512]{3,2,1,0:T(8,128)} %bitcast.52, ...), custom_call_target="tpu_custom_call" | custom-call | tf_op jit(solution)/shard_map/pallas_call | solution.py:101
  (68 shorter events, 6.7 us)
Async XLA Ops:
  0.0 4.3 %copy-start = (f32[512,128]{1,0:T(8,128)S(1)}, f32[512,128]{1,0:T(8,128)}, u32[]{:S(2)}) copy-start(f32[512,128]{1,0:T(8,128)} %param.24) | copy-start | bytes 786436
  6.3 11.5 %copy-start.2 = (f32[10,64,512]{2,1,0:T(8,128)S(1)}, f32[10,64,512]{2,1,0:T(8,128)}, u32[]{:S(2)}) copy-start(f32[10,64,512]{2,1,0:T(8,128)} %diff_ref.1) | copy-start | bytes 3932164
  6.4 11.5 %copy-start.1 = (s32[10,64,512]{2,1,0:T(8,128)S(1)}, s32[10,64,512]{2,1,0:T(8,128)}, u32[]{:S(2)}) copy-start(s32[10,64,512]{2,1,0:T(8,128)} %mask_ref.1) | copy-start | bytes 3932164
  7.6 62.4 %all-to-all-start = ((f32[128,1,1152]{2,1,0:T(1,128)}), f32[128,1,1152]{2,1,0:T(1,128)S(1)}, u32[]{:S(2)}, u32[]{:S(2)}) async-start(f32[128,1,1152]{2,1,0:T(1,128)} %all_to_all.8), calls=%async_computation | async-start | bytes 1179648 | tf_op jit(solution)/shard_map/all_to_all | solution.py:263
  21.1 32.9 %collective-permute-start.16 = (f32[50,3,512]{2,0,1:T(8,128)}, f32[50,3,512]{2,0,1:T(8,128)}, u32[]{:S(2)}, u32[]{:S(2)}) collective-permute-start(f32[50,3,512]{2,0,1:T(8,128)} %pad_maximum_fusion.11), channel_id=1, source_target_pairs={{1,0},{2,1},{3,2},{4,3},{5,4},{6,5},{7,6},{8,7},{9,8},{10,9},{11,1... | collective-permute-start | bytes 921608 | tf_op jit(solution)/shard_map/ppermute | solution.py:190
  24.9 30.0 %collective-permute-start.17 = (f32[50,3,512]{2,0,1:T(8,128)}, f32[50,3,512]{2,0,1:T(8,128)}, u32[]{:S(2)}, u32[]{:S(2)}) collective-permute-start(f32[50,3,512]{2,0,1:T(8,128)} %pad_maximum_fusion.12), channel_id=1, source_target_pairs={{0,1},{1,2},{2,3},{3,4},{4,5},{5,6},{6,7},{7,8},{8,9},{9,10},{10,1... | collective-permute-start | bytes 921608 | tf_op jit(solution)/shard_map/ppermute | solution.py:189
  28.1 2.6 %copy-start.4 = (f32[4,10,3,512]{3,2,1,0:T(4,128)S(1)}, f32[4,10,3,512]{3,2,1,0:T(4,128)}, u32[]{:S(2)}) copy-start(f32[4,10,3,512]{3,2,1,0:T(4,128)} %get-tuple-element.23) | copy-start | bytes 737284
  31.0 2.1 %copy-start.5 = (f32[10,64,128]{2,1,0:T(8,128)S(1)}, f32[10,64,128]{2,1,0:T(8,128)}, u32[]{:S(2)}) copy-start(f32[10,64,128]{2,1,0:T(8,128)} %get-tuple-element.38) | copy-start | bytes 983044
  31.0 2.1 %copy-start.6 = (pred[8]{0:T(512)(128)(4,1)S(1)}, pred[8]{0:T(512)(128)(4,1)}, u32[]{:S(2)}) copy-start(pred[8]{0:T(512)(128)(4,1)} %iota_compare_fusion.14) | copy-start | bytes 28
  33.1 2.1 %copy-start.3 = (f32[10,64,128]{2,1,0:T(8,128)S(1)}, f32[10,64,128]{2,1,0:T(8,128)}, u32[]{:S(2)}) copy-start(f32[10,64,128]{2,1,0:T(8,128)} %get-tuple-element.37) | copy-start | bytes 983044
  33.1 2.1 %copy-start.7 = (pred[8]{0:T(512)(128)(4,1)S(1)}, pred[8]{0:T(512)(128)(4,1)}, u32[]{:S(2)}) copy-start(pred[8]{0:T(512)(128)(4,1)} %iota_compare_fusion.13) | copy-start | bytes 28
  33.1 2.1 %copy-start.8 = (s32[8]{0:T(128)S(1)}, s32[8]{0:T(128)}, u32[]{:S(2)}) copy-start(s32[8]{0:T(128)} %iota_add_fusion) | copy-start | bytes 100
  37.4 5.5 %collective-permute-start.13 = (f32[50,3,512]{2,1,0:T(4,128)S(1)}, f32[50,3,512]{2,1,0:T(4,128)S(1)}, u32[]{:S(2)}, u32[]{:S(2)}) collective-permute-start(f32[50,3,512]{2,1,0:T(4,128)S(1)} %param.6), channel_id=1, source_target_pairs={{111,15},{95,31},{79,47},{63,63},{47,79},{31,95},{15,111},{127,127}} | collective-permute-start | bytes 921608 | tf_op jit(solution)/shard_map/cond/branch_6_fun/ppermute | solution.py:147
  38.1 15.1 %collective-permute-start.12 = (f32[50,3,512]{2,1,0:T(4,128)S(1)}, f32[50,3,512]{2,1,0:T(4,128)S(1)}, u32[]{:S(2)}, u32[]{:S(2)}) collective-permute-start(f32[50,3,512]{2,1,0:T(4,128)S(1)} %param.6), channel_id=1, source_target_pairs={{95,15},{79,31},{63,47},{47,63},{31,79},{15,95},{127,111},{111,127}} | collective-permute-start | bytes 921608 | tf_op jit(solution)/shard_map/cond/branch_6_fun/ppermute | solution.py:146
  54.9 5.4 %copy-start.9 = (f32[64]{0:T(128)S(1)}, f32[64]{0:T(128)}, u32[]{:S(2)}) copy-start(f32[64]{0:T(128)} %param.23) | copy-start | bytes 772
  57.3 5.8 %collective-permute-start.19 = (f32[50,8,72]{2,1,0:T(8,128)S(1)}, f32[50,8,72]{2,1,0:T(8,128)S(1)}, u32[]{:S(2)}, u32[]{:S(2)}) collective-permute-start(f32[50,8,72]{2,1,0:T(8,128)S(1)} %pad_maximum_fusion.13), channel_id=1, source_target_pairs={{0,16},{16,32},{32,48},{48,64},{64,80},{80,96},{96,112},{112,0},{1... | collective-permute-start | bytes 345608 | tf_op jit(solution)/shard_map/ppermute | solution.py:233
  60.3 6.7 %collective-permute-start.18 = (f32[50,8,72]{2,1,0:T(8,128)S(1)}, f32[50,8,72]{2,1,0:T(8,128)S(1)}, u32[]{:S(2)}, u32[]{:S(2)}) collective-permute-start(f32[50,8,72]{2,1,0:T(8,128)S(1)} %pad_maximum_fusion.13), channel_id=1, source_target_pairs={{0,112},{16,0},{32,16},{48,32},{64,48},{80,64},{96,80},{112,96},{1... | collective-permute-start | bytes 345608 | tf_op jit(solution)/shard_map/ppermute | solution.py:232

commit v11 on v10

--- a/solution.py
+++ b/solution.py
@@ -254,9 +254,10 @@
     dest_index = owner_index * CAP + slot_index
     slot_ids = jnp.arange(devices * CAP, dtype=jnp.int32)
     placement = (dest_index[:, None] == slot_ids[None, :]).astype(jnp.float32)
-    send_values = exact_dot(placement, obs_values, 0).reshape(devices, CAP, seg_width)
     meta = jnp.stack([obs_weight, obs_offset.astype(jnp.float32)], axis=1)
-    send_meta = exact_dot(placement, meta, 0).reshape(devices, CAP, 2)
+    placed = exact_dot(placement, jnp.concatenate([obs_values, meta], axis=1), 0)
+    send_values = placed[:, :seg_width].reshape(devices, CAP, seg_width)
+    send_meta = placed[:, seg_width:].reshape(devices, CAP, 2)
     send_meta = jnp.swapaxes(send_meta, 1, 2).reshape(devices, 2 * CAP)
     send_meta = jnp.pad(send_meta, ((0, 0), (0, seg_width - 2 * CAP)))
     send = jnp.concatenate([send_values.reshape(devices, CAP * seg_width), send_meta], axis=1)

time: 105 us -> 103 us (0.981)
  other arithmetic: 11.1 us -> 8.56 us
  local copies, waits for them, and re-layouts: 10.2 us -> 12.2 us
  matrix products: 13.3 us -> 11.9 us
    ppermute x1, waiting for transfers between devices: 10.3 us -> 4.71 us  [run(): got_a = lax.ppermute(msg, ('lon', 'lat'), pairs_a)]
    ppermute x1, waiting for transfers between devices: 0.01 us -> 5.41 us  [run(): got_b = lax.ppermute(msg, ('lon', 'lat'), pairs_b)]
    ppermute x1, starting transfers between devices: 4.81 us -> 2.43 us  [run(): got_a = lax.ppermute(msg, ('lon', 'lat'), pairs_a)]
    ppermute x1, starting transfers between devices: 0.68 us -> 3.06 us  [run(): got_b = lax.ppermute(msg, ('lon', 'lat'), pairs_b)]
    ppermute x1, starting transfers between devices: 3.07 us -> 1.64 us  [per_device(): from_west = lax.ppermute(col_msg, 'lon', ring_east)]
    dot_general x3 -> x2, matrix products: 4.35 us -> 2.98 us  [exact_dot(): lax.dot_general(left, right, (((left_dim,), (0,)), ((), ())), precision=l...]
  transfers between devices with their start and end apart: 7 -> 7, of which waited for: 3 -> 4; matrix products, arithmetic and copies ran while one was open for 22% -> 20% of each run, Pallas kernels for 0% -> 0%
where the time goes in v11:
time: 103 us; the launch traced here: 102 us
  Pallas kernels  31.7 us (31%)
  starting transfers between devices  22 us (21%)
  waiting for transfers between devices  14.8 us (14%)
  local copies, waits for them, and re-layouts  12.2 us (12%)
  matrix products  11.9 us (12%)
  other arithmetic  8.56 us (8%)
  between operations  1.11 us (1%)
    pallas_call x1, Pallas kernels, step_call(): pl.pallas_call(step_kernel, grid_spec=pltpu.PrefetchScalarGridSpec(num_sc...  31.7 us
    all_to_all x1, starting transfers between devices, per_device(): lax.all_to_all(send, ('lon', 'lat'), split_axis=0, concat_axis=0, tiled=T...  10.6 us
    ppermute x1, waiting for transfers between devices, run(): got_b = lax.ppermute(msg, ('lon', 'lat'), pairs_b)  5.41 us
    ppermute x1, waiting for transfers between devices, run(): got_a = lax.ppermute(msg, ('lon', 'lat'), pairs_a)  4.71 us
    ppermute x1, waiting for transfers between devices, per_device(): from_east = lax.ppermute(col_msg, 'lon', ring_west)  3.68 us
    ppermute x1, starting transfers between devices, run(): got_b = lax.ppermute(msg, ('lon', 'lat'), pairs_b)  3.06 us
    ppermute x1, starting transfers between devices, per_device(): from_above = lax.ppermute(bot_msg, 'lat', down)  2.99 us
    dot_general x2, matrix products, exact_dot(): lax.dot_general(left, right, (((left_dim,), (0,)), ((), ())), precision=l...  2.98 us
  transfers between devices with their start and end apart: 7, of which 4 were waited for; matrix products, arithmetic and copies ran while one was open for 20% of the time, Pallas kernels for 0%

profile of v11, /device:TPU:95, one launch (start us, length us, event | category | flops | bytes accessed | tf_op | source)
XLA Modules:
  0.0 102.5 jit_solution(17833188385744418128)
XLA Ops:
  0.7 1.1 %fusion.21 = f32[512]{0:T(512)S(1)} fusion(s32[512]{0:T(512)} %bitcast.64), kind=kOutput, calls=%fused_computation.27 | convolution fusion | flops 67763712 | bytes 4096 | tf_op jit(solution)/shard_map/dot_general | solution.py:250
  1.8 0.7 multiply_add_fusion
  2.6 0.8 copy.62
  3.4 2.0 %fusion = f32[1024,130]{0,1:T(8,128)S(1)} fusion(s32[512]{0:T(512)S(1)} %bitcast.65, f32[512,1]{1,0:T(8,128)S(1)} %copy.63, f32[512,1]{1,0:T(8,128)S(1)} %copy.62, f32[512,128]{1,0:T(8,128)} %param.24), kind=kOutput, calls=%fused_computation.10 | convolution fusion | flops 818546688 | bytes 800768 | tf_op jit(solution)/shard_map/dot_general | solution.py:16
  6.2 1.4 %copy.67 = f32[128,1,1152]{2,1,0:T(1,128)} copy(f32[128,1,1152]{2,0,1:T(8,128)S(1)} %fusion.24) | data formatting | bytes 1179648 | tf_op jit(solution)/shard_map/all_to_all | solution.py:264
  7.6 10.6 %all-to-all-start = ((f32[128,1,1152]{2,1,0:T(1,128)}), f32[128,1,1152]{2,1,0:T(1,128)}, u32[]{:S(2)}, u32[]{:S(2)}) async-start(f32[128,1,1152]{2,1,0:T(1,128)} %copy.67), calls=%async_computation | async-start | bytes 1179648 | tf_op jit(solution)/shard_map/all_to_all | solution.py:264
  18.3 1.5 %broadcast_multiply_fusion = (f32[4,10,3,512]{3,2,1,0:T(4,128)S(1)}, f32[4,10,3,512]{3,2,1,0:T(4,128)S(1)}, f32[4,10,3,512]{3,2,1,0:T(4,128)S(1)}) fusion(f32[4]{0:T(128)S(1)} %copy-done.4, f32[10,3,512]{2,1,0:T(4,128)S(1)} %get-tuple-element.40, f32[4,10,64,512]{3,2,1,0:T(8,128)} %adj_ref.1, f32[10,3,512]{2,1,0:T(4,128)S(1)} %get-tuple-element.39), kind=kLoop, calls=%fused_computation.63 | loop fusion | flops 184320 | bytes 1351696 | tf_op jit(solution)/shard_map/mul | solution.py:192
  20.0 0.8 pad_maximum_fusion.11
  20.7 3.0 %collective-permute-start.16 = (f32[50,3,512]{2,0,1:T(8,128)}, f32[50,3,512]{2,0,1:T(8,128)}, u32[]{:S(2)}, u32[]{:S(2)}) collective-permute-start(f32[50,3,512]{2,0,1:T(8,128)} %pad_maximum_fusion.11), channel_id=1, source_target_pairs={{1,0},{2,1},{3,2},{4,3},{5,4},{6,5},{7,6},{8,7},{9,8},{10,9},{11,1... | collective-permute-start | bytes 921608 | tf_op jit(solution)/shard_map/ppermute | solution.py:190
  23.8 0.8 pad_maximum_fusion.12
  24.6 1.3 %collective-permute-start.17 = (f32[50,3,512]{2,0,1:T(8,128)}, f32[50,3,512]{2,0,1:T(8,128)}, u32[]{:S(2)}, u32[]{:S(2)}) collective-permute-start(f32[50,3,512]{2,0,1:T(8,128)} %pad_maximum_fusion.12), channel_id=1, source_target_pairs={{0,1},{1,2},{2,3},{3,4},{4,5},{5,6},{6,7},{7,8},{8,9},{9,10},{10,1... | collective-permute-start | bytes 921608 | tf_op jit(solution)/shard_map/ppermute | solution.py:189
  25.9 1.2 %slice.77 = s32[1]{0:T(128)} slice(s32[512]{0:T(512)} %param.28), slice={[0:1]} | slice | bytes 8 | tf_op jit(solution)/shard_map/slice | solution.py:133
  27.8 0.8 fusion.69
  29.0 2.0 %slice_multiply_fusion = (f32[4,10,64,128]{3,2,1,0:T(8,128)S(1)}, f32[4,10,64,128]{3,2,1,0:T(8,128)S(1)}) fusion(f32[4,10,64,512]{3,2,1,0:T(8,128)} %adj_ref.1, f32[10,64,128]{2,1,0:T(8,128)S(1)} %get-tuple-element.35, f32[10,64,128]{2,1,0:T(8,128)S(1)} %get-tuple-element.36), kind=kLoop, calls=%fused_computation.21 | loop fusion | flops 655360 | bytes 5898240 | tf_op jit(solution)/shard_map/mul | solution.py:215
  31.0 2.0 %fusion.4 = f32[8,50,64]{2,0,1:T(8,128)S(1)} fusion(f32[10,64,128]{2,1,0:T(8,128)S(1)} %get-tuple-element.38, f32[40,64,128]{2,1,0:T(8,128)S(1)} %bitcast.52, pred[8]{0:T(512)(128)(4,1)S(1)} %iota_compare_fusion.13), kind=kOutput, calls=%fused_computation.13 | convolution fusion | flops 39733248 | bytes 1740808 | tf_op jit(solution)/shard_map/nyx,xc->ncy/dot_general | solution.py:218
  33.1 2.1 %fusion.18 = f32[50,8,64]{2,1,0:T(8,128)S(1)} fusion(f32[8,50,64]{2,0,1:T(8,128)S(1)} %fusion.4, f32[10,64,128]{2,1,0:T(8,128)S(1)} %copy-done.2, f32[40,64,128]{2,1,0:T(8,128)S(1)} %bitcast.50, s32[8]{0:T(128)S(1)} %iota_add_fusion, pred[8]{0:T(512)(128)(4,1)S(1)} %iota_compare_fusion.12), kind=kOutput, calls=%fused_computation.26 | convolution fusion | flops 39758848 | bytes 1843240 | tf_op jit(solution)/shard_map/nyx,xc->ncy/dot_general | solution.py:223
  35.2 16.4 %conditional.1 = (f32[50,3,1024]{2,0,1:T(8,128)S(1)}) conditional(s32[]{:T(128)} %clamp.3, f32[50,3,512]{2,1,0:T(4,128)S(1)} %fusion.30, f32[50,3,512]{2,1,0:T(4,128)S(1)} %fusion.30, f32[50,3,512]{2,1,0:T(4,128)S(1)} %fusion.30, f32[50,3,512]{2,1,0:T(4,128)S(1)} %fusion.30, f32[50,3,512]{2,1,0:T(4,128)S(1)} %fusion.30, ...), branch_computations={%region_1.2_spmd, %region_2.3_spmd, %region_3.4_spmd, %region_4.5_... | conditional | flops 153600 | bytes 4915288 | solution.py:152
  35.2 3.1 %collective-permute-start.5 = (f32[50,3,512]{2,1,0:T(4,128)S(1)}, f32[50,3,512]{2,1,0:T(4,128)S(1)}, u32[]{:S(2)}, u32[]{:S(2)}) collective-permute-start(f32[50,3,512]{2,1,0:T(4,128)S(1)} %param.2), channel_id=1, source_target_pairs={{47,15},{31,31},{15,47},{127,63},{111,79},{95,95},{79,111},{63,127}} | collective-permute-start | bytes 921608 | tf_op jit(solution)/shard_map/cond/branch_2_fun/ppermute | solution.py:147
  38.3 2.4 %collective-permute-start.4 = (f32[50,3,512]{2,1,0:T(4,128)S(1)}, f32[50,3,512]{2,1,0:T(4,128)S(1)}, u32[]{:S(2)}, u32[]{:S(2)}) collective-permute-start(f32[50,3,512]{2,1,0:T(4,128)S(1)} %param.2), channel_id=1, source_target_pairs={{31,15},{15,31},{127,47},{111,63},{95,79},{79,95},{63,111},{47,127}} | collective-permute-start | bytes 921608 | tf_op jit(solution)/shard_map/cond/branch_2_fun/ppermute | solution.py:146
  40.7 5.4 %collective-permute-done.5 = f32[50,3,512]{2,1,0:T(4,128)S(1)} collective-permute-done((f32[50,3,512]{2,1,0:T(4,128)S(1)}, f32[50,3,512]{2,1,0:T(4,128)S(1)}, u32[]{:S(2)}, u32[]{:S(2)}) %collective-permute-start.5) | collective-permute-done | bytes 307232 | tf_op jit(solution)/shard_map/cond/branch_2_fun/ppermute | solution.py:147
  46.2 4.7 %collective-permute-done.4 = f32[50,3,512]{2,1,0:T(4,128)S(1)} collective-permute-done((f32[50,3,512]{2,1,0:T(4,128)S(1)}, f32[50,3,512]{2,1,0:T(4,128)S(1)}, u32[]{:S(2)}, u32[]{:S(2)}) %collective-permute-start.4) | collective-permute-done | bytes 307232 | tf_op jit(solution)/shard_map/cond/branch_2_fun/ppermute | solution.py:146
  51.7 0.9 fusion.12
  52.6 1.1 %pad_maximum_fusion.8 = f32[50,8,512]{2,0,1:T(8,128)S(1)} fusion(f32[50,3,512]{2,0,1:T(8,128)} %collective-permute-done.17, f32[50,3,512]{2,0,1:T(8,128)S(1)} %fusion.12, f32[8]{0:T(128)S(1)} %pad.43.clone), kind=kLoop, calls=%fused_computation.31 | loop fusion | flops 409600 | bytes 1433632 | tf_op jit(solution)/shard_map/concatenate | solution.py:200
  55.0 1.6 %collective-permute-start.19 = (f32[50,8,72]{2,1,0:T(8,128)S(1)}, f32[50,8,72]{2,1,0:T(8,128)S(1)}, u32[]{:S(2)}, u32[]{:S(2)}) collective-permute-start(f32[50,8,72]{2,1,0:T(8,128)S(1)} %pad_maximum_fusion.13), channel_id=1, source_target_pairs={{0,16},{16,32},{32,48},{48,64},{64,80},{80,96},{96,112},{112,0},{1... | collective-permute-start | bytes 345608 | tf_op jit(solution)/shard_map/ppermute | solution.py:233
  56.6 0.7 copy.82.cor_ref
  57.3 1.4 %copy.77 = f32[50,8,512]{2,1,0:T(8,128)} copy(f32[50,8,512]{2,0,1:T(8,128)S(1)} %pad_maximum_fusion.8) | data formatting | bytes 1638400 | tf_op jit(solution)/shard_map/concatenate | solution.py:200
  58.7 1.0 collective-permute-done.19
  59.6 3.7 %collective-permute-done.18 = f32[50,8,72]{2,1,0:T(8,128)S(1)} collective-permute-done((f32[50,8,72]{2,1,0:T(8,128)S(1)}, f32[50,8,72]{2,1,0:T(8,128)S(1)}, u32[]{:S(2)}, u32[]{:S(2)}) %collective-permute-start.18) | collective-permute-done | bytes 115232 | tf_op jit(solution)/shard_map/ppermute | solution.py:232
  63.3 3.0 %fusion.38 = f32[50,72,128]{2,1,0:T(8,128)} fusion(f32[50,8,72]{2,1,0:T(8,128)S(1)} %collective-permute-done.18, f32[50,8,72]{2,1,0:T(8,128)S(1)} %collective-permute-done.19, pred[8]{0:T(512)(128)(4,1)S(1)} %iota_compare_fusion.13, s32[8]{0:T(128)S(1)} %iota_add_fusion, pred[8]{0:T(512)(128)(4,1)S(1)} %iota_compare_fusion.12), kind=kOutput, calls=%fused_computation.61 | convolution fusion | flops 44270720 | bytes 2073648 | tf_op jit(solution)/shard_map/ncy,cl->nyl/dot_general | solution.py:237
  66.3 1.5 %copy.68 = f32[128,1,1152]{0,2,1:T(8,128)S(1)} copy(f32[128,1,1152]{2,1,0:T(1,128)} %all-to-all-done) | data formatting | bytes 1179648 | tf_op jit(solution)/shard_map/all_to_all | solution.py:264
  68.1 0.8 pad.19.vals_ref
  70.8 31.7 %shard_map.109 = f32[4,10,64,512]{3,2,1,0:T(8,128)} custom-call(s32[6,1040]{1,0:T(8,128)} %pad.17.where_ref, f32[1040]{0:T(1024)} %pad.18.weight_ref, f32[4,10,64,512]{3,2,1,0:T(8,128)} %adj_ref.1, s32[10,64,512]{2,1,0:T(8,128)} %mask_ref.1, f32[10,64,512]{2,1,0:T(8,128)} %diff_ref.1, f32[5,10,8,512]{3,2,1,0:T(8,128)} %bitcast.53, ...), custom_call_target="tpu_custom_call" | custom-call | tf_op jit(solution)/shard_map/pallas_call | solution.py:101
  (62 shorter events, 6.1 us)
Async XLA Ops:
  6.1 12.1 %copy-start.1 = (f32[10,64,512]{2,1,0:T(8,128)S(1)}, f32[10,64,512]{2,1,0:T(8,128)}, u32[]{:S(2)}) copy-start(f32[10,64,512]{2,1,0:T(8,128)} %diff_ref.1) | copy-start | bytes 3932164
  6.2 12.1 %copy-start = (s32[10,64,512]{2,1,0:T(8,128)S(1)}, s32[10,64,512]{2,1,0:T(8,128)}, u32[]{:S(2)}) copy-start(s32[10,64,512]{2,1,0:T(8,128)} %mask_ref.1) | copy-start | bytes 3932164
  6.2 12.2 %copy-start.4 = (f32[4]{0:T(128)S(1)}, f32[4]{0:T(128)}, u32[]{:S(2)}) copy-start(f32[4]{0:T(128)} %constant.148.clone) | copy-start | bytes 52
  7.6 58.7 %all-to-all-start = ((f32[128,1,1152]{2,1,0:T(1,128)}), f32[128,1,1152]{2,1,0:T(1,128)}, u32[]{:S(2)}, u32[]{:S(2)}) async-start(f32[128,1,1152]{2,1,0:T(1,128)} %copy.67), calls=%async_computation | async-start | bytes 1179648 | tf_op jit(solution)/shard_map/all_to_all | solution.py:264
  20.7 30.9 %collective-permute-start.16 = (f32[50,3,512]{2,0,1:T(8,128)}, f32[50,3,512]{2,0,1:T(8,128)}, u32[]{:S(2)}, u32[]{:S(2)}) collective-permute-start(f32[50,3,512]{2,0,1:T(8,128)} %pad_maximum_fusion.11), channel_id=1, source_target_pairs={{1,0},{2,1},{3,2},{4,3},{5,4},{6,5},{7,6},{8,7},{9,8},{10,9},{11,1... | collective-permute-start | bytes 921608 | tf_op jit(solution)/shard_map/ppermute | solution.py:190
  24.6 28.1 %collective-permute-start.17 = (f32[50,3,512]{2,0,1:T(8,128)}, f32[50,3,512]{2,0,1:T(8,128)}, u32[]{:S(2)}, u32[]{:S(2)}) collective-permute-start(f32[50,3,512]{2,0,1:T(8,128)} %pad_maximum_fusion.12), channel_id=1, source_target_pairs={{0,1},{1,2},{2,3},{3,4},{4,5},{5,6},{6,7},{7,8},{8,9},{9,10},{10,1... | collective-permute-start | bytes 921608 | tf_op jit(solution)/shard_map/ppermute | solution.py:189
  31.0 2.0 %copy-start.2 = (f32[10,64,128]{2,1,0:T(8,128)S(1)}, f32[10,64,128]{2,1,0:T(8,128)}, u32[]{:S(2)}) copy-start(f32[10,64,128]{2,1,0:T(8,128)} %get-tuple-element.37) | copy-start | bytes 983044
  35.2 10.9 %collective-permute-start.5 = (f32[50,3,512]{2,1,0:T(4,128)S(1)}, f32[50,3,512]{2,1,0:T(4,128)S(1)}, u32[]{:S(2)}, u32[]{:S(2)}) collective-permute-start(f32[50,3,512]{2,1,0:T(4,128)S(1)} %param.2), channel_id=1, source_target_pairs={{47,15},{31,31},{15,47},{127,63},{111,79},{95,95},{79,111},{63,127}} | collective-permute-start | bytes 921608 | tf_op jit(solution)/shard_map/cond/branch_2_fun/ppermute | solution.py:147
  38.3 12.6 %collective-permute-start.4 = (f32[50,3,512]{2,1,0:T(4,128)S(1)}, f32[50,3,512]{2,1,0:T(4,128)S(1)}, u32[]{:S(2)}, u32[]{:S(2)}) collective-permute-start(f32[50,3,512]{2,1,0:T(4,128)S(1)} %param.2), channel_id=1, source_target_pairs={{31,15},{15,31},{127,47},{111,63},{95,79},{79,95},{63,111},{47,127}} | collective-permute-start | bytes 921608 | tf_op jit(solution)/shard_map/cond/branch_2_fun/ppermute | solution.py:146
  52.6 4.0 %copy-start.3 = (f32[64]{0:T(128)S(1)}, f32[64]{0:T(128)}, u32[]{:S(2)}) copy-start(f32[64]{0:T(128)} %param.23) | copy-start | bytes 772
  55.0 4.7 %collective-permute-start.19 = (f32[50,8,72]{2,1,0:T(8,128)S(1)}, f32[50,8,72]{2,1,0:T(8,128)S(1)}, u32[]{:S(2)}, u32[]{:S(2)}) collective-permute-start(f32[50,8,72]{2,1,0:T(8,128)S(1)} %pad_maximum_fusion.13), channel_id=1, source_target_pairs={{0,16},{16,32},{32,48},{48,64},{64,80},{80,96},{96,112},{112,0},{1... | collective-permute-start | bytes 345608 | tf_op jit(solution)/shard_map/ppermute | solution.py:233
  56.6 6.7 %collective-permute-start.18 = (f32[50,8,72]{2,1,0:T(8,128)S(1)}, f32[50,8,72]{2,1,0:T(8,128)S(1)}, u32[]{:S(2)}, u32[]{:S(2)}) collective-permute-start(f32[50,8,72]{2,1,0:T(8,128)S(1)} %pad_maximum_fusion.13), channel_id=1, source_target_pairs={{0,112},{16,0},{32,16},{48,32},{64,48},{80,64},{96,80},{112,96},{1... | collective-permute-start | bytes 345608 | tf_op jit(solution)/shard_map/ppermute | solution.py:232

commit v12 on v11

--- a/solution.py
+++ b/solution.py
@@ -226,7 +226,8 @@
         take_last.astype(jnp.float32),
         precision=lax.Precision.HIGHEST,
     )
-    col_msg = jnp.concatenate([interior, edges(rows_all)], axis=2)
+    corner_gap = jnp.zeros((n_work + levels, PAD_ROWS, PAD_ROWS - 2 * HALO), jnp.float32)
+    col_msg = jnp.concatenate([interior, edges(north), corner_gap, edges(from_below)], axis=2)
     ring_west = [(i, (i - 1) % lon_count) for i in range(lon_count)]
     ring_east = [(i, (i + 1) % lon_count) for i in range(lon_count)]
     from_east = lax.ppermute(col_msg, "lon", ring_west)

time: 103 us -> 105 us (1.019)
  waiting for transfers between devices: 14.8 us -> 12.5 us
  other arithmetic: 8.56 us -> 10.7 us
  matrix products: 11.9 us -> 13.9 us
    dot_general x2 -> x4, matrix products: 0.84 us -> 2.79 us  [edges(): jnp.einsum('nyx,xc->ncy', part, sel.astype(jnp.float32), precision=lax.Pr...]
    concatenate x1, other arithmetic: 0.27 us -> 1.62 us  [per_device(): jnp.concatenate([signed_top[:, HALO - 1 - m:HALO - m, :] for m in range(H...]
    ppermute x1, starting transfers between devices: 1.64 us -> 0.5 us  [per_device(): from_west = lax.ppermute(col_msg, 'lon', ring_east)]
    ppermute x1, waiting for transfers between devices: 3.68 us -> 2.54 us  [per_device(): from_east = lax.ppermute(col_msg, 'lon', ring_west)]
  transfers between devices with their start and end apart: 7 -> 7, of which waited for: 4 -> 4; matrix products, arithmetic and copies ran while one was open for 20% -> 25% of each run, Pallas kernels for 0% -> 0%
where the time goes in v12:
time: 105 us; the launch traced here: 104 us
  Pallas kernels  31.7 us (30%)
  starting transfers between devices  21.2 us (20%)
  matrix products  13.9 us (13%)
  waiting for transfers between devices  12.5 us (12%)
  local copies, waits for them, and re-layouts  12.3 us (12%)
  other arithmetic  10.7 us (10%)
  between operations  1.09 us (1%)
    pallas_call x1, Pallas kernels, step_call(): pl.pallas_call(step_kernel, grid_spec=pltpu.PrefetchScalarGridSpec(num_sc...  31.7 us
    all_to_all x1, starting transfers between devices, per_device(): lax.all_to_all(send, ('lon', 'lat'), split_axis=0, concat_axis=0, tiled=T...  10.2 us
    ppermute x1, waiting for transfers between devices, run(): got_b = lax.ppermute(msg, ('lon', 'lat'), pairs_b)  5.08 us
    ppermute x1, waiting for transfers between devices, run(): got_a = lax.ppermute(msg, ('lon', 'lat'), pairs_a)  4.28 us
    ppermute x1, starting transfers between devices, run(): got_b = lax.ppermute(msg, ('lon', 'lat'), pairs_b)  3.06 us
    dot_general x2, matrix products, exact_dot(): lax.dot_general(left, right, (((left_dim,), (0,)), ((), ())), precision=l...  3 us
    ppermute x1, starting transfers between devices, per_device(): from_above = lax.ppermute(bot_msg, 'lat', down)  2.99 us
    dot_general x1, matrix products, per_device(): jnp.einsum('ncy,cl->nyl', got_cols, place, precision=lax.Precision.HIGHEST)  2.94 us
  transfers between devices with their start and end apart: 7, of which 4 were waited for; matrix products, arithmetic and copies ran while one was open for 25% of the time, Pallas kernels for 0%

profile of v12, /device:TPU:95, one launch (start us, length us, event | category | flops | bytes accessed | tf_op | source)
XLA Modules:
  0.0 103.7 jit_solution(9535924975016642389)
XLA Ops:
  0.7 1.1 %fusion.21 = f32[512]{0:T(512)S(1)} fusion(s32[512]{0:T(512)} %bitcast.68), kind=kOutput, calls=%fused_computation.27 | convolution fusion | flops 67763712 | bytes 4096 | tf_op jit(solution)/shard_map/dot_general | solution.py:251
  2.6 0.8 copy.68
  3.4 2.0 %fusion = f32[1024,130]{0,1:T(8,128)S(1)} fusion(s32[512]{0:T(512)S(1)} %bitcast.69, f32[512,1]{1,0:T(8,128)S(1)} %copy.69, f32[512,1]{1,0:T(8,128)S(1)} %copy.68, f32[512,128]{1,0:T(8,128)} %param.24), kind=kOutput, calls=%fused_computation.10 | convolution fusion | flops 818546688 | bytes 800768 | tf_op jit(solution)/shard_map/dot_general | solution.py:16
  6.2 1.4 %copy.73 = f32[128,1,1152]{2,1,0:T(1,128)} copy(f32[128,1,1152]{2,0,1:T(8,128)S(1)} %fusion.26) | data formatting | bytes 1179648 | tf_op jit(solution)/shard_map/all_to_all | solution.py:265
  7.6 10.2 %all-to-all-start = ((f32[128,1,1152]{2,1,0:T(1,128)}), f32[128,1,1152]{2,1,0:T(1,128)S(1)}, u32[]{:S(2)}, u32[]{:S(2)}) async-start(f32[128,1,1152]{2,1,0:T(1,128)} %copy.73), calls=%async_computation | async-start | bytes 1179648 | tf_op jit(solution)/shard_map/all_to_all | solution.py:265
  18.0 2.3 %broadcast_multiply_fusion = (f32[4,10,3,512]{3,2,1,0:T(4,128)}, f32[4,10,3,512]{3,2,1,0:T(4,128)S(1)}, f32[4,10,3,512]{3,2,1,0:T(4,128)S(1)}) fusion(f32[4]{0:T(128)S(1)} %copy-done.6, f32[10,3,512]{2,1,0:T(4,128)S(1)} %get-tuple-element.40, f32[4,10,64,512]{3,2,1,0:T(8,128)} %adj_ref.1, f32[10,3,512]{2,1,0:T(4,128)S(1)} %get-tuple-element.39), kind=kLoop, calls=%fused_computation.63 | loop fusion | flops 184320 | bytes 1351696 | tf_op jit(solution)/shard_map/mul | solution.py:192
  20.3 0.8 pad_maximum_fusion.11
  21.1 3.0 %collective-permute-start.16 = (f32[50,3,512]{2,0,1:T(8,128)}, f32[50,3,512]{2,0,1:T(8,128)}, u32[]{:S(2)}, u32[]{:S(2)}) collective-permute-start(f32[50,3,512]{2,0,1:T(8,128)} %pad_maximum_fusion.11), channel_id=1, source_target_pairs={{1,0},{2,1},{3,2},{4,3},{5,4},{6,5},{7,6},{8,7},{9,8},{10,9},{11,1... | collective-permute-start | bytes 921608 | tf_op jit(solution)/shard_map/ppermute | solution.py:190
  24.2 0.8 pad_maximum_fusion.12
  25.0 1.3 %collective-permute-start.17 = (f32[50,3,512]{2,0,1:T(8,128)}, f32[50,3,512]{2,0,1:T(8,128)}, u32[]{:S(2)}, u32[]{:S(2)}) collective-permute-start(f32[50,3,512]{2,0,1:T(8,128)} %pad_maximum_fusion.12), channel_id=1, source_target_pairs={{0,1},{1,2},{2,3},{3,4},{4,5},{5,6},{6,7},{7,8},{8,9},{9,10},{10,1... | collective-permute-start | bytes 921608 | tf_op jit(solution)/shard_map/ppermute | solution.py:189
  26.3 1.2 %slice.83 = s32[1]{0:T(128)} slice(s32[512]{0:T(512)} %param.28), slice={[0:1]} | slice | bytes 8 | tf_op jit(solution)/shard_map/slice | solution.py:133
  28.9 0.8 fusion.77
  29.8 0.7 copy.87.cor_ref
  30.5 1.6 %fusion.32 = f32[50,3,512]{2,1,0:T(4,128)S(1)} fusion(f32[10,3,512]{2,1,0:T(4,128)} %copy-done.3, f32[40,3,512]{2,1,0:T(4,128)} %bitcast.60), kind=kLoop, calls=%fused_computation.47 | loop fusion | flops 768000 | bytes 614400 | tf_op jit(solution)/shard_map/concatenate | solution.py:194
  32.1 15.4 %conditional.1 = (f32[50,3,1024]{2,0,1:T(8,128)S(1)}) conditional(s32[]{:T(128)} %clamp.3, f32[50,3,512]{2,1,0:T(4,128)S(1)} %fusion.32, f32[50,3,512]{2,1,0:T(4,128)S(1)} %fusion.32, f32[50,3,512]{2,1,0:T(4,128)S(1)} %fusion.32, f32[50,3,512]{2,1,0:T(4,128)S(1)} %fusion.32, f32[50,3,512]{2,1,0:T(4,128)S(1)} %fusion.32, ...), branch_computations={%region_1.2_spmd, %region_2.3_spmd, %region_3.4_spmd, %region_4.5_... | conditional | flops 153600 | bytes 4915288 | solution.py:152
  32.2 3.1 %collective-permute-start.9 = (f32[50,3,512]{2,1,0:T(4,128)S(1)}, f32[50,3,512]{2,1,0:T(4,128)S(1)}, u32[]{:S(2)}, u32[]{:S(2)}) collective-permute-start(f32[50,3,512]{2,1,0:T(4,128)S(1)} %param.4), channel_id=1, source_target_pairs={{79,15},{63,31},{47,47},{31,63},{15,79},{127,95},{111,111},{95,127}} | collective-permute-start | bytes 921608 | tf_op jit(solution)/shard_map/cond/branch_4_fun/ppermute | solution.py:147
  35.2 2.2 %collective-permute-start.8 = (f32[50,3,512]{2,1,0:T(4,128)S(1)}, f32[50,3,512]{2,1,0:T(4,128)S(1)}, u32[]{:S(2)}, u32[]{:S(2)}) collective-permute-start(f32[50,3,512]{2,1,0:T(4,128)S(1)} %param.4), channel_id=1, source_target_pairs={{63,15},{47,31},{31,47},{15,63},{127,79},{111,95},{95,111},{79,127}} | collective-permute-start | bytes 921608 | tf_op jit(solution)/shard_map/cond/branch_4_fun/ppermute | solution.py:146
  37.4 5.1 %collective-permute-done.9 = f32[50,3,512]{2,1,0:T(4,128)S(1)} collective-permute-done((f32[50,3,512]{2,1,0:T(4,128)S(1)}, f32[50,3,512]{2,1,0:T(4,128)S(1)}, u32[]{:S(2)}, u32[]{:S(2)}) %collective-permute-start.9) | collective-permute-done | bytes 307232 | tf_op jit(solution)/shard_map/cond/branch_4_fun/ppermute | solution.py:147
  42.5 4.3 %collective-permute-done.8 = f32[50,3,512]{2,1,0:T(4,128)S(1)} collective-permute-done((f32[50,3,512]{2,1,0:T(4,128)S(1)}, f32[50,3,512]{2,1,0:T(4,128)S(1)}, u32[]{:S(2)}, u32[]{:S(2)}) %collective-permute-start.8) | collective-permute-done | bytes 307232 | tf_op jit(solution)/shard_map/cond/branch_4_fun/ppermute | solution.py:146
  47.5 2.1 %slice_multiply_fusion = (f32[4,10,64,128]{3,2,1,0:T(8,128)S(1)}, f32[4,10,64,128]{3,2,1,0:T(8,128)S(1)}) fusion(f32[4,10,64,512]{3,2,1,0:T(8,128)} %adj_ref.1, f32[10,64,128]{2,1,0:T(8,128)S(1)} %get-tuple-element.35, f32[10,64,128]{2,1,0:T(8,128)S(1)} %get-tuple-element.36), kind=kLoop, calls=%fused_computation.21 | loop fusion | flops 655360 | bytes 5898240 | tf_op jit(solution)/shard_map/mul | solution.py:215
  49.6 2.0 %fusion.4 = f32[8,50,64]{2,0,1:T(8,128)S(1)} fusion(f32[10,64,128]{2,1,0:T(8,128)S(1)} %copy-done.2, f32[40,64,128]{2,1,0:T(8,128)S(1)} %bitcast.56, pred[8]{0:T(512)(128)(4,1)S(1)} %get-tuple-element.47), kind=kOutput, calls=%fused_computation.13 | convolution fusion | flops 39733248 | bytes 1740808 | tf_op jit(solution)/shard_map/nyx,xc->ncy/dot_general | solution.py:218
  51.7 2.1 %fusion.18 = f32[50,8,64]{2,1,0:T(8,128)S(1)} fusion(f32[8,50,64]{2,0,1:T(8,128)S(1)} %fusion.4, f32[10,64,128]{2,1,0:T(8,128)S(1)} %get-tuple-element.37, f32[40,64,128]{2,1,0:T(8,128)S(1)} %bitcast.54, s32[8]{0:T(128)S(1)} %iota_add_fusion, pred[8]{0:T(512)(128)(4,1)S(1)} %get-tuple-element.46), kind=kOutput, calls=%fused_computation.26 | convolution fusion | flops 39758848 | bytes 1843240 | tf_op jit(solution)/shard_map/nyx,xc->ncy/dot_general | solution.py:223
  53.8 1.0 fusion.12
  55.4 1.1 %fusion.40 = f32[8,50,3]{1,0,2:T(8,128)S(1)} fusion(f32[50,3,512]{2,0,1:T(8,128)} %collective-permute-done.17, s32[8]{0:T(128)S(1)} %iota_add_fusion, pred[8]{0:T(512)(128)(4,1)S(1)} %get-tuple-element.46), kind=kOutput, calls=%fused_computation.66 | convolution fusion | flops 1845248 | bytes 90856 | tf_op jit(solution)/shard_map/nyx,xc->ncy/dot_general | solution.py:209
  56.6 1.2 %fusion.22 = f32[50,8,3]{0,1,2:T(8,128)S(1)} fusion(f32[8,50,3]{1,0,2:T(8,128)S(1)} %fusion.40, f32[50,3,512]{2,0,1:T(8,128)} %collective-permute-done.17, pred[8]{0:T(512)(128)(4,1)S(1)} %get-tuple-element.47), kind=kOutput, calls=%fused_computation.29 | convolution fusion | flops 1846448 | bytes 95624 | tf_op jit(solution)/shard_map/nyx,xc->ncy/dot_general | solution.py:209
  58.6 1.0 collective-permute-start.18
  59.7 1.1 %pad_maximum_fusion.8 = f32[50,8,512]{2,0,1:T(8,128)S(1)} fusion(f32[50,3,512]{2,0,1:T(8,128)} %collective-permute-done.17, f32[50,3,512]{2,0,1:T(8,128)S(1)} %fusion.12, f32[8]{0:T(128)S(1)} %pad.45.clone), kind=kLoop, calls=%fused_computation.35 | loop fusion | flops 409600 | bytes 1433632 | tf_op jit(solution)/shard_map/concatenate | solution.py:200
  60.8 1.4 %copy.83 = f32[50,8,512]{2,1,0:T(8,128)} copy(f32[50,8,512]{2,0,1:T(8,128)S(1)} %pad_maximum_fusion.8) | data formatting | bytes 1638400 | tf_op jit(solution)/shard_map/concatenate | solution.py:200
  62.8 2.5 %collective-permute-done.18 = f32[50,8,72]{2,1,0:T(8,128)S(1)} collective-permute-done((f32[50,8,72]{2,1,0:T(8,128)S(1)}, f32[50,8,72]{2,1,0:T(8,128)S(1)}, u32[]{:S(2)}, u32[]{:S(2)}) %collective-permute-start.18) | collective-permute-done | bytes 115232 | tf_op jit(solution)/shard_map/ppermute | solution.py:233
  65.3 2.9 %fusion.36 = f32[50,72,128]{2,1,0:T(8,128)} fusion(f32[50,8,72]{2,1,0:T(8,128)S(1)} %collective-permute-done.18, f32[50,8,72]{2,1,0:T(8,128)S(1)} %collective-permute-done.19, pred[8]{0:T(512)(128)(4,1)S(1)} %get-tuple-element.47, s32[8]{0:T(128)S(1)} %iota_add_fusion, pred[8]{0:T(512)(128)(4,1)S(1)} %get-tuple-element.46), kind=kOutput, calls=%fused_computation.61 | convolution fusion | flops 44270720 | bytes 2073648 | tf_op jit(solution)/shard_map/ncy,cl->nyl/dot_general | solution.py:238
  69.3 0.8 pad.19.vals_ref
  72.0 31.7 %shard_map.109 = f32[4,10,64,512]{3,2,1,0:T(8,128)} custom-call(s32[6,1040]{1,0:T(8,128)} %pad.17.where_ref, f32[1040]{0:T(1024)} %pad.18.weight_ref, f32[4,10,64,512]{3,2,1,0:T(8,128)} %adj_ref.1, s32[10,64,512]{2,1,0:T(8,128)} %mask_ref.1, f32[10,64,512]{2,1,0:T(8,128)} %diff_ref.1, f32[5,10,8,512]{3,2,1,0:T(8,128)} %bitcast.57, ...), custom_call_target="tpu_custom_call" | custom-call | tf_op jit(solution)/shard_map/pallas_call | solution.py:101
  (68 shorter events, 8.9 us)
Async XLA Ops:
  6.1 11.7 %copy-start.1 = (f32[10,64,512]{2,1,0:T(8,128)S(1)}, f32[10,64,512]{2,1,0:T(8,128)}, u32[]{:S(2)}) copy-start(f32[10,64,512]{2,1,0:T(8,128)} %diff_ref.1) | copy-start | bytes 3932164
  6.2 11.7 %copy-start = (s32[10,64,512]{2,1,0:T(8,128)S(1)}, s32[10,64,512]{2,1,0:T(8,128)}, u32[]{:S(2)}) copy-start(s32[10,64,512]{2,1,0:T(8,128)} %mask_ref.1) | copy-start | bytes 3932164
  6.2 11.8 %copy-start.6 = (f32[4]{0:T(128)S(1)}, f32[4]{0:T(128)}, u32[]{:S(2)}) copy-start(f32[4]{0:T(128)} %constant.149.clone) | copy-start | bytes 52
  7.6 60.7 %all-to-all-start = ((f32[128,1,1152]{2,1,0:T(1,128)}), f32[128,1,1152]{2,1,0:T(1,128)S(1)}, u32[]{:S(2)}, u32[]{:S(2)}) async-start(f32[128,1,1152]{2,1,0:T(1,128)} %copy.73), calls=%async_computation | async-start | bytes 1179648 | tf_op jit(solution)/shard_map/all_to_all | solution.py:265
  17.9 7.1 %copy-start.3 = (f32[10,3,512]{2,1,0:T(4,128)}, f32[10,3,512]{2,1,0:T(4,128)S(1)}, u32[]{:S(2)}) copy-start(f32[10,3,512]{2,1,0:T(4,128)S(1)} %get-tuple-element.42) | copy-start | bytes 184324
  21.1 32.7 %collective-permute-start.16 = (f32[50,3,512]{2,0,1:T(8,128)}, f32[50,3,512]{2,0,1:T(8,128)}, u32[]{:S(2)}, u32[]{:S(2)}) collective-permute-start(f32[50,3,512]{2,0,1:T(8,128)} %pad_maximum_fusion.11), channel_id=1, source_target_pairs={{1,0},{2,1},{3,2},{4,3},{5,4},{6,5},{7,6},{8,7},{9,8},{10,9},{11,1... | collective-permute-start | bytes 921608 | tf_op jit(solution)/shard_map/ppermute | solution.py:190
  24.2 5.6 %copy-start.4 = (f32[64]{0:T(128)S(1)}, f32[64]{0:T(128)}, u32[]{:S(2)}) copy-start(f32[64]{0:T(128)} %param.23) | copy-start | bytes 772
  25.0 30.5 %collective-permute-start.17 = (f32[50,3,512]{2,0,1:T(8,128)}, f32[50,3,512]{2,0,1:T(8,128)}, u32[]{:S(2)}, u32[]{:S(2)}) collective-permute-start(f32[50,3,512]{2,0,1:T(8,128)} %pad_maximum_fusion.12), channel_id=1, source_target_pairs={{0,1},{1,2},{2,3},{3,4},{4,5},{5,6},{6,7},{7,8},{8,9},{9,10},{10,1... | collective-permute-start | bytes 921608 | tf_op jit(solution)/shard_map/ppermute | solution.py:189
  32.2 10.3 %collective-permute-start.9 = (f32[50,3,512]{2,1,0:T(4,128)S(1)}, f32[50,3,512]{2,1,0:T(4,128)S(1)}, u32[]{:S(2)}, u32[]{:S(2)}) collective-permute-start(f32[50,3,512]{2,1,0:T(4,128)S(1)} %param.4), channel_id=1, source_target_pairs={{79,15},{63,31},{47,47},{31,63},{15,79},{127,95},{111,111},{95,127}} | collective-permute-start | bytes 921608 | tf_op jit(solution)/shard_map/cond/branch_4_fun/ppermute | solution.py:147
  35.2 11.5 %collective-permute-start.8 = (f32[50,3,512]{2,1,0:T(4,128)S(1)}, f32[50,3,512]{2,1,0:T(4,128)S(1)}, u32[]{:S(2)}, u32[]{:S(2)}) collective-permute-start(f32[50,3,512]{2,1,0:T(4,128)S(1)} %param.4), channel_id=1, source_target_pairs={{63,15},{47,31},{31,47},{15,63},{127,79},{111,95},{95,111},{79,127}} | collective-permute-start | bytes 921608 | tf_op jit(solution)/shard_map/cond/branch_4_fun/ppermute | solution.py:146
  47.5 2.1 %copy-start.2 = (f32[10,64,128]{2,1,0:T(8,128)S(1)}, f32[10,64,128]{2,1,0:T(8,128)}, u32[]{:S(2)}) copy-start(f32[10,64,128]{2,1,0:T(8,128)} %get-tuple-element.38) | copy-start | bytes 983044
  53.7 4.2 %copy-start.5 = (f32[72]{0:T(128)S(1)}, f32[72]{0:T(128)}, u32[]{:S(2)}) copy-start(f32[72]{0:T(128)} %pad.38.clone) | copy-start | bytes 868
  58.1 4.7 %collective-permute-start.19 = (f32[50,8,72]{2,1,0:T(8,128)S(1)}, f32[50,8,72]{2,1,0:T(8,128)S(1)}, u32[]{:S(2)}, u32[]{:S(2)}) collective-permute-start(f32[50,8,72]{2,1,0:T(8,128)S(1)} %pad_maximum_fusion.13), channel_id=1, source_target_pairs={{0,16},{16,32},{32,48},{48,64},{64,80},{80,96},{96,112},{112,0},{1... | collective-permute-start | bytes 345608 | tf_op jit(solution)/shard_map/ppermute | solution.py:234
  58.6 6.7 %collective-permute-start.18 = (f32[50,8,72]{2,1,0:T(8,128)S(1)}, f32[50,8,72]{2,1,0:T(8,128)S(1)}, u32[]{:S(2)}, u32[]{:S(2)}) collective-permute-start(f32[50,8,72]{2,1,0:T(8,128)S(1)} %pad_maximum_fusion.13), channel_id=1, source_target_pairs={{0,112},{16,0},{32,16},{48,32},{64,48},{80,64},{96,80},{112,96},{1... | collective-permute-start | bytes 345608 | tf_op jit(solution)/shard_map/ppermute | solution.py:233
